TPU v7x, 32 devices: a whole 2x2x4 slice. The times are simulated.
32 devices in a mesh: store: 4 (over x, core), blk: 2 (over y), batch: 4 (over z).
Axes of the slice: x: 2, y: 2, z: 4, core: 2. Of those that a mesh axis runs over, the one named last changes fastest.
Arguments:
- cands: bfloat16 [16, 256, 1024], P(('batch', 'store'), 'blk'), parts along dimension 0, may hold values from -6 to 6
- kv_store: bfloat16 [16, 512, 2, 1024], P('batch', ('blk', 'store')), parts along dimension 0, may hold values from -6 to 6
- proj_weight: bfloat16 [1024, 2, 1024], P(None, None, 'blk'), may hold values from -0.1875 to 0.1875
- norm_gain: float32 [1024], replicated, may hold values from 0.5 to 1.5
- users: int32 [16], P('batch'), parts along dimension 0, may hold values from 0 to 3, each once
- lengths: int32 [16], P('batch'), parts along dimension 0, may hold values from 128 to 512, as said below
Outputs:
- scored: bfloat16 [16, 256, 1024], P(('batch', 'store'), 'blk'), parts along dimension 0
There are 4 independent parts, one for each index of `batch`. A program takes and returns all parts, laid end to end along the dimension named above; an argument that names none is the same for every part. Nothing has to cross between parts.
Inputs may be any that keep to these rules, and one draw needn't show every extreme that they name: A permutation of the users. `lengths`: some user has all 512 events live.
All inputs are finite; a program needn't handle non-finite values.
Results may differ from a plain program's by a relative error of at most 0.014.
Values may be sent and summed in bfloat16 or wider, within the bound.
No kernel may reach another device: no remote copies, remote signals or barrier semaphores. Data moves between devices by JAX's collectives and lax.ppermute only.
A program may use at most 64 MiB of HBM per device.

v0:
```python
import jax
import jax.numpy as jnp
from jax import lax
from jax.sharding import PartitionSpec as P

D = 1024
HEADS = 8


def attend(query, keys, values, offset, count):
    head_size = D // HEADS
    inverse = head_size ** (-0.5)
    rows = query.shape[0]
    local_heads = query.shape[1] // head_size
    total = keys.shape[0]
    block = min(total, 256)
    qheads = query.reshape(rows, local_heads, head_size)
    scale_count = count.astype(jnp.float32)

    def one_block(index, accum):
        start = index * block
        key_block = lax.dynamic_slice_in_dim(keys, start, block, 0).reshape(
            block, local_heads, head_size
        )
        value_block = lax.dynamic_slice_in_dim(values, start, block, 0).reshape(
            block, local_heads, head_size
        )
        scores = (
            jnp.einsum("chd,khd->hck", qheads, key_block, preferred_element_type=jnp.float32)
            * inverse
        )
        live = (offset + start + jnp.arange(block) < count).astype(jnp.float32)
        weights = (jax.nn.silu(scores) * live[None, None, :] / scale_count).astype(jnp.bfloat16)
        part_sum = jnp.einsum(
            "hck,khd->chd", weights, value_block, preferred_element_type=jnp.float32
        )
        return accum + part_sum.reshape(rows, local_heads * head_size)

    empty = jnp.zeros((rows, local_heads * head_size), jnp.float32)
    return lax.fori_loop(0, total // block, one_block, empty)


def finish(attended, gate, norm_gain):
    wide = attended.astype(jnp.float32)
    mean = jnp.mean(wide, axis=1, keepdims=True)
    var = jnp.mean((wide - mean) ** 2, axis=1, keepdims=True)
    normed = (wide - mean) * lax.rsqrt(var + 1e-05) * norm_gain[None, :]
    return (normed * gate.astype(jnp.float32)).astype(jnp.bfloat16)


def per_device(cands, kv_store, proj_weight, norm_gain, users, lengths):
    slot = lax.axis_index("store")
    person = lax.dynamic_index_in_dim(users, slot, 0, keepdims=False)
    count = lax.dynamic_index_in_dim(lengths, person, 0, keepdims=False)
    ordered = jnp.take(kv_store, users, axis=0)
    feats = cands[0]
    fetched = lax.all_to_all(ordered, "store", split_axis=0, concat_axis=1, tiled=True)
    keys = fetched[0, :, 0, :]
    values = fetched[0, :, 1, :]
    offset = lax.axis_index("blk") * keys.shape[0]
    full_weight = lax.all_gather(proj_weight, "blk", axis=2, tiled=True)
    width = full_weight.shape[0]
    own_proj = jnp.dot(
        feats, full_weight.reshape(width, 2 * width), preferred_element_type=jnp.float32
    )
    own_query = own_proj[:, :width].astype(jnp.bfloat16)
    gate = jax.nn.silu(own_proj[:, width:]).astype(jnp.bfloat16)
    query = lax.all_gather(own_query, "blk", axis=0, tiled=True)
    attended = lax.psum_scatter(
        attend(query, keys, values, offset, count), "blk", scatter_dimension=0, tiled=True
    ).astype(jnp.bfloat16)
    return finish(attended, gate, norm_gain)[None]


def solution(mesh):
    in_specs = (
        P(("batch", "store"), "blk", None),
        P("batch", ("blk", "store"), None, None),
        P(None, None, "blk"),
        P(),
        P("batch"),
        P("batch"),
    )
    out_specs = P(("batch", "store"), "blk", None)
    return jax.shard_map(
        per_device, mesh=mesh, in_specs=in_specs, out_specs=out_specs, check_vma=False
    )
```

profile of v0, /device:TPU:0, one launch (start us, length us, event | category | flops | bytes accessed | tf_op | source)
XLA Modules:
  0.0 117.1 jit_solution(7535598614453149541)
XLA Ops:
  6.5 0.0 copy-start
  6.5 0.0 copy-start.3
  6.5 0.0 all-gather.2.cloned.1.call-start
  6.5 0.7 all-gather.2.cloned.1.call-update
  7.3 0.0 copy-done.3
  7.3 0.5 copy-done
  7.8 2.7 %gather_fusion = bf16[4,64,2,1024]{3,2,1,0:T(2,128)(2,1)S(1)} fusion(bf16[4,64,2,1024]{3,2,1,0:T(2,128)(2,1)S(1)} %copy-done, s32[1024]{0:T(1024)S(1)} %pad_clamp_fusion), kind=kCustom, calls=%fused_computation | custom fusion | bytes 2097168 | tf_op jit(solution)/shard_map/jit(_take)/gather | solution.py:55
  10.5 0.0 copy-start.4
  10.5 1.9 %broadcast_select_fusion = bf16[4,64,2,1024]{3,2,1,0:T(2,128)(2,1)} fusion(bf16[4,64,2,1024]{3,2,1,0:T(2,128)(2,1)S(1)} %gather_fusion, pred[4]{0:T(512)(128)(4,1)S(1)} %compare_and_fusion), kind=kLoop, calls=%fused_computation.2 | loop fusion | flops 524288 | bytes 2097156 | tf_op jit(solution)/shard_map/jit(_take)/select_n | solution.py:55
  12.4 4.2 %all-to-all-start = ((bf16[4,64,2,1024]{3,2,1,0:T(2,128)(2,1)}), bf16[4,64,2,1024]{3,2,1,0:T(2,128)(2,1)S(1)}, u32[]{:S(2)}, u32[]{:S(2)}) async-start(bf16[4,64,2,1024]{3,2,1,0:T(2,128)(2,1)} %broadcast_select_fusion), calls=%async_computation | async-start | bytes 2097152 | tf_op jit(solution)/shard_map/all_to_all | solution.py:57
  16.6 0.0 reduce-scatter.2.cloned.1.call-start
  16.6 0.6 dynamic_slice.11
  19.2 0.0 copy-done.4
  19.2 0.6 dynamic_slice.12
  20.4 0.7 compare_convert_fusion
  21.1 10.0 %all-to-all-done = bf16[4,64,2,1024]{3,2,1,0:T(2,128)(2,1)S(1)} async-done(((bf16[4,64,2,1024]{3,2,1,0:T(2,128)(2,1)}), bf16[4,64,2,1024]{3,2,1,0:T(2,128)(2,1)S(1)}, u32[]{:S(2)}, u32[]{:S(2)}) %all-to-all-start) | async-done | bytes 1048608 | tf_op jit(solution)/shard_map/all_to_all | solution.py:57
  31.1 0.3 copy.19
  31.4 0.1 fusion.20
  31.4 1.0 copy.20
  32.5 1.0 copy.21
  33.5 34.9 %all-gather.2.cloned.1.call-done = bf16[1024,2,1024]{2,1,0:T(2,128)(2,1)} async-done(((bf16[1024,2,512]{2,1,0:T(2,128)(2,1)}), bf16[1024,2,1024]{2,1,0:T(2,128)(2,1)}) %all-gather.2.cloned.1.call-update) | async-done | bytes 4194320 | tf_op jit(solution)/shard_map/all_gather | solution.py:61
  68.3 0.0 copy-start.1
  68.3 3.7 %copy.28 = bf16[128,8,2,1024]{3,1,2,0:T(8,128)(2,1)S(1)} copy(bf16[128,8,2,1024]{3,2,1,0:T(2,128)(2,1)} %bitcast.28) | data formatting | bytes 8388608
  72.0 0.0 copy-done.1
  72.0 0.7 fusion.15
  72.8 8.8 %all_gather.7 = bf16[256,1024]{1,0:T(8,128)(2,1)} all-gather(bf16[128,1024]{1,0:T(8,128)(2,1)S(1)} %slice.29), channel_id=1, replica_groups=mesh['store'=4,'blk'=2,'batch'=4] {'blk'}, dimensions={0}, use_global_device_ids=true | all-gather | bytes 786432 | tf_op jit(solution)/shard_map/all_gather | solution.py:68
  81.6 2.4 %fusion = f32[8,128,256]{2,1,0:T(8,128)S(1)} fusion(bf16[256,8,128]{0,2,1:T(8,128)(2,1)} %bitcast.31, bf16[256,8,128]{0,2,1:T(8,128)(2,1)} %bitcast.32, f32[]{:T(128)S(6)} %convert_element_type.32, f32[256]{0:T(256)S(1)} %compare_convert_fusion, bf16[256,1024]{1,0:T(8,128)(2,1)} %all_gather.7), kind=kOutput, calls=%fused_computation.3 | convolution fusion | flops 272629760 | bytes 2622468 | tf_op jit(solution)/shard_map/while/body/eval_jaxpr/hck,khd->chd/dot_general | solution.py:34
  84.1 0.0 copy-start.2
  84.1 1.3 %copy.26 = f32[256,1024]{1,0:T(8,128)} copy(f32[256,1024]{0,1:T(8,128)S(1)} %bitcast.30) | data formatting | bytes 2097152 | tf_op jit(solution)/shard_map/while/body/eval_jaxpr/reshape | solution.py:37
  85.4 0.0 reduce-scatter.2.cloned.1.call-update
  85.4 20.5 %reduce-scatter.2.cloned.1.call-done = f32[128,1024]{1,0:T(8,128)} async-done(((f32[256,1024]{1,0:T(8,128)}), f32[128,1024]{1,0:T(8,128)}) %reduce-scatter.2.cloned.1.call-update) | async-done | bytes 524304 | tf_op jit(solution)/shard_map/reduce_scatter | solution.py:69
  105.9 1.1 convert_reduce_fusion
  107.1 1.2 %fusion.7 = f32[128]{0:T(128)S(1)} fusion(f32[128]{0:T(128)S(1)} %broadcast_multiply_fusion, f32[128,1024]{1,0:T(8,128)} %reduce-scatter.2.cloned.1.call-done), kind=kLoop, calls=%fused_computation.12 | loop fusion | flops 655232 | bytes 525312 | tf_op jit(solution)/shard_map/reduce_sum | solution.py:46
  108.3 0.0 copy-done.2
  108.3 2.0 %fusion.17 = bf16[1,128,1024]{2,1,0:T(8,128)(2,1)} fusion(f32[128,2048]{1,0:T(8,128)S(1)} %fusion.15, f32[1024]{0:T(1024)S(1)} %copy-done.2, f32[128]{0:T(128)S(1)} %add_rsqrt_fusion, f32[128]{0:T(128)S(1)} %broadcast_multiply_fusion, f32[128,1024]{1,0:T(8,128)} %reduce-scatter.2.cloned.1.call-done), kind=kLoop, calls=%fused_computation.22 | loop fusion | flops 1703936 | bytes 1315840 | tf_op jit(solution)/shard_map/broadcast_in_dim | solution.py:72
  (6 shorter events, 0.1 us)
Async XLA Ops:
  6.5 1.2 %copy-start = (bf16[4,64,2,1024]{3,2,1,0:T(2,128)(2,1)S(1)}, bf16[4,64,2,1024]{3,2,1,0:T(2,128)(2,1)}, u32[]{:S(2)}) copy-start(bf16[4,64,2,1024]{3,2,1,0:T(2,128)(2,1)} %param.7) | copy-start | bytes 3145732
  6.5 0.7 copy-start.3
  6.5 61.8 %all-gather.2.cloned.1.call-start = ((), (), s32[]{:S(2)}) async-start(), calls=%async_computation.2 | async-start | bytes 6291456 | tf_op jit(solution)/shard_map/all_gather | solution.py:61
  10.5 8.7 %copy-start.4 = (s32[4]{0:T(128)S(1)}, s32[4]{0:T(128)}, u32[]{:S(2)}) copy-start(s32[4]{0:T(128)} %param.11) | copy-start | bytes 52
  12.4 18.7 %all-to-all-start = ((bf16[4,64,2,1024]{3,2,1,0:T(2,128)(2,1)}), bf16[4,64,2,1024]{3,2,1,0:T(2,128)(2,1)S(1)}, u32[]{:S(2)}, u32[]{:S(2)}) async-start(bf16[4,64,2,1024]{3,2,1,0:T(2,128)(2,1)} %broadcast_select_fusion), calls=%async_computation | async-start | bytes 2097152 | tf_op jit(solution)/shard_map/all_to_all | solution.py:57
  16.6 89.3 %reduce-scatter.2.cloned.1.call-start = ((), (), s32[]{:S(2)}) async-start(), calls=%async_computation.3 | async-start | bytes 1572864 | tf_op jit(solution)/shard_map/reduce_scatter | solution.py:69
  68.3 3.7 %copy-start.1 = (bf16[1,128,1024]{2,1,0:T(8,128)(2,1)S(1)}, bf16[1,128,1024]{2,1,0:T(8,128)(2,1)}, u32[]{:S(2)}) copy-start(bf16[1,128,1024]{2,1,0:T(8,128)(2,1)} %param.6) | copy-start | bytes 786436
  84.1 24.2 %copy-start.2 = (f32[1024]{0:T(1024)S(1)}, f32[1024]{0:T(1024)}, u32[]{:S(2)}) copy-start(f32[1024]{0:T(1024)} %param.9) | copy-start | bytes 12292
Sparse Core Ops, SparseCore 0:
  8.9 59.4 all-gather.1
  85.5 20.3 reduce-scatter.1
where the time goes:
time: 118 us; the launch traced here: 117 us
  waiting for transfers between devices  66.1 us (56%)
  between operations  16.1 us (14%)
  local copies, waits for them, and re-layouts  11.7 us (10%)
  blocking collectives  8.83 us (7%)
  other arithmetic  7 us (6%)
  starting transfers between devices  4.21 us (4%)
  matrix products  3.16 us (3%)
    all_gather x1, waiting for transfers between devices, per_device(): full_weight = lax.all_gather(proj_weight, 'blk', axis=2, tiled=True)  34.9 us
    reduce_scatter x1, waiting for transfers between devices, per_device(): lax.psum_scatter(attend(query, keys, values, offset, count), 'blk', scatt...  20.5 us
    all_to_all x1, waiting for transfers between devices, per_device(): lax.all_to_all(ordered, 'store', split_axis=0, concat_axis=1, tiled=True)  9.99 us
    all_gather x1, blocking collectives, per_device(): query = lax.all_gather(own_query, 'blk', axis=0, tiled=True)  8.83 us
    all_to_all x1, starting transfers between devices, per_device(): lax.all_to_all(ordered, 'store', split_axis=0, concat_axis=1, tiled=True)  4.21 us
    unnamed x11, local copies, waits for them, and re-layouts  4.18 us
    gather x1, local copies, waits for them, and re-layouts, per_device(): ordered = jnp.take(kv_store, users, axis=0)  2.65 us
    dot_general x1, matrix products, one_block(): jnp.einsum('hck,khd->chd', weights, value_block, preferred_element_type=j...  2.44 us
  transfers between devices with their start and end apart: 3, of which 3 were waited for; matrix products, arithmetic and copies ran while one was open for 8% of the time, Pallas kernels for 0%

commit v1 on v0

v1 whole, which is shorter than its diff:
```python
import jax
import jax.numpy as jnp
from jax import lax
from jax.sharding import PartitionSpec as P

D = 1024
HEADS = 8


def attend(query, keys, values, count):
    head_size = D // HEADS
    inverse = head_size ** (-0.5)
    rows = query.shape[0]
    local_heads = query.shape[1] // head_size
    total = keys.shape[0]
    block = min(total, 512)
    qheads = query.reshape(rows, local_heads, head_size)
    scale_count = count.astype(jnp.float32)

    def one_block(index, accum):
        start = index * block
        key_block = lax.dynamic_slice_in_dim(keys, start, block, 0).reshape(
            block, local_heads, head_size
        )
        value_block = lax.dynamic_slice_in_dim(values, start, block, 0).reshape(
            block, local_heads, head_size
        )
        scores = (
            jnp.einsum("chd,khd->hck", qheads, key_block, preferred_element_type=jnp.float32)
            * inverse
        )
        live = (start + jnp.arange(block) < count).astype(jnp.float32)
        weights = (jax.nn.silu(scores) * live[None, None, :] / scale_count).astype(jnp.bfloat16)
        part_sum = jnp.einsum(
            "hck,khd->chd", weights, value_block, preferred_element_type=jnp.float32
        )
        return accum + part_sum.reshape(rows, local_heads * head_size)

    empty = jnp.zeros((rows, local_heads * head_size), jnp.float32)
    steps = total // block
    if steps == 1:
        return one_block(0, empty)
    return lax.fori_loop(0, steps, one_block, empty)


def finish(attended, gate, norm_gain):
    wide = attended.astype(jnp.float32)
    mean = jnp.mean(wide, axis=1, keepdims=True)
    var = jnp.mean((wide - mean) ** 2, axis=1, keepdims=True)
    normed = (wide - mean) * lax.rsqrt(var + 1e-05) * norm_gain[None, :]
    return (normed * gate.astype(jnp.float32)).astype(jnp.bfloat16)


def per_device(cands, kv_store, proj_weight, norm_gain, users, lengths):
    n_blk = lax.axis_size("blk")
    slot = lax.axis_index("store")
    person = lax.dynamic_index_in_dim(users, slot, 0, keepdims=False)
    count = lax.dynamic_index_in_dim(lengths, person, 0, keepdims=False)
    width = proj_weight.shape[0]
    half = proj_weight.shape[2]

    ordered = jnp.take(kv_store, users, axis=0)
    n_users, n_pos = ordered.shape[0], ordered.shape[1]
    ordered = ordered.reshape(n_users, n_pos, 2, n_blk, half)
    ordered = jnp.transpose(ordered, (3, 0, 1, 2, 4)).reshape(n_blk * n_users, n_pos, 2, half)
    fetched = lax.all_to_all(
        ordered, ("blk", "store"), split_axis=0, concat_axis=1, tiled=True
    )
    keys = fetched[0, :, 0, :]
    values = fetched[0, :, 1, :]

    feats = lax.all_gather(cands[0], "blk", axis=0, tiled=True)
    proj = jnp.dot(
        feats, proj_weight.reshape(width, 2 * half), preferred_element_type=jnp.float32
    )
    query = proj[:, :half].astype(jnp.bfloat16)
    gate = jax.nn.silu(proj[:, half:]).astype(jnp.bfloat16)

    attended = attend(query, keys, values, count).astype(jnp.bfloat16)
    rows = attended.shape[0] // n_blk
    both = jnp.stack([attended, gate]).reshape(2, n_blk, rows, half)
    mine = lax.all_to_all(both, "blk", split_axis=1, concat_axis=3, tiled=True)
    mine = mine.reshape(2, rows, n_blk * half)
    return finish(mine[0], mine[1], norm_gain)[None]


def solution(mesh):
    in_specs = (
        P(("batch", "store"), "blk", None),
        P("batch", ("blk", "store"), None, None),
        P(None, None, "blk"),
        P(),
        P("batch"),
        P("batch"),
    )
    out_specs = P(("batch", "store"), "blk", None)
    return jax.shard_map(
        per_device, mesh=mesh, in_specs=in_specs, out_specs=out_specs, check_vma=False
    )
```

time: 118 us -> 51.9 us (0.44)
  waiting for transfers between devices: 66.1 us -> 0.01 us
  blocking collectives: 8.83 us -> 23.9 us
  between operations: 16.1 us -> 2.82 us
  other arithmetic: 7 us -> 3.82 us
  local copies, waits for them, and re-layouts: 11.7 us -> 12.9 us
    all_gather x1 -> x0, waiting for transfers between devices: 34.9 us -> none  [per_device(): full_weight = lax.all_gather(proj_weight, 'blk', axis=2, tiled=True)]
    reduce_scatter x1 -> x0, waiting for transfers between devices: 20.5 us -> none  [per_device(): lax.psum_scatter(attend(query, keys, values, offset, count), 'blk', scatt...]
    all_to_all x0 -> x1, blocking collectives: none -> 10.5 us  [per_device(): mine = lax.all_to_all(both, 'blk', split_axis=1, concat_axis=3, tiled=True)]
    all_to_all x1, waiting for transfers between devices: 9.99 us -> 0.01 us  [per_device(): lax.all_to_all(ordered, ('blk', 'store'), split_axis=0, concat_axis=1, ti...]
    all_gather x1, blocking collectives: 8.83 us -> 13.4 us  [per_device(): feats = lax.all_gather(cands[0], 'blk', axis=0, tiled=True)]
    broadcast_in_dim x1 -> x0, other arithmetic: 1.97 us -> none  [per_device(): return finish(attended, gate, norm_gain)[None]]
    all_to_all x1 -> x2, local copies, waits for them, and re-layouts: 0.27 us -> 1.58 us  [the longest x1 1.31 us: per_device(): lax.all_to_all(ordered, ('blk', 'store'), split_axis=0, concat_axis=1, ti...]
    reshape x1 -> x0, local copies, waits for them, and re-layouts: 1.31 us -> none  [one_block(): return accum + part_sum.reshape(rows, local_heads * head_size)]
  transfers between devices with their start and end apart: 3 -> 1, of which waited for: 3 -> 0; matrix products, arithmetic and copies ran while one was open for 8% -> 9% of each run, Pallas kernels for 0% -> 0%
where the time goes in v1:
time: 51.9 us; the launch traced here: 51.5 us
  blocking collectives  23.9 us (46%)
  local copies, waits for them, and re-layouts  12.9 us (25%)
  starting transfers between devices  5.17 us (10%)
  other arithmetic  3.82 us (7%)
  matrix products  2.88 us (6%)
  between operations  2.82 us (5%)
    all_gather x1, blocking collectives, per_device(): feats = lax.all_gather(cands[0], 'blk', axis=0, tiled=True)  13.4 us
    all_to_all x1, blocking collectives, per_device(): mine = lax.all_to_all(both, 'blk', split_axis=1, concat_axis=3, tiled=True)  10.5 us
    all_to_all x1, starting transfers between devices, per_device(): lax.all_to_all(ordered, ('blk', 'store'), split_axis=0, concat_axis=1, ti...  5.17 us
    gather x2, local copies, waits for them, and re-layouts, per_device(): ordered = jnp.take(kv_store, users, axis=0)  3.37 us
    unnamed x15, local copies, waits for them, and re-layouts  3.19 us
    dot_general x1, matrix products, one_block(): jnp.einsum('hck,khd->chd', weights, value_block, preferred_element_type=j...  2.18 us
    all_to_all x1, local copies, waits for them, and re-layouts, per_device(): lax.all_to_all(ordered, ('blk', 'store'), split_axis=0, concat_axis=1, ti...  1.31 us
    transpose x1, local copies, waits for them, and re-layouts, per_device(): jnp.transpose(ordered, (3, 0, 1, 2, 4))  1.2 us
  transfers between devices with their start and end apart: 1, of which 0 were waited for; matrix products, arithmetic and copies ran while one was open for 9% of the time, Pallas kernels for 0%

profile of v1, /device:TPU:0, one launch (start us, length us, event | category | flops | bytes accessed | tf_op | source)
XLA Modules:
  0.0 51.5 jit_solution(15680569099738875013)
XLA Ops:
  0.0 0.0 copy-start
  0.0 0.7 %compare_select_fusion = s32[4]{0:T(128)S(1)} fusion(s32[4]{0:T(128)} %param.10), kind=kLoop, calls=%fused_computation.28 | loop fusion | flops 12 | bytes 32 | tf_op jit(solution)/shard_map/jit(_take)/jit(_where)/select_n | solution.py:62
  0.8 0.7 %compare_and_fusion = pred[4]{0:T(512)(128)(4,1)S(1)} fusion(s32[4]{0:T(128)} %param.10), kind=kLoop, calls=%fused_computation.31 | loop fusion | flops 24 | bytes 20 | tf_op jit(solution)/shard_map/jit(_take)/and | solution.py:62
  1.4 0.0 copy-done
  1.4 2.7 %gather_fusion = bf16[4,64,2,1024]{3,2,1,0:T(2,128)(2,1)S(1)} fusion(bf16[4,64,2,1024]{3,2,1,0:T(2,128)(2,1)S(1)} %copy-done, s32[1024]{0:T(1024)S(1)} %pad_clamp_fusion), kind=kCustom, calls=%fused_computation | custom fusion | bytes 2097168 | tf_op jit(solution)/shard_map/jit(_take)/gather | solution.py:62
  4.1 0.7 %reshape.180 = bf16[4,64,2,2,512]{4,3,2,1,0:T(2,128)(2,1)S(1)} reshape(bf16[4,64,2,1024]{3,2,1,0:T(2,128)(2,1)S(1)} %gather_fusion) | data formatting | bytes 2097152 | tf_op jit(solution)/shard_map/jit(_take)/gather | solution.py:62
  4.8 1.0 %fusion.7 = bf16[2,4,64,2,512]{4,0,2,3,1:T(2,128)(2,1)S(1)} fusion(bf16[4,64,2,2,512]{4,3,2,1,0:T(2,128)(2,1)S(1)} %reshape.180, pred[4]{0:T(512)(128)(4,1)S(1)} %compare_and_fusion), kind=kLoop, calls=%fused_computation.10 | loop fusion | flops 524288 | bytes 2097156 | tf_op jit(solution)/shard_map/transpose | solution.py:65
  5.8 0.0 copy-start.5
  5.8 1.2 %copy.39 = bf16[2,4,64,2,512]{4,2,3,1,0:T(8,128)(2,1)} copy(bf16[2,4,64,2,512]{4,0,2,3,1:T(2,128)(2,1)S(1)} %fusion.7) | data formatting | bytes 2097152 | tf_op jit(solution)/shard_map/transpose | solution.py:65
  7.0 5.2 %all-to-all-start = ((bf16[8,64,2,512]{3,1,2,0:T(8,128)(2,1)}), bf16[8,64,2,512]{3,1,2,0:T(8,128)(2,1)}, u32[]{:S(2)}, u32[]{:S(2)}) async-start(bf16[8,64,2,512]{3,1,2,0:T(8,128)(2,1)} %bitcast.1), calls=%async_computation | async-start | bytes 2097152 | tf_op jit(solution)/shard_map/all_to_all | solution.py:66
  12.2 0.0 copy-done.5
  12.2 0.6 %dynamic_slice.7 = s32[1]{0:T(128)} dynamic-slice(s32[4]{0:T(128)S(1)} %copy-done.5, s32[]{:T(128)S(6)} %select_n.19), dynamic_slice_sizes={1} | dynamic-slice | bytes 12 | tf_op jit(solution)/shard_map/jit(dynamic_index_in_dim)/dynamic_slice | solution.py:57
  14.1 0.0 copy-start.6
  14.1 0.0 copy-start.3
  14.1 2.2 %copy.52 = bf16[128,8,2,512]{3,1,2,0:T(8,128)(2,1)S(1)} copy(bf16[128,8,2,512]{3,2,1,0:T(2,128)(2,1)} %bitcast.51) | data formatting | bytes 4194304
  16.9 0.0 copy-done.6
  16.9 0.6 %dynamic_slice.8 = s32[1]{0:T(128)} dynamic-slice(s32[4]{0:T(128)S(1)} %copy-done.6, s32[]{:T(128)S(6)} %select_n.20), dynamic_slice_sizes={1} | dynamic-slice | bytes 12 | tf_op jit(solution)/shard_map/jit(dynamic_index_in_dim)/dynamic_slice | solution.py:58
  18.2 0.6 %fusion.19 = f32[512]{0:T(512)S(1)} fusion(s32[]{:T(128)} %bitcast.7), kind=kLoop, calls=%fused_computation.30 | loop fusion | flops 1024 | bytes 2052 | tf_op jit(solution)/shard_map/convert_element_type | solution.py:32
  18.8 0.0 copy-done.3
  18.9 13.4 %all-gather = bf16[1,256,1024]{2,1,0:T(8,128)(2,1)S(1)} all-gather(bf16[1,128,1024]{2,1,0:T(8,128)(2,1)S(1)} %copy-done.3), channel_id=2, replica_groups=mesh['store'=4,'blk'=2,'batch'=4] {'blk'}, dimensions={1}, use_global_device_ids=true | all-gather | bytes 786432 | tf_op jit(solution)/shard_map/all_gather | solution.py:72
  32.2 0.7 %fusion.11 = f32[256,1024]{1,0:T(8,128)S(1)} fusion(bf16[1024,1024]{1,0:T(8,128)(2,1)S(1)} %bitcast.46, bf16[1,256,1024]{2,1,0:T(8,128)(2,1)S(1)} %all-gather), kind=kOutput, calls=%fused_computation.18 | convolution fusion | flops 536870912 | bytes 3670016 | tf_op jit(solution)/shard_map/dot_general | solution.py:73
  33.0 0.0 copy-start.1
  33.0 1.0 %copy-done.1 = f32[256,1024]{1,0:T(8,128)} copy-done((f32[256,1024]{1,0:T(8,128)}, f32[256,1024]{1,0:T(8,128)S(1)}, u32[]{:S(2)}) %copy-start.1) | copy-done | bytes 1048600
  33.9 0.1 multiply_convert_fusion
  34.1 0.0 all-to-all-done
  34.1 1.3 %copy.40 = bf16[8,64,2,512]{3,1,0,2:T(8,128)(2,1)S(1)} copy(bf16[8,64,2,512]{3,1,2,0:T(8,128)(2,1)} %all-to-all-done) | data formatting | bytes 2097152 | tf_op jit(solution)/shard_map/all_to_all | solution.py:66
  35.4 0.0 copy-start.2
  35.4 0.1 fusion.22
  35.5 1.0 %copy.41 = bf16[1,512,1,512]{1,3,2,0:T(8,128)(2,1)} copy(bf16[1,512,1,512]{3,1,2,0:T(8,128)(2,1)S(1)} %get-tuple-element.6) | data formatting | bytes 1048576 | tf_op jit(solution)/shard_map/slice | solution.py:70
  36.5 0.2 copy.42
  36.7 0.0 copy-done.2
  36.7 2.2 %fusion.2 = bf16[256,4,128]{0,2,1:T(8,128)(2,1)S(1)} fusion(bf16[512,4,128]{0,2,1:T(8,128)(2,1)} %bitcast.53, bf16[512,4,128]{0,2,1:T(8,128)(2,1)S(1)} %bitcast.54, f32[]{:T(128)S(6)} %convert_element_type.75, f32[512]{0:T(512)S(1)} %fusion.19, f32[256,1024]{1,0:T(8,128)S(1)} %copy-done.2), kind=kOutput, calls=%fused_computation.5 | convolution fusion | flops 272760832 | bytes 1574916 | tf_op jit(solution)/shard_map/hck,khd->chd/dot_general | solution.py:34
  38.9 0.1 convert_element_type.79
  39.0 0.2 copy.45
  39.2 0.1 pad_maximum_fusion
  39.2 0.0 copy-start.4
  39.2 10.5 %all_to_all.27 = bf16[2,2,128,512]{3,2,0,1:T(8,128)(2,1)S(1)} all-to-all(bf16[2,2,128,512]{3,2,0,1:T(8,128)(2,1)S(1)} %pad_maximum_fusion), channel_id=1, replica_groups=mesh['store'=4,'blk'=2,'batch'=4] {'blk'}, dimensions={1} | all-to-all | bytes 1048576 | tf_op jit(solution)/shard_map/all_to_all | solution.py:82
  49.7 0.3 copy.47
  50.0 0.1 fusion.23
  50.1 0.2 fusion.18
  50.2 0.2 multiply_reduce_fusion
  50.4 0.0 copy-done.4
  50.4 0.2 fusion.8
  50.6 0.9 %copy.48 = bf16[1,128,1024]{2,1,0:T(8,128)(2,1)} copy(bf16[1,128,1024]{1,2,0:T(8,128)(2,1)S(1)} %fusion.8) | data formatting | bytes 524288 | tf_op jit(solution)/shard_map/convert_element_type | solution.py:51
  (3 shorter events, 0.0 us)
Async XLA Ops:
  0.0 1.4 %copy-start = (bf16[4,64,2,1024]{3,2,1,0:T(2,128)(2,1)S(1)}, bf16[4,64,2,1024]{3,2,1,0:T(2,128)(2,1)}, u32[]{:S(2)}) copy-start(bf16[4,64,2,1024]{3,2,1,0:T(2,128)(2,1)} %param.7) | copy-start | bytes 3145732
  5.8 6.4 %copy-start.5 = (s32[4]{0:T(128)S(1)}, s32[4]{0:T(128)}, u32[]{:S(2)}) copy-start(s32[4]{0:T(128)} %param.10) | copy-start | bytes 52
  7.0 27.1 %all-to-all-start = ((bf16[8,64,2,512]{3,1,2,0:T(8,128)(2,1)}), bf16[8,64,2,512]{3,1,2,0:T(8,128)(2,1)}, u32[]{:S(2)}, u32[]{:S(2)}) async-start(bf16[8,64,2,512]{3,1,2,0:T(8,128)(2,1)} %bitcast.1), calls=%async_computation | async-start | bytes 2097152 | tf_op jit(solution)/shard_map/all_to_all | solution.py:66
  14.1 2.9 %copy-start.6 = (s32[4]{0:T(128)S(1)}, s32[4]{0:T(128)}, u32[]{:S(2)}) copy-start(s32[4]{0:T(128)} %param.11) | copy-start | bytes 52
  14.1 4.8 %copy-start.3 = (bf16[1,128,1024]{2,1,0:T(8,128)(2,1)S(1)}, bf16[1,128,1024]{2,1,0:T(8,128)(2,1)}, u32[]{:S(2)}) copy-start(bf16[1,128,1024]{2,1,0:T(8,128)(2,1)} %param.6) | copy-start | bytes 786436
  33.0 1.0 %copy-start.1 = (f32[256,1024]{1,0:T(8,128)}, f32[256,1024]{1,0:T(8,128)S(1)}, u32[]{:S(2)}) copy-start(f32[256,1024]{1,0:T(8,128)S(1)} %fusion.11) | copy-start | bytes 3145732
  35.4 1.3 %copy-start.2 = (f32[256,1024]{1,0:T(8,128)S(1)}, f32[256,1024]{1,0:T(8,128)}, u32[]{:S(2)}) copy-start(f32[256,1024]{1,0:T(8,128)} %copy-done.1) | copy-start | bytes 3145732
  39.2 11.1 %copy-start.4 = (f32[1024]{0:T(1024)S(1)}, f32[1024]{0:T(1024)}, u32[]{:S(2)}) copy-start(f32[1024]{0:T(1024)} %param.9) | copy-start | bytes 12292

commit v2 on v1

--- a/solution.py
+++ b/solution.py
@@ -2,6 +2,8 @@
 import jax.numpy as jnp
 from jax import lax
 from jax.sharding import PartitionSpec as P
+from jax.experimental import pallas as pl
+from jax.experimental.pallas import tpu as pltpu
 
 D = 1024
 HEADS = 8
@@ -51,37 +53,89 @@
     return (normed * gate.astype(jnp.float32)).astype(jnp.bfloat16)
 
 
+def gather_kv(kv_store, users, n_blk):
+    n_users, n_pos, two, width = kv_store.shape
+    half = width // n_blk
+    targets = n_blk * n_users
+
+    def kernel(users_ref, kv_hbm, out_hbm, sems):
+        def start(t, carry):
+            b = t // n_users
+            s = t % n_users
+            pltpu.make_async_copy(
+                kv_hbm.at[users_ref[s], :, :, pl.ds(pl.multiple_of(b * half, 128), half)],
+                out_hbm.at[t],
+                sems.at[t],
+            ).start()
+            return carry
+
+        def wait(t, carry):
+            pltpu.make_async_copy(
+                kv_hbm.at[0, :, :, pl.ds(0, half)], out_hbm.at[t], sems.at[t]
+            ).wait()
+            return carry
+
+        lax.fori_loop(0, targets, start, 0)
+        lax.fori_loop(0, targets, wait, 0)
+
+    return pl.pallas_call(
+        kernel,
+        out_shape=jax.ShapeDtypeStruct((targets, n_pos, two, half), kv_store.dtype),
+        grid_spec=pltpu.PrefetchScalarGridSpec(
+            num_scalar_prefetch=1,
+            grid=(1,),
+            in_specs=[pl.BlockSpec(memory_space=pl.ANY)],
+            out_specs=pl.BlockSpec(memory_space=pl.ANY),
+            scratch_shapes=[pltpu.SemaphoreType.DMA((targets,))],
+        ),
+    )(users, kv_store)
+
+
 def per_device(cands, kv_store, proj_weight, norm_gain, users, lengths):
     n_blk = lax.axis_size("blk")
+    blk = lax.axis_index("blk")
     slot = lax.axis_index("store")
     person = lax.dynamic_index_in_dim(users, slot, 0, keepdims=False)
     count = lax.dynamic_index_in_dim(lengths, person, 0, keepdims=False)
-    width = proj_weight.shape[0]
     half = proj_weight.shape[2]
 
-    ordered = jnp.take(kv_store, users, axis=0)
-    n_users, n_pos = ordered.shape[0], ordered.shape[1]
-    ordered = ordered.reshape(n_users, n_pos, 2, n_blk, half)
-    ordered = jnp.transpose(ordered, (3, 0, 1, 2, 4)).reshape(n_blk * n_users, n_pos, 2, half)
+    ordered = gather_kv(kv_store, users, n_blk)
     fetched = lax.all_to_all(
         ordered, ("blk", "store"), split_axis=0, concat_axis=1, tiled=True
     )
     keys = fetched[0, :, 0, :]
     values = fetched[0, :, 1, :]
 
-    feats = lax.all_gather(cands[0], "blk", axis=0, tiled=True)
-    proj = jnp.dot(
-        feats, proj_weight.reshape(width, 2 * half), preferred_element_type=jnp.float32
-    )
-    query = proj[:, :half].astype(jnp.bfloat16)
-    gate = jax.nn.silu(proj[:, half:]).astype(jnp.bfloat16)
+    mine = cands[0]
+    rows = mine.shape[0]
+    if n_blk == 2:
+        swap = [(0, 1), (1, 0)]
+        peer = lax.ppermute(mine, "blk", swap)
+        proj = jnp.einsum(
+            "cd,dkh->kch", jnp.concatenate([peer, mine]), proj_weight,
+            preferred_element_type=jnp.float32,
+        )
+        query = proj[0].astype(jnp.bfloat16)
+        gate = jax.nn.silu(proj[1]).astype(jnp.bfloat16)
+        sent = attend(query[:rows], keys, values, count).astype(jnp.bfloat16)
+        back = lax.ppermute(jnp.stack([sent, gate[:rows]]), "blk", swap)
+        kept = attend(query[rows:], keys, values, count).astype(jnp.bfloat16)
+        first = blk == 0
+        attended = jnp.where(first, jnp.concatenate([kept, back[0]], axis=1),
+                             jnp.concatenate([back[0], kept], axis=1))
+        gate_own = jnp.where(first, jnp.concatenate([gate[rows:], back[1]], axis=1),
+                             jnp.concatenate([back[1], gate[rows:]], axis=1))
+        return finish(attended, gate_own, norm_gain)[None]
 
+    feats = lax.all_gather(mine, "blk", axis=0, tiled=True)
+    proj = jnp.einsum("cd,dkh->kch", feats, proj_weight, preferred_element_type=jnp.float32)
+    query = proj[0].astype(jnp.bfloat16)
+    gate = jax.nn.silu(proj[1]).astype(jnp.bfloat16)
     attended = attend(query, keys, values, count).astype(jnp.bfloat16)
-    rows = attended.shape[0] // n_blk
     both = jnp.stack([attended, gate]).reshape(2, n_blk, rows, half)
-    mine = lax.all_to_all(both, "blk", split_axis=1, concat_axis=3, tiled=True)
-    mine = mine.reshape(2, rows, n_blk * half)
-    return finish(mine[0], mine[1], norm_gain)[None]
+    own = lax.all_to_all(both, "blk", split_axis=1, concat_axis=3, tiled=True)
+    own = own.reshape(2, rows, n_blk * half)
+    return finish(own[0], own[1], norm_gain)[None]
 
 
 def solution(mesh):

time: 51.9 us -> 77.7 us (1.50)
  Pallas kernels: 0 us -> 33.6 us
  blocking collectives: 23.9 us -> 0 us
  waiting for transfers between devices: 0.01 us -> 9.84 us
  matrix products: 2.88 us -> 6.96 us
  starting transfers between devices: 5.17 us -> 7.14 us
    pallas_call x0 -> x1, Pallas kernels: none -> 33.6 us  [gather_kv(): pl.pallas_call(kernel, out_shape=jax.ShapeDtypeStruct((targets, n_pos, tw...]
    all_gather x1 -> x0, blocking collectives: 13.4 us -> none  [per_device(): feats = lax.all_gather(cands[0], 'blk', axis=0, tiled=True)]
    all_to_all x1 -> x0, blocking collectives: 10.5 us -> none  [per_device(): mine = lax.all_to_all(both, 'blk', split_axis=1, concat_axis=3, tiled=True)]
    all_to_all x1, waiting for transfers between devices: 0.01 us -> 5.55 us  [per_device(): lax.all_to_all(ordered, ('blk', 'store'), split_axis=0, concat_axis=1, ti...]
    ppermute x0 -> x2, waiting for transfers between devices: none -> 4.29 us  [the longest x1 4.28 us: per_device(): back = lax.ppermute(jnp.stack([sent, gate[:rows]]), 'blk', swap)]
    ppermute x0 -> x2, starting transfers between devices: none -> 3.58 us  [the longest x1 3.04 us: per_device(): peer = lax.ppermute(mine, 'blk', swap)]
    gather x2 -> x0, local copies, waits for them, and re-layouts: 3.37 us -> none  [per_device(): ordered = jnp.take(kv_store, users, axis=0)]
    slice x2 -> x1, local copies, waits for them, and re-layouts: 0.28 us -> 2.44 us  [per_device(): keys = fetched[0, :, 0, :]]
  transfers between devices with their start and end apart: 1 -> 3, of which waited for: 0 -> 2; matrix products, arithmetic and copies ran while one was open for 9% -> 12% of each run, Pallas kernels for 0% -> 44%
where the time goes in v2:
time: 77.7 us; the launch traced here: 77.2 us
  Pallas kernels  33.6 us (43%)
  local copies, waits for them, and re-layouts  13.1 us (17%)
  waiting for transfers between devices  9.84 us (13%)
  starting transfers between devices  7.14 us (9%)
  matrix products  6.96 us (9%)
  other arithmetic  3.79 us (5%)
  between operations  2.74 us (4%)
    pallas_call x1, Pallas kernels, gather_kv(): pl.pallas_call(kernel, out_shape=jax.ShapeDtypeStruct((targets, n_pos, tw...  33.6 us
    all_to_all x1, waiting for transfers between devices, per_device(): lax.all_to_all(ordered, ('blk', 'store'), split_axis=0, concat_axis=1, ti...  5.55 us
    ppermute x1, waiting for transfers between devices, per_device(): back = lax.ppermute(jnp.stack([sent, gate[:rows]]), 'blk', swap)  4.28 us
    dot_general x2, matrix products, one_block(): jnp.einsum('hck,khd->chd', weights, value_block, preferred_element_type=j...  4.27 us
    unnamed x19, local copies, waits for them, and re-layouts  3.61 us
    all_to_all x1, starting transfers between devices, per_device(): lax.all_to_all(ordered, ('blk', 'store'), split_axis=0, concat_axis=1, ti...  3.57 us
    ppermute x1, starting transfers between devices, per_device(): peer = lax.ppermute(mine, 'blk', swap)  3.04 us
    dot_general x1, matrix products, per_device(): jnp.einsum('cd,dkh->kch', jnp.concatenate([peer, mine]), proj_weight, pre...  2.69 us
  transfers between devices with their start and end apart: 3, of which 2 were waited for; matrix products, arithmetic and copies ran while one was open for 12% of the time, Pallas kernels for 44%

profile of v2, /device:TPU:0, one launch (start us, length us, event | category | flops | bytes accessed | tf_op | source)
XLA Modules:
  0.0 77.2 jit_solution(18006608257982580038)
XLA Ops:
  0.0 0.0 copy-start
  0.0 0.0 copy-start.6
  0.0 0.0 copy-start.8
  0.0 0.0 copy-start.7
  0.0 3.0 %collective-permute-start = (bf16[128,1024]{1,0:T(8,128)(2,1)}, bf16[128,1024]{1,0:T(8,128)(2,1)}, u32[]{:S(2)}, u32[]{:S(2)}) collective-permute-start(bf16[128,1024]{1,0:T(8,128)(2,1)} %bitcast.43), channel_id=1, source_target_pairs={{0,4},{4,0},{1,5},{5,1},{2,6},{6,2},{3,7},{7,3},{8,12},{12,8},{9,1... | collective-permute-start | bytes 786440 | tf_op jit(solution)/shard_map/ppermute | solution.py:113
  3.1 33.6 %shard_map.64 = bf16[8,64,2,512]{3,2,1,0:T(2,128)(2,1)} custom-call(s32[4]{0:T(128)} %users_ref.1, bf16[4,64,2,1024]{3,2,1,0:T(2,128)(2,1)} %kv_hbm.1), custom_call_target="tpu_custom_call" | custom-call | tf_op jit(solution)/shard_map/pallas_call | solution.py:81
  36.7 3.6 %all-to-all-start = ((bf16[8,64,2,512]{3,2,1,0:T(2,128)(2,1)}), bf16[8,64,2,512]{3,2,1,0:T(2,128)(2,1)S(1)}, u32[]{:S(2)}, u32[]{:S(2)}) async-start(bf16[8,64,2,512]{3,2,1,0:T(2,128)(2,1)} %shard_map.64), calls=%async_computation | async-start | bytes 2097152 | tf_op jit(solution)/shard_map/all_to_all | solution.py:103
  40.2 0.0 copy-done.6
  40.3 0.6 dynamic_slice.7
  42.8 0.0 copy-done.8
  42.8 0.6 dynamic_slice.8
  44.0 0.6 fusion.21
  44.7 0.0 collective-permute-done
  44.7 0.0 copy-done
  44.7 0.0 copy-done.7
  44.7 2.7 %fusion.29 = (bf16[2,256,512]{2,1,0:T(8,128)(2,1)S(1)}, f32[2,256,512]{2,1,0:T(8,128)}) fusion(bf16[1024,2,512]{2,1,0:T(2,128)(2,1)S(1)} %copy-done, bf16[128,1024]{1,0:T(8,128)(2,1)S(1)} %bitcast.44, bf16[128,1024]{1,0:T(8,128)(2,1)} %collective-permute-done), kind=kOutput, calls=%fused_computation.47 | convolution fusion | flops 538181632 | bytes 4194304 | tf_op jit(solution)/shard_map/cd,dkh->kch/dot_general | solution.py:114
  47.4 0.7 reshape.226
  48.1 0.7 reshape.227
  48.8 1.2 %multiply_convert_fusion.1 = bf16[256,512]{1,0:T(8,128)(2,1)S(1)} fusion(f32[2,256,512]{2,1,0:T(8,128)} %get-tuple-element.15), kind=kLoop, calls=%fused_computation.18 | loop fusion | flops 655360 | bytes 786432 | tf_op jit(solution)/shard_map/convert_element_type | solution.py:119
  50.0 5.6 %all-to-all-done = bf16[8,64,2,512]{3,2,1,0:T(2,128)(2,1)S(1)} async-done(((bf16[8,64,2,512]{3,2,1,0:T(2,128)(2,1)}), bf16[8,64,2,512]{3,2,1,0:T(2,128)(2,1)S(1)}, u32[]{:S(2)}, u32[]{:S(2)}) %all-to-all-start) | async-done | bytes 1048608 | tf_op jit(solution)/shard_map/all_to_all | solution.py:103
  55.6 2.4 %fusion.27 = (bf16[1,512,1,512]{3,2,1,0:T(2,128)(2,1)}, bf16[1,512,1,512]{3,2,1,0:T(2,128)(2,1)}) fusion(bf16[1,512,2,512]{3,2,1,0:T(2,128)(2,1)S(1)} %bitcast.35), kind=kLoop, calls=%fused_computation.45 | loop fusion | bytes 2097152 | tf_op jit(solution)/shard_map/slice | solution.py:106
  58.0 0.0 copy-start.1
  58.0 0.0 copy-start.4
  58.0 3.6 %copy.29 = bf16[1,512,1,512]{1,3,2,0:T(8,128)(2,1)} copy(bf16[1,512,1,512]{3,2,1,0:T(2,128)(2,1)} %get-tuple-element.5) | data formatting | bytes 1048576
  61.6 0.0 copy-done.1
  61.6 2.3 %copy.14 = bf16[1,512,1,512]{1,3,2,0:T(8,128)(2,1)} copy(bf16[1,512,1,512]{3,2,1,0:T(2,128)(2,1)S(1)} %copy-done.1) | data formatting | bytes 1048576 | tf_op jit(solution)/shard_map/slice | solution.py:107
  63.9 0.0 copy-done.4
  63.9 0.0 copy-start.2
  63.9 0.0 copy-start.3
  63.9 2.7 %convolution_convert_fusion = bf16[4,128,128]{2,1,0:T(8,128)(2,1)} fusion(bf16[512,4,128]{0,2,1:T(8,128)(2,1)} %bitcast.38, bf16[512,4,128]{0,2,1:T(8,128)(2,1)} %bitcast.36, f32[]{:T(128)S(6)} %convert_element_type.90, f32[512]{0:T(512)S(1)} %fusion.21, bf16[128,4,128]{2,1,0:T(4,128)(2,1)S(1)} %copy-done.4), kind=kOutput, calls=%fused_computation.5 | convolution fusion | flops 136380416 | bytes 1312772 | tf_op jit(solution)/shard_map/hck,khd->chd/dot_general | solution.py:36
  66.5 1.0 %copy.27 = bf16[1,128,512]{2,1,0:T(8,128)(2,1)S(1)} copy(bf16[1,128,512]{1,2,0:T(8,128)(2,1)} %bitcast.42) | data formatting | bytes 262144 | tf_op jit(solution)/shard_map/convert_element_type | solution.py:120
  67.6 0.7 pad_maximum_fusion
  68.3 0.0 copy-start.5
  68.3 0.5 collective-permute-start.1
  68.8 0.0 copy-done.2
  68.8 0.0 copy-done.3
  68.8 1.6 %convolution_convert_fusion.1 = bf16[4,128,128]{2,1,0:T(8,128)(2,1)S(1)} fusion(bf16[512,4,128]{0,2,1:T(8,128)(2,1)S(1)} %bitcast.39, bf16[512,4,128]{0,2,1:T(8,128)(2,1)S(1)} %bitcast.37, f32[]{:T(128)S(6)} %convert_element_type.90, f32[512]{0:T(512)S(1)} %fusion.21, bf16[128,4,128]{2,1,0:T(4,128)(2,1)} %reshape.226), kind=kOutput, calls=%fused_computation.6 | convolution fusion | flops 136380416 | bytes 1312772 | tf_op jit(solution)/shard_map/hck,khd->chd/dot_general | solution.py:36
  70.4 0.1 copy.28
  70.6 0.1 copy.26
  70.7 4.3 %collective-permute-done.1 = bf16[2,128,512]{2,1,0:T(8,128)(2,1)} collective-permute-done((bf16[2,128,512]{2,1,0:T(8,128)(2,1)}, bf16[2,128,512]{2,1,0:T(8,128)(2,1)}, u32[]{:S(2)}, u32[]{:S(2)}) %collective-permute-start.1) | collective-permute-done | bytes 262176 | tf_op jit(solution)/shard_map/ppermute | solution.py:121
  75.0 1.0 %slice_bitcast_fusion.3 = (bf16[128,512]{1,0:T(8,128)(2,1)S(1)}, bf16[1,128,512]{2,1,0:T(8,128)(2,1)S(1)}, bf16[1,128,512]{2,1,0:T(8,128)(2,1)S(1)}) fusion(bf16[2,128,512]{2,1,0:T(8,128)(2,1)} %collective-permute-done.1), kind=kLoop, calls=%fused_computation.44 | loop fusion | bytes 655360 | tf_op jit(solution)/shard_map/squeeze | solution.py:124
  76.0 0.1 convert_reduce_fusion
  76.1 0.2 fusion.6
  76.3 0.0 copy-done.5
  76.3 0.9 %multiply_convert_fusion = bf16[1,128,1024]{2,1,0:T(8,128)(2,1)} fusion(bf16[1,128,512]{2,1,0:T(8,128)(2,1)S(1)} %get-tuple-element.11, bf16[1,128,512]{2,1,0:T(8,128)(2,1)S(1)} %copy.26, bf16[1,128,512]{2,1,0:T(8,128)(2,1)S(1)} %get-tuple-element.10, bf16[1,128,512]{2,1,0:T(8,128)(2,1)S(1)} %get-tuple-element.12, f32[1024]{0:T(1024)S(1)} %copy-done.5, ...), kind=kLoop, calls=%fused_computation.17 | loop fusion | flops 3276800 | bytes 791553 | tf_op jit(solution)/shard_map/convert_element_type | solution.py:53
  (4 shorter events, 0.1 us)
Async XLA Ops:
  0.0 44.7 %copy-start = (bf16[1024,2,512]{2,1,0:T(2,128)(2,1)S(1)}, bf16[1024,2,512]{2,1,0:T(2,128)(2,1)}, u32[]{:S(2)}) copy-start(bf16[1024,2,512]{2,1,0:T(2,128)(2,1)} %param.8) | copy-start | bytes 6291460
  0.0 40.2 %copy-start.6 = (s32[4]{0:T(128)S(1)}, s32[4]{0:T(128)}, u32[]{:S(2)}) copy-start(s32[4]{0:T(128)} %users_ref.1) | copy-start | bytes 52
  0.0 42.8 %copy-start.8 = (s32[4]{0:T(128)S(1)}, s32[4]{0:T(128)}, u32[]{:S(2)}) copy-start(s32[4]{0:T(128)} %param.11) | copy-start | bytes 52
  0.0 44.7 %copy-start.7 = (bf16[1,128,1024]{2,1,0:T(8,128)(2,1)S(1)}, bf16[1,128,1024]{2,1,0:T(8,128)(2,1)}, u32[]{:S(2)}) copy-start(bf16[1,128,1024]{2,1,0:T(8,128)(2,1)} %param.6) | copy-start | bytes 786436
  0.0 44.7 %collective-permute-start = (bf16[128,1024]{1,0:T(8,128)(2,1)}, bf16[128,1024]{1,0:T(8,128)(2,1)}, u32[]{:S(2)}, u32[]{:S(2)}) collective-permute-start(bf16[128,1024]{1,0:T(8,128)(2,1)} %bitcast.43), channel_id=1, source_target_pairs={{0,4},{4,0},{1,5},{5,1},{2,6},{6,2},{3,7},{7,3},{8,12},{12,8},{9,1... | collective-permute-start | bytes 786440 | tf_op jit(solution)/shard_map/ppermute | solution.py:113
  36.7 18.9 %all-to-all-start = ((bf16[8,64,2,512]{3,2,1,0:T(2,128)(2,1)}), bf16[8,64,2,512]{3,2,1,0:T(2,128)(2,1)S(1)}, u32[]{:S(2)}, u32[]{:S(2)}) async-start(bf16[8,64,2,512]{3,2,1,0:T(2,128)(2,1)} %shard_map.64), calls=%async_computation | async-start | bytes 2097152 | tf_op jit(solution)/shard_map/all_to_all | solution.py:103
  58.0 3.6 %copy-start.1 = (bf16[1,512,1,512]{3,2,1,0:T(2,128)(2,1)S(1)}, bf16[1,512,1,512]{3,2,1,0:T(2,128)(2,1)}, u32[]{:S(2)}) copy-start(bf16[1,512,1,512]{3,2,1,0:T(2,128)(2,1)} %get-tuple-element.6) | copy-start | bytes 1572868
  58.0 5.9 %copy-start.4 = (bf16[128,4,128]{2,1,0:T(4,128)(2,1)S(1)}, bf16[128,4,128]{2,1,0:T(4,128)(2,1)}, u32[]{:S(2)}) copy-start(bf16[128,4,128]{2,1,0:T(4,128)(2,1)} %reshape.227) | copy-start | bytes 393220
  63.9 4.9 %copy-start.2 = (bf16[1,512,1,512]{1,3,2,0:T(8,128)(2,1)S(1)}, bf16[1,512,1,512]{1,3,2,0:T(8,128)(2,1)}, u32[]{:S(2)}) copy-start(bf16[1,512,1,512]{1,3,2,0:T(8,128)(2,1)} %copy.29) | copy-start | bytes 1572868
  63.9 4.9 %copy-start.3 = (bf16[1,512,1,512]{1,3,2,0:T(8,128)(2,1)S(1)}, bf16[1,512,1,512]{1,3,2,0:T(8,128)(2,1)}, u32[]{:S(2)}) copy-start(bf16[1,512,1,512]{1,3,2,0:T(8,128)(2,1)} %copy.14) | copy-start | bytes 1572868
  68.3 8.0 %copy-start.5 = (f32[1024]{0:T(1024)S(1)}, f32[1024]{0:T(1024)}, u32[]{:S(2)}) copy-start(f32[1024]{0:T(1024)} %param.9) | copy-start | bytes 12292
  68.3 6.7 %collective-permute-start.1 = (bf16[2,128,512]{2,1,0:T(8,128)(2,1)}, bf16[2,128,512]{2,1,0:T(8,128)(2,1)}, u32[]{:S(2)}, u32[]{:S(2)}) collective-permute-start(bf16[2,128,512]{2,1,0:T(8,128)(2,1)} %pad_maximum_fusion), channel_id=1, source_target_pairs={{0,4},{4,0},{1,5},{5,1},{2,6},{6,2},{3,7},{7,3},{8,12},{12,8},{9,1... | collective-permute-start | bytes 786440 | tf_op jit(solution)/shard_map/ppermute | solution.py:121

commit v3 on v1

v3 whole, which is shorter than its diff:
```python
import jax
import jax.numpy as jnp
from jax import lax
from jax.sharding import PartitionSpec as P

D = 1024
HEADS = 8
HEAD_SIZE = D // HEADS


def attend(qheads, keys, values, count):
    inverse = HEAD_SIZE ** (-0.5)
    local_heads, rows, _ = qheads.shape
    total = keys.shape[1]
    block = min(total, 512)
    scale_count = count.astype(jnp.float32)

    def one_block(index, accum):
        start = index * block
        key_block = lax.dynamic_slice_in_dim(keys, start, block, 1)
        value_block = lax.dynamic_slice_in_dim(values, start, block, 1)
        scores = (
            jnp.einsum("hcd,hkd->hck", qheads, key_block, preferred_element_type=jnp.float32)
            * inverse
        )
        live = (start + jnp.arange(block) < count).astype(jnp.float32)
        weights = (jax.nn.silu(scores) * live[None, None, :] / scale_count).astype(jnp.bfloat16)
        part_sum = jnp.einsum(
            "hck,hkd->chd", weights, value_block, preferred_element_type=jnp.float32
        )
        return accum + part_sum.reshape(rows, local_heads * HEAD_SIZE)

    empty = jnp.zeros((rows, local_heads * HEAD_SIZE), jnp.float32)
    steps = total // block
    if steps == 1:
        return one_block(0, empty)
    return lax.fori_loop(0, steps, one_block, empty)


def finish(attended, gate, norm_gain):
    wide = attended.astype(jnp.float32)
    mean = jnp.mean(wide, axis=1, keepdims=True)
    var = jnp.mean((wide - mean) ** 2, axis=1, keepdims=True)
    normed = (wide - mean) * lax.rsqrt(var + 1e-05) * norm_gain[None, :]
    return (normed * gate.astype(jnp.float32)).astype(jnp.bfloat16)


def per_device(cands, kv_store, proj_weight, norm_gain, users, lengths):
    n_blk = lax.axis_size("blk")
    blk = lax.axis_index("blk")
    slot = lax.axis_index("store")
    person = lax.dynamic_index_in_dim(users, slot, 0, keepdims=False)
    count = lax.dynamic_index_in_dim(lengths, person, 0, keepdims=False)
    half = proj_weight.shape[2]
    local_heads = half // HEAD_SIZE

    n_users, n_pos = kv_store.shape[0], kv_store.shape[1]
    ordered = jnp.take(kv_store, users, axis=0).reshape(
        n_users, n_pos, 2, n_blk, local_heads, HEAD_SIZE
    )
    ordered = jnp.transpose(ordered, (3, 0, 2, 4, 1, 5)).reshape(
        n_blk * n_users, 2, local_heads, n_pos, HEAD_SIZE
    )
    fetched = lax.all_to_all(
        ordered, ("blk", "store"), split_axis=0, concat_axis=3, tiled=True
    )
    keys = fetched[0, 0]
    values = fetched[0, 1]

    mine = cands[0]
    rows = mine.shape[0]

    def project(feats):
        proj = jnp.einsum("cd,dkh->kch", feats, proj_weight, preferred_element_type=jnp.float32)
        query = proj[0].astype(jnp.bfloat16).reshape(-1, local_heads, HEAD_SIZE)
        gate = jax.nn.silu(proj[1]).astype(jnp.bfloat16)
        return jnp.transpose(query, (1, 0, 2)), gate

    if n_blk == 2:
        swap = [(0, 1), (1, 0)]
        peer = lax.ppermute(mine, "blk", swap)
        query_own, gate_own = project(mine)
        query_peer, gate_peer = project(peer)
        sent = attend(query_peer, keys, values, count).astype(jnp.bfloat16)
        back = lax.ppermute(jnp.stack([sent, gate_peer]), "blk", swap)
        kept = attend(query_own, keys, values, count).astype(jnp.bfloat16)
        first = blk == 0
        attended = jnp.where(first, jnp.concatenate([kept, back[0]], axis=1),
                             jnp.concatenate([back[0], kept], axis=1))
        gate_full = jnp.where(first, jnp.concatenate([gate_own, back[1]], axis=1),
                              jnp.concatenate([back[1], gate_own], axis=1))
        return finish(attended, gate_full, norm_gain)[None]

    feats = lax.all_gather(mine, "blk", axis=0, tiled=True)
    query, gate = project(feats)
    attended = attend(query, keys, values, count).astype(jnp.bfloat16)
    both = jnp.stack([attended, gate]).reshape(2, n_blk, rows, half)
    own = lax.all_to_all(both, "blk", split_axis=1, concat_axis=3, tiled=True)
    own = own.reshape(2, rows, n_blk * half)
    return finish(own[0], own[1], norm_gain)[None]


def solution(mesh):
    in_specs = (
        P(("batch", "store"), "blk", None),
        P("batch", ("blk", "store"), None, None),
        P(None, None, "blk"),
        P(),
        P("batch"),
        P("batch"),
    )
    out_specs = P(("batch", "store"), "blk", None)
    return jax.shard_map(
        per_device, mesh=mesh, in_specs=in_specs, out_specs=out_specs, check_vma=False
    )
```

time: 51.9 us -> 42.5 us (0.82)
  blocking collectives: 23.9 us -> 0 us
  waiting for transfers between devices: 0.01 us -> 5.95 us
  starting transfers between devices: 5.17 us -> 9.17 us
  other arithmetic: 3.82 us -> 5.91 us
  matrix products: 2.88 us -> 4.61 us
  local copies, waits for them, and re-layouts: 12.9 us -> 13.6 us
    all_gather x1 -> x0, blocking collectives: 13.4 us -> none  [per_device(): feats = lax.all_gather(cands[0], 'blk', axis=0, tiled=True)]
    all_to_all x1 -> x0, blocking collectives: 10.5 us -> none  [per_device(): mine = lax.all_to_all(both, 'blk', split_axis=1, concat_axis=3, tiled=True)]
    ppermute x0 -> x2, waiting for transfers between devices: none -> 5.94 us  [the longest x1 5.94 us: per_device(): back = lax.ppermute(jnp.stack([sent, gate_peer]), 'blk', swap)]
    ppermute x0 -> x2, starting transfers between devices: none -> 4.93 us  [the longest x1 2.97 us: per_device(): peer = lax.ppermute(mine, 'blk', swap)]
    unnamed x15 -> x13, local copies, waits for them, and re-layouts: 3.19 us -> 5.59 us
    convert_element_type x1 -> x2, other arithmetic: 0.14 us -> 2.06 us  [project(): gate = jax.nn.silu(proj[1]).astype(jnp.bfloat16)]
    dot_general x2 -> x4, matrix products: 2.88 us -> 4.61 us  [the longest x2 3.16 us: project(): jnp.einsum('cd,dkh->kch', feats, proj_weight, preferred_element_type=jnp....]
    transpose x1 -> x0, local copies, waits for them, and re-layouts: 1.2 us -> none  [per_device(): jnp.transpose(ordered, (3, 0, 1, 2, 4))]
  transfers between devices with their start and end apart: 1 -> 3, of which waited for: 0 -> 1; matrix products, arithmetic and copies ran while one was open for 9% -> 47% of each run, Pallas kernels for 0% -> 0%
where the time goes in v3:
time: 42.5 us; the launch traced here: 42 us
  local copies, waits for them, and re-layouts  13.6 us (32%)
  starting transfers between devices  9.17 us (22%)
  waiting for transfers between devices  5.95 us (14%)
  other arithmetic  5.91 us (14%)
  matrix products  4.61 us (11%)
  between operations  2.79 us (7%)
    ppermute x1, waiting for transfers between devices, per_device(): back = lax.ppermute(jnp.stack([sent, gate_peer]), 'blk', swap)  5.94 us
    unnamed x13, local copies, waits for them, and re-layouts  5.59 us
    all_to_all x1, starting transfers between devices, per_device(): lax.all_to_all(ordered, ('blk', 'store'), split_axis=0, concat_axis=3, ti...  4.24 us
    gather x2, local copies, waits for them, and re-layouts, per_device(): jnp.take(kv_store, users, axis=0)  3.37 us
    dot_general x2, matrix products, project(): jnp.einsum('cd,dkh->kch', feats, proj_weight, preferred_element_type=jnp....  3.16 us
    ppermute x1, starting transfers between devices, per_device(): peer = lax.ppermute(mine, 'blk', swap)  2.97 us
    convert_element_type x2, other arithmetic, project(): gate = jax.nn.silu(proj[1]).astype(jnp.bfloat16)  2.06 us
    ppermute x1, starting transfers between devices, per_device(): back = lax.ppermute(jnp.stack([sent, gate_peer]), 'blk', swap)  1.96 us
  transfers between devices with their start and end apart: 3, of which 1 were waited for; matrix products, arithmetic and copies ran while one was open for 47% of the time, Pallas kernels for 0%

profile of v3, /device:TPU:0, one launch (start us, length us, event | category | flops | bytes accessed | tf_op | source)
XLA Modules:
  0.0 42.0 jit_solution(6818854181658717820)
XLA Ops:
  0.0 0.0 copy-start
  0.0 3.0 %collective-permute-start = (bf16[128,1024]{1,0:T(8,128)(2,1)}, bf16[128,1024]{1,0:T(8,128)(2,1)}, u32[]{:S(2)}, u32[]{:S(2)}) collective-permute-start(bf16[128,1024]{1,0:T(8,128)(2,1)} %bitcast.59), channel_id=1, source_target_pairs={{0,4},{4,0},{1,5},{5,1},{2,6},{6,2},{3,7},{7,3},{8,12},{12,8},{9,1... | collective-permute-start | bytes 786440 | tf_op jit(solution)/shard_map/ppermute | solution.py:81
  3.0 0.7 %compare_and_fusion = pred[4]{0:T(512)(128)(4,1)S(1)} fusion(s32[4]{0:T(128)} %param.10), kind=kLoop, calls=%fused_computation.41 | loop fusion | flops 24 | bytes 20 | tf_op jit(solution)/shard_map/jit(_take)/and | solution.py:58
  3.6 0.7 %compare_select_fusion = s32[4]{0:T(128)S(1)} fusion(s32[4]{0:T(128)} %param.10), kind=kLoop, calls=%fused_computation.38 | loop fusion | flops 12 | bytes 32 | tf_op jit(solution)/shard_map/jit(_take)/jit(_where)/select_n | solution.py:58
  4.3 0.0 copy-done
  4.3 2.7 %gather_fusion = bf16[4,64,2,1024]{3,2,1,0:T(2,128)(2,1)S(1)} fusion(bf16[4,64,2,1024]{3,2,1,0:T(2,128)(2,1)S(1)} %copy-done, s32[1024]{0:T(1024)S(1)} %pad_clamp_fusion), kind=kCustom, calls=%fused_computation | custom fusion | bytes 2097168 | tf_op jit(solution)/shard_map/jit(_take)/gather | solution.py:58
  7.0 0.7 %gather.7 = bf16[4,64,2,2,4,128]{5,4,3,2,1,0:T(4,128)(2,1)S(1)} reshape(bf16[4,64,2,1024]{3,2,1,0:T(2,128)(2,1)S(1)} %gather_fusion) | data formatting | bytes 2097152 | tf_op jit(solution)/shard_map/jit(_take)/gather | solution.py:58
  7.7 1.3 %copy_select_fusion = bf16[4,64,2,2,4,128]{5,1,4,2,0,3:T(8,128)(2,1)} fusion(bf16[4,64,2,2,4,128]{5,4,3,2,1,0:T(4,128)(2,1)S(1)} %gather.7, pred[4]{0:T(512)(128)(4,1)S(1)} %compare_and_fusion), kind=kLoop, calls=%fused_computation.7 | loop fusion | flops 524288 | bytes 2097156 | tf_op jit(solution)/shard_map/jit(_take)/select_n | solution.py:58
  9.0 4.2 %all-to-all-start = ((bf16[8,2,4,64,128]{4,3,2,1,0:T(8,128)(2,1)}), bf16[8,2,4,64,128]{4,3,2,1,0:T(8,128)(2,1)}, u32[]{:S(2)}, u32[]{:S(2)}) async-start(bf16[8,2,4,64,128]{4,3,2,1,0:T(8,128)(2,1)} %bitcast.1), calls=%async_computation | async-start | bytes 2097152 | tf_op jit(solution)/shard_map/all_to_all | solution.py:64
  13.2 0.0 copy-start.2
  13.2 4.8 %copy.17 = bf16[1024,2,512]{0,2,1:T(8,128)(2,1)S(1)} copy(bf16[1024,2,512]{2,1,0:T(2,128)(2,1)} %param.8) | data formatting | bytes 4194304 | tf_op args[2]
  18.0 0.0 copy-done.2
  18.0 0.0 copy-start.4
  18.0 0.0 copy-start.5
  18.0 1.5 %convolution_bitcast_fusion.1 = f32[2,128,512]{1,2,0:T(8,128)} fusion(bf16[1024,2,512]{0,2,1:T(8,128)(2,1)S(1)} %copy.17, bf16[1,128,1024]{2,1,0:T(8,128)(2,1)S(1)} %copy-done.2), kind=kOutput, calls=%fused_computation.4 | convolution fusion | flops 268435456 | bytes 2883584 | tf_op jit(solution)/shard_map/cd,dkh->kch/dot_general | solution.py:74
  19.5 0.0 copy-done.4
  19.5 0.6 %dynamic_slice.7 = s32[1]{0:T(128)} dynamic-slice(s32[4]{0:T(128)S(1)} %copy-done.4, s32[]{:T(128)S(6)} %select_n.50), dynamic_slice_sizes={1} | dynamic-slice | bytes 12 | tf_op jit(solution)/shard_map/jit(dynamic_index_in_dim)/dynamic_slice | solution.py:52
  22.1 0.0 copy-done.5
  22.1 0.6 %dynamic_slice.8 = s32[1]{0:T(128)} dynamic-slice(s32[4]{0:T(128)S(1)} %copy-done.5, s32[]{:T(128)S(6)} %select_n.51), dynamic_slice_sizes={1} | dynamic-slice | bytes 12 | tf_op jit(solution)/shard_map/jit(dynamic_index_in_dim)/dynamic_slice | solution.py:53
  22.7 0.6 %fusion.16 = f32[512]{0:T(512)S(1)} fusion(s32[]{:T(128)} %bitcast.13), kind=kLoop, calls=%fused_computation.40 | loop fusion | flops 1024 | bytes 2052 | tf_op jit(solution)/shard_map/convert_element_type | solution.py:26
  24.0 1.0 %slice.60 = bf16[1,128,512]{1,2,0:T(8,128)(2,1)S(1)} slice(f32[2,128,512]{1,2,0:T(8,128)} %convolution_bitcast_fusion.1), slice={[0:1], [0:128], [0:512]} | slice | bytes 262144 | tf_op jit(solution)/shard_map/slice | solution.py:75
  24.9 0.1 copy.18
  25.1 1.0 %multiply_convert_fusion.1 = bf16[1,128,512]{1,2,0:T(8,128)(2,1)S(1)} fusion(f32[2,128,512]{1,2,0:T(8,128)} %convolution_bitcast_fusion.1), kind=kLoop, calls=%fused_computation.33 | loop fusion | flops 327680 | bytes 393216 | tf_op jit(solution)/shard_map/convert_element_type | solution.py:76
  26.1 0.0 collective-permute-done
  26.1 1.7 %convolution_bitcast_fusion = f32[2,128,512]{1,2,0:T(8,128)S(1)} fusion(bf16[1024,2,512]{0,2,1:T(8,128)(2,1)S(1)} %copy.17, bf16[128,1024]{1,0:T(8,128)(2,1)} %collective-permute-done), kind=kOutput, calls=%fused_computation.3 | convolution fusion | flops 268435456 | bytes 2883584 | tf_op jit(solution)/shard_map/cd,dkh->kch/dot_general | solution.py:74
  27.8 0.0 copy-start.1
  27.8 0.8 %copy-done.1 = f32[2,128,512]{1,2,0:T(8,128)} copy-done((f32[2,128,512]{1,2,0:T(8,128)}, f32[2,128,512]{1,2,0:T(8,128)S(1)}, u32[]{:S(2)}) %copy-start.1) | copy-done | bytes 524312
  28.6 0.1 copy.21
  28.7 1.0 %multiply_convert_fusion.2 = bf16[1,128,512]{1,2,0:T(8,128)(2,1)S(1)} fusion(f32[2,128,512]{1,2,0:T(8,128)} %copy-done.1), kind=kLoop, calls=%fused_computation.34 | loop fusion | flops 327680 | bytes 393216 | tf_op jit(solution)/shard_map/convert_element_type | solution.py:76
  29.8 0.0 all-to-all-done
  29.8 1.3 %copy.16 = bf16[1,2,4,8,64,128]{5,4,3,2,1,0:T(8,128)(2,1)S(1)} copy(bf16[1,2,4,8,64,128]{5,4,2,1,3,0:T(8,128)(2,1)} %bitcast.3) | data formatting | bytes 2097152 | tf_op jit(solution)/shard_map/all_to_all | solution.py:64
  31.1 0.7 %convolution_convert_fusion = bf16[4,128,128]{2,1,0:T(8,128)(2,1)S(1)} fusion(f32[]{:T(128)S(6)} %convert_element_type.104, f32[512]{0:T(512)S(1)} %fusion.16, bf16[1,2,4,512,128]{4,3,2,1,0:T(8,128)(2,1)S(1)} %bitcast.55, bf16[128,4,128]{2,0,1:T(8,128)(2,1)S(1)} %copy.21), kind=kOutput, calls=%fused_computation.5 | convolution fusion | flops 136380416 | bytes 1312772 | tf_op jit(solution)/shard_map/hck,hkd->chd/dot_general | solution.py:28
  31.9 0.0 copy-start.3
  31.9 2.0 %collective-permute-start.1 = (bf16[2,128,512]{1,2,0:T(8,128)(2,1)S(1)}, bf16[2,128,512]{1,2,0:T(8,128)(2,1)S(1)}, u32[]{:S(2)}, u32[]{:S(2)}) collective-permute-start(bf16[2,128,512]{1,2,0:T(8,128)(2,1)S(1)} %pad_maximum_fusion), channel_id=1, source_target_pairs={{0,4},{4,0},{1,5},{5,1},{2,6},{6,2},{3,7},{7,3},{8,12},{12,8},{9,1... | collective-permute-start | bytes 786440 | tf_op jit(solution)/shard_map/ppermute | solution.py:85
  33.8 0.7 %convolution_convert_fusion.1 = bf16[4,128,128]{2,1,0:T(8,128)(2,1)S(1)} fusion(f32[]{:T(128)S(6)} %convert_element_type.104, f32[512]{0:T(512)S(1)} %fusion.16, bf16[1,2,4,512,128]{4,3,2,1,0:T(8,128)(2,1)S(1)} %bitcast.56, bf16[128,4,128]{2,0,1:T(8,128)(2,1)S(1)} %copy.18), kind=kOutput, calls=%fused_computation.6 | convolution fusion | flops 136380416 | bytes 1312772 | tf_op jit(solution)/shard_map/hck,hkd->chd/dot_general | solution.py:28
  34.6 5.9 %collective-permute-done.1 = bf16[2,128,512]{1,2,0:T(8,128)(2,1)S(1)} collective-permute-done((bf16[2,128,512]{1,2,0:T(8,128)(2,1)S(1)}, bf16[2,128,512]{1,2,0:T(8,128)(2,1)S(1)}, u32[]{:S(2)}, u32[]{:S(2)}) %collective-permute-start.1) | collective-permute-done | bytes 262176 | tf_op jit(solution)/shard_map/ppermute | solution.py:85
  40.6 0.2 convert_reduce_fusion
  40.7 0.2 fusion.1
  40.9 0.0 copy-done.3
  40.9 0.2 multiply_convert_fusion
  41.1 0.9 %copy.23 = bf16[1,128,1024]{2,1,0:T(8,128)(2,1)} copy(bf16[1,128,1024]{1,2,0:T(8,128)(2,1)S(1)} %multiply_convert_fusion) | data formatting | bytes 524288 | tf_op jit(solution)/shard_map/convert_element_type | solution.py:45
  (6 shorter events, 0.1 us)
Async XLA Ops:
  0.0 4.3 %copy-start = (bf16[4,64,2,1024]{3,2,1,0:T(2,128)(2,1)S(1)}, bf16[4,64,2,1024]{3,2,1,0:T(2,128)(2,1)}, u32[]{:S(2)}) copy-start(bf16[4,64,2,1024]{3,2,1,0:T(2,128)(2,1)} %param.7) | copy-start | bytes 3145732
  0.0 26.1 %collective-permute-start = (bf16[128,1024]{1,0:T(8,128)(2,1)}, bf16[128,1024]{1,0:T(8,128)(2,1)}, u32[]{:S(2)}, u32[]{:S(2)}) collective-permute-start(bf16[128,1024]{1,0:T(8,128)(2,1)} %bitcast.59), channel_id=1, source_target_pairs={{0,4},{4,0},{1,5},{5,1},{2,6},{6,2},{3,7},{7,3},{8,12},{12,8},{9,1... | collective-permute-start | bytes 786440 | tf_op jit(solution)/shard_map/ppermute | solution.py:81
  9.0 20.8 %all-to-all-start = ((bf16[8,2,4,64,128]{4,3,2,1,0:T(8,128)(2,1)}), bf16[8,2,4,64,128]{4,3,2,1,0:T(8,128)(2,1)}, u32[]{:S(2)}, u32[]{:S(2)}) async-start(bf16[8,2,4,64,128]{4,3,2,1,0:T(8,128)(2,1)} %bitcast.1), calls=%async_computation | async-start | bytes 2097152 | tf_op jit(solution)/shard_map/all_to_all | solution.py:64
  13.2 4.8 %copy-start.2 = (bf16[1,128,1024]{2,1,0:T(8,128)(2,1)S(1)}, bf16[1,128,1024]{2,1,0:T(8,128)(2,1)}, u32[]{:S(2)}) copy-start(bf16[1,128,1024]{2,1,0:T(8,128)(2,1)} %param.6) | copy-start | bytes 786436
  18.0 1.5 %copy-start.4 = (s32[4]{0:T(128)S(1)}, s32[4]{0:T(128)}, u32[]{:S(2)}) copy-start(s32[4]{0:T(128)} %param.10) | copy-start | bytes 52
  18.0 4.0 %copy-start.5 = (s32[4]{0:T(128)S(1)}, s32[4]{0:T(128)}, u32[]{:S(2)}) copy-start(s32[4]{0:T(128)} %param.11) | copy-start | bytes 52
  27.8 0.8 %copy-start.1 = (f32[2,128,512]{1,2,0:T(8,128)}, f32[2,128,512]{1,2,0:T(8,128)S(1)}, u32[]{:S(2)}) copy-start(f32[2,128,512]{1,2,0:T(8,128)S(1)} %convolution_bitcast_fusion) | copy-start | bytes 1572868
  31.9 9.0 %copy-start.3 = (f32[1024]{0:T(1024)S(1)}, f32[1024]{0:T(1024)}, u32[]{:S(2)}) copy-start(f32[1024]{0:T(1024)} %param.9) | copy-start | bytes 12292
  31.9 8.6 %collective-permute-start.1 = (bf16[2,128,512]{1,2,0:T(8,128)(2,1)S(1)}, bf16[2,128,512]{1,2,0:T(8,128)(2,1)S(1)}, u32[]{:S(2)}, u32[]{:S(2)}) collective-permute-start(bf16[2,128,512]{1,2,0:T(8,128)(2,1)S(1)} %pad_maximum_fusion), channel_id=1, source_target_pairs={{0,4},{4,0},{1,5},{5,1},{2,6},{6,2},{3,7},{7,3},{8,12},{12,8},{9,1... | collective-permute-start | bytes 786440 | tf_op jit(solution)/shard_map/ppermute | solution.py:85

commit v4 on v3

--- a/solution.py
+++ b/solution.py
@@ -55,7 +55,7 @@
     local_heads = half // HEAD_SIZE
 
     n_users, n_pos = kv_store.shape[0], kv_store.shape[1]
-    ordered = jnp.take(kv_store, users, axis=0).reshape(
+    ordered = kv_store.at[users].get(mode="promise_in_bounds", unique_indices=True).reshape(
         n_users, n_pos, 2, n_blk, local_heads, HEAD_SIZE
     )
     ordered = jnp.transpose(ordered, (3, 0, 2, 4, 1, 5)).reshape(
@@ -71,7 +71,7 @@
     rows = mine.shape[0]
 
     def project(feats):
-        proj = jnp.einsum("cd,dkh->kch", feats, proj_weight, preferred_element_type=jnp.float32)
+        proj = jnp.einsum("cd,dkh->ckh", feats, proj_weight, preferred_element_type=jnp.float32).transpose(1, 0, 2)
         query = proj[0].astype(jnp.bfloat16).reshape(-1, local_heads, HEAD_SIZE)
         gate = jax.nn.silu(proj[1]).astype(jnp.bfloat16)
         return jnp.transpose(query, (1, 0, 2)), gate

time: 42.5 us -> 53.9 us (1.27)
  waiting for transfers between devices: 5.95 us -> 15.7 us
  matrix products: 4.61 us -> 6.94 us
  starting transfers between devices: 9.17 us -> 7.68 us
  local copies, waits for them, and re-layouts: 13.6 us -> 14.9 us
    ppermute x1, waiting for transfers between devices: 0.01 us -> 9.77 us  [per_device(): peer = lax.ppermute(mine, 'blk', swap)]
    unnamed x13 -> x14, local copies, waits for them, and re-layouts: 5.59 us -> 0.82 us
    reshape x0 -> x2, local copies, waits for them, and re-layouts: none -> 4.01 us  [per_device(): kv_store.at[users].get(mode='promise_in_bounds', unique_indices=True)]
    dot_general x2, matrix products: 1.45 us -> 4.31 us  [one_block(): jnp.einsum('hck,hkd->chd', weights, value_block, preferred_element_type=j...]
    ppermute x1, starting transfers between devices: 1.96 us -> 0.36 us  [per_device(): back = lax.ppermute(jnp.stack([sent, gate_peer]), 'blk', swap)]
    select_n x2 -> x1, other arithmetic: 1.93 us -> 0.81 us  [per_device(): kv_store.at[users].get(mode='promise_in_bounds', unique_indices=True)]
    all_to_all x1, starting transfers between devices: 4.24 us -> 5.3 us  [per_device(): lax.all_to_all(ordered, ('blk', 'store'), split_axis=0, concat_axis=3, ti...]
    squeeze x1, local copies, waits for them, and re-layouts: 0.04 us -> 0.99 us  [per_device(): back[0]]
  transfers between devices with their start and end apart: 3 -> 3, of which waited for: 1 -> 2; matrix products, arithmetic and copies ran while one was open for 47% -> 19% of each run, Pallas kernels for 0% -> 0%
where the time goes in v4:
time: 53.9 us; the launch traced here: 53.4 us
  waiting for transfers between devices  15.7 us (29%)
  local copies, waits for them, and re-layouts  14.9 us (28%)
  starting transfers between devices  7.68 us (14%)
  matrix products  6.94 us (13%)
  other arithmetic  5.48 us (10%)
  between operations  2.71 us (5%)
    ppermute x1, waiting for transfers between devices, per_device(): peer = lax.ppermute(mine, 'blk', swap)  9.77 us
    ppermute x1, waiting for transfers between devices, per_device(): back = lax.ppermute(jnp.stack([sent, gate_peer]), 'blk', swap)  5.92 us
    all_to_all x1, starting transfers between devices, per_device(): lax.all_to_all(ordered, ('blk', 'store'), split_axis=0, concat_axis=3, ti...  5.3 us
    dot_general x2, matrix products, one_block(): jnp.einsum('hck,hkd->chd', weights, value_block, preferred_element_type=j...  4.31 us
    reshape x2, local copies, waits for them, and re-layouts, per_device(): kv_store.at[users].get(mode='promise_in_bounds', unique_indices=True)  4.01 us
    gather x1, local copies, waits for them, and re-layouts, per_device(): kv_store.at[users].get(mode='promise_in_bounds', unique_indices=True)  3.88 us
    dot_general x2, matrix products, project(): jnp.einsum('cd,dkh->ckh', feats, proj_weight, preferred_element_type=jnp....  2.64 us
    convert_element_type x2, other arithmetic, project(): gate = jax.nn.silu(proj[1]).astype(jnp.bfloat16)  2.05 us
  transfers between devices with their start and end apart: 3, of which 2 were waited for; matrix products, arithmetic and copies ran while one was open for 19% of the time, Pallas kernels for 0%

profile of v4, /device:TPU:0, one launch (start us, length us, event | category | flops | bytes accessed | tf_op | source)
XLA Modules:
  0.0 53.4 jit_solution(15917443855258609171)
XLA Ops:
  0.0 0.0 copy-start
  0.0 0.8 %compare_select_fusion = s32[4]{0:T(128)S(1)} fusion(s32[4]{0:T(128)} %param.10), kind=kLoop, calls=%fused_computation.43 | loop fusion | flops 12 | bytes 32 | tf_op jit(solution)/shard_map/select_n | solution.py:58
  0.8 3.9 %gather_fusion = bf16[4,64,2,1024]{3,2,1,0:T(2,128)(2,1)S(1)} fusion(bf16[4,64,2,1024]{3,2,1,0:T(2,128)(2,1)} %param.7, s32[1024]{0:T(1024)S(1)} %pad_clamp_fusion), kind=kCustom, calls=%fused_computation | custom fusion | bytes 2097168 | tf_op jit(solution)/shard_map/gather | solution.py:58
  4.7 1.5 %reshape.218 = bf16[4,64,2,2,4,128]{5,4,3,2,1,0:T(4,128)(2,1)} reshape(bf16[4,64,2,1024]{3,2,1,0:T(2,128)(2,1)S(1)} %gather_fusion) | data formatting | bytes 2097152 | tf_op jit(solution)/shard_map/reshape | solution.py:58
  6.2 0.0 copy-start.4
  6.2 2.5 %copy.17 = bf16[4,64,2,2,4,128]{5,1,4,2,0,3:T(8,128)(2,1)} copy(bf16[4,64,2,2,4,128]{5,4,3,2,1,0:T(4,128)(2,1)} %reshape.218) | data formatting | bytes 2097152 | tf_op jit(solution)/shard_map/reshape | solution.py:58
  8.7 0.0 copy-start.5
  8.7 0.0 copy-start.6
  8.7 5.3 %all-to-all-start = ((bf16[8,2,4,64,128]{4,3,2,1,0:T(8,128)(2,1)}), bf16[8,2,4,64,128]{4,3,2,1,0:T(8,128)(2,1)S(1)}, u32[]{:S(2)}, u32[]{:S(2)}) async-start(bf16[8,2,4,64,128]{4,3,2,1,0:T(8,128)(2,1)} %bitcast.49), calls=%async_computation | async-start | bytes 2097152 | tf_op jit(solution)/shard_map/all_to_all | solution.py:64
  14.0 0.0 copy-done.4
  14.0 2.0 %collective-permute-start = (bf16[128,1024]{1,0:T(8,128)(2,1)S(1)}, bf16[128,1024]{1,0:T(8,128)(2,1)}, u32[]{:S(2)}, u32[]{:S(2)}) collective-permute-start(bf16[128,1024]{1,0:T(8,128)(2,1)S(1)} %bitcast.55), channel_id=1, source_target_pairs={{0,4},{4,0},{1,5},{5,1},{2,6},{6,2},{3,7},{7,3},{8,12},{12,8},{9,1... | collective-permute-start | bytes 786440 | tf_op jit(solution)/shard_map/ppermute | solution.py:81
  16.1 0.0 copy-done
  16.1 1.2 %fusion.4 = f32[2,128,512]{2,1,0:T(8,128)} fusion(bf16[1024,2,512]{2,1,0:T(2,128)(2,1)S(1)} %copy-done, bf16[1,128,1024]{2,1,0:T(8,128)(2,1)S(1)} %copy-done.4), kind=kOutput, calls=%fused_computation.7 | convolution fusion | flops 268435456 | bytes 2883584 | tf_op jit(solution)/shard_map/cd,dkh->ckh/dot_general | solution.py:74
  17.3 0.0 copy-done.5
  17.3 0.6 %dynamic_slice.7 = s32[1]{0:T(128)} dynamic-slice(s32[4]{0:T(128)S(1)} %copy-done.5, s32[]{:T(128)S(6)} %select_n.42), dynamic_slice_sizes={1} | dynamic-slice | bytes 12 | tf_op jit(solution)/shard_map/jit(dynamic_index_in_dim)/dynamic_slice | solution.py:52
  19.8 0.0 copy-done.6
  19.8 0.6 %dynamic_slice.8 = s32[1]{0:T(128)} dynamic-slice(s32[4]{0:T(128)S(1)} %copy-done.6, s32[]{:T(128)S(6)} %select_n.43), dynamic_slice_sizes={1} | dynamic-slice | bytes 12 | tf_op jit(solution)/shard_map/jit(dynamic_index_in_dim)/dynamic_slice | solution.py:53
  20.4 0.6 %fusion.30 = f32[512]{0:T(512)S(1)} fusion(s32[]{:T(128)} %bitcast.12), kind=kLoop, calls=%fused_computation.45 | loop fusion | flops 1024 | bytes 2052 | tf_op jit(solution)/shard_map/convert_element_type | solution.py:26
  21.7 1.0 %slice.60 = bf16[1,128,512]{2,1,0:T(8,128)(2,1)S(1)} slice(f32[2,128,512]{2,1,0:T(8,128)} %fusion.4), slice={[0:1], [0:128], [0:512]} | slice | bytes 262144 | tf_op jit(solution)/shard_map/slice | solution.py:75
  22.7 0.7 %convert_element_type.102 = bf16[128,4,128]{2,1,0:T(4,128)(2,1)} reshape(bf16[1,128,512]{2,1,0:T(8,128)(2,1)S(1)} %slice.60) | data formatting | bytes 262144 | tf_op jit(solution)/shard_map/convert_element_type | solution.py:75
  23.4 1.0 %multiply_convert_fusion.1 = bf16[1,128,512]{2,1,0:T(8,128)(2,1)S(1)} fusion(f32[2,128,512]{2,1,0:T(8,128)} %fusion.4), kind=kLoop, calls=%fused_computation.36 | loop fusion | flops 327680 | bytes 393216 | tf_op jit(solution)/shard_map/convert_element_type | solution.py:76
  24.4 9.8 %collective-permute-done = bf16[128,1024]{1,0:T(8,128)(2,1)} collective-permute-done((bf16[128,1024]{1,0:T(8,128)(2,1)S(1)}, bf16[128,1024]{1,0:T(8,128)(2,1)}, u32[]{:S(2)}, u32[]{:S(2)}) %collective-permute-start) | collective-permute-done | bytes 262176 | tf_op jit(solution)/shard_map/ppermute | solution.py:81
  34.2 1.4 %fusion.7 = f32[2,128,512]{2,1,0:T(8,128)S(1)} fusion(bf16[1024,2,512]{2,1,0:T(2,128)(2,1)S(1)} %copy-done, bf16[128,1024]{1,0:T(8,128)(2,1)} %collective-permute-done), kind=kOutput, calls=%fused_computation.8 | convolution fusion | flops 268435456 | bytes 2883584 | tf_op jit(solution)/shard_map/cd,dkh->ckh/dot_general | solution.py:74
  35.6 0.0 copy-start.2
  35.6 0.8 %copy-done.2 = f32[2,128,512]{2,1,0:T(8,128)} copy-done((f32[2,128,512]{2,1,0:T(8,128)}, f32[2,128,512]{2,1,0:T(8,128)S(1)}, u32[]{:S(2)}) %copy-start.2) | copy-done | bytes 524312
  36.5 1.0 %multiply_convert_fusion.2 = bf16[1,128,512]{2,1,0:T(8,128)(2,1)S(1)} fusion(f32[2,128,512]{2,1,0:T(8,128)} %copy-done.2), kind=kLoop, calls=%fused_computation.37 | loop fusion | flops 327680 | bytes 393216 | tf_op jit(solution)/shard_map/convert_element_type | solution.py:76
  37.5 0.0 all-to-all-done
  37.5 1.1 %copy.18 = bf16[1,2,4,8,64,128]{5,4,3,2,1,0:T(8,128)(2,1)} copy(bf16[1,2,4,8,64,128]{5,4,2,1,3,0:T(8,128)(2,1)S(1)} %bitcast.48) | data formatting | bytes 2097152 | tf_op jit(solution)/shard_map/all_to_all | solution.py:64
  38.6 0.0 copy-start.1
  38.6 2.7 %convolution_convert_fusion = bf16[4,128,128]{2,1,0:T(8,128)(2,1)} fusion(f32[]{:T(128)S(6)} %convert_element_type.104, f32[512]{0:T(512)S(1)} %fusion.30, bf16[1,2,4,512,128]{4,3,2,1,0:T(8,128)(2,1)} %bitcast.50, bf16[128,4,128]{2,1,0:T(4,128)(2,1)S(1)} %convert_element_type.108), kind=kOutput, calls=%fused_computation.9 | convolution fusion | flops 136380416 | bytes 1312772 | tf_op jit(solution)/shard_map/hck,hkd->chd/dot_general | solution.py:28
  41.3 1.0 %copy.31 = bf16[1,128,512]{2,1,0:T(8,128)(2,1)S(1)} copy(bf16[1,128,512]{1,2,0:T(8,128)(2,1)} %bitcast.54) | data formatting | bytes 262144 | tf_op jit(solution)/shard_map/convert_element_type | solution.py:84
  42.3 0.7 %pad_maximum_fusion = bf16[2,128,512]{2,1,0:T(8,128)(2,1)} fusion(bf16[1,128,512]{2,1,0:T(8,128)(2,1)S(1)} %multiply_convert_fusion.2, bf16[1,128,512]{2,1,0:T(8,128)(2,1)S(1)} %copy.31), kind=kLoop, calls=%fused_computation.30 | loop fusion | flops 131072 | bytes 524288 | tf_op jit(solution)/shard_map/stack | solution.py:85
  43.0 0.0 copy-start.3
  43.0 0.4 collective-permute-start.1
  43.4 0.0 copy-done.1
  43.4 1.6 %convolution_convert_fusion.1 = bf16[4,128,128]{2,1,0:T(8,128)(2,1)S(1)} fusion(f32[]{:T(128)S(6)} %convert_element_type.104, f32[512]{0:T(512)S(1)} %fusion.30, bf16[1,2,4,512,128]{4,3,2,1,0:T(8,128)(2,1)S(1)} %bitcast.51, bf16[128,4,128]{2,1,0:T(4,128)(2,1)} %convert_element_type.102), kind=kOutput, calls=%fused_computation.10 | convolution fusion | flops 136380416 | bytes 1312772 | tf_op jit(solution)/shard_map/hck,hkd->chd/dot_general | solution.py:28
  45.0 0.1 copy.32
  45.1 0.1 copy.30
  45.2 5.9 %collective-permute-done.1 = bf16[2,128,512]{2,1,0:T(8,128)(2,1)} collective-permute-done((bf16[2,128,512]{2,1,0:T(8,128)(2,1)}, bf16[2,128,512]{2,1,0:T(8,128)(2,1)}, u32[]{:S(2)}, u32[]{:S(2)}) %collective-permute-start.1) | collective-permute-done | bytes 262176 | tf_op jit(solution)/shard_map/ppermute | solution.py:85
  51.2 1.0 %slice_bitcast_fusion.8 = (bf16[128,512]{1,0:T(8,128)(2,1)S(1)}, bf16[1,128,512]{2,1,0:T(8,128)(2,1)S(1)}, bf16[1,128,512]{2,1,0:T(8,128)(2,1)S(1)}) fusion(bf16[2,128,512]{2,1,0:T(8,128)(2,1)} %collective-permute-done.1), kind=kLoop, calls=%fused_computation.52 | loop fusion | bytes 655360 | tf_op jit(solution)/shard_map/squeeze | solution.py:88
  52.2 0.1 convert_reduce_fusion
  52.3 0.2 fusion.11
  52.5 0.0 copy-done.3
  52.5 0.9 %multiply_convert_fusion = bf16[1,128,1024]{2,1,0:T(8,128)(2,1)} fusion(bf16[1,128,512]{2,1,0:T(8,128)(2,1)S(1)} %get-tuple-element.7, bf16[1,128,512]{2,1,0:T(8,128)(2,1)S(1)} %copy.30, bf16[1,128,512]{2,1,0:T(8,128)(2,1)S(1)} %get-tuple-element.6, bf16[1,128,512]{2,1,0:T(8,128)(2,1)S(1)} %multiply_convert_fusion.1, f32[1024]{0:T(1024)S(1)} %copy-done.3, ...), kind=kLoop, calls=%fused_computation.19 | loop fusion | flops 3276800 | bytes 791553 | tf_op jit(solution)/shard_map/convert_element_type | solution.py:45
  (5 shorter events, 0.1 us)
Async XLA Ops:
  0.0 16.1 %copy-start = (bf16[1024,2,512]{2,1,0:T(2,128)(2,1)S(1)}, bf16[1024,2,512]{2,1,0:T(2,128)(2,1)}, u32[]{:S(2)}) copy-start(bf16[1024,2,512]{2,1,0:T(2,128)(2,1)} %param.8) | copy-start | bytes 6291460
  6.2 7.8 %copy-start.4 = (bf16[1,128,1024]{2,1,0:T(8,128)(2,1)S(1)}, bf16[1,128,1024]{2,1,0:T(8,128)(2,1)}, u32[]{:S(2)}) copy-start(bf16[1,128,1024]{2,1,0:T(8,128)(2,1)} %param.6) | copy-start | bytes 786436
  8.7 8.6 %copy-start.5 = (s32[4]{0:T(128)S(1)}, s32[4]{0:T(128)}, u32[]{:S(2)}) copy-start(s32[4]{0:T(128)} %param.10) | copy-start | bytes 52
  8.7 11.1 %copy-start.6 = (s32[4]{0:T(128)S(1)}, s32[4]{0:T(128)}, u32[]{:S(2)}) copy-start(s32[4]{0:T(128)} %param.11) | copy-start | bytes 52
  8.7 28.8 %all-to-all-start = ((bf16[8,2,4,64,128]{4,3,2,1,0:T(8,128)(2,1)}), bf16[8,2,4,64,128]{4,3,2,1,0:T(8,128)(2,1)S(1)}, u32[]{:S(2)}, u32[]{:S(2)}) async-start(bf16[8,2,4,64,128]{4,3,2,1,0:T(8,128)(2,1)} %bitcast.49), calls=%async_computation | async-start | bytes 2097152 | tf_op jit(solution)/shard_map/all_to_all | solution.py:64
  14.0 20.2 %collective-permute-start = (bf16[128,1024]{1,0:T(8,128)(2,1)S(1)}, bf16[128,1024]{1,0:T(8,128)(2,1)}, u32[]{:S(2)}, u32[]{:S(2)}) collective-permute-start(bf16[128,1024]{1,0:T(8,128)(2,1)S(1)} %bitcast.55), channel_id=1, source_target_pairs={{0,4},{4,0},{1,5},{5,1},{2,6},{6,2},{3,7},{7,3},{8,12},{12,8},{9,1... | collective-permute-start | bytes 786440 | tf_op jit(solution)/shard_map/ppermute | solution.py:81
  35.6 0.8 %copy-start.2 = (f32[2,128,512]{2,1,0:T(8,128)}, f32[2,128,512]{2,1,0:T(8,128)S(1)}, u32[]{:S(2)}) copy-start(f32[2,128,512]{2,1,0:T(8,128)S(1)} %fusion.7) | copy-start | bytes 1572868
  38.6 4.8 %copy-start.1 = (bf16[1,2,4,8,64,128]{5,4,3,2,1,0:T(8,128)(2,1)S(1)}, bf16[1,2,4,8,64,128]{5,4,3,2,1,0:T(8,128)(2,1)}, u32[]{:S(2)}) copy-start(bf16[1,2,4,8,64,128]{5,4,3,2,1,0:T(8,128)(2,1)} %copy.18) | copy-start | bytes 3145732
  43.0 9.5 %copy-start.3 = (f32[1024]{0:T(1024)S(1)}, f32[1024]{0:T(1024)}, u32[]{:S(2)}) copy-start(f32[1024]{0:T(1024)} %param.9) | copy-start | bytes 12292
  43.0 8.2 %collective-permute-start.1 = (bf16[2,128,512]{2,1,0:T(8,128)(2,1)}, bf16[2,128,512]{2,1,0:T(8,128)(2,1)}, u32[]{:S(2)}, u32[]{:S(2)}) collective-permute-start(bf16[2,128,512]{2,1,0:T(8,128)(2,1)} %pad_maximum_fusion), channel_id=1, source_target_pairs={{0,4},{4,0},{1,5},{5,1},{2,6},{6,2},{3,7},{7,3},{8,12},{12,8},{9,1... | collective-permute-start | bytes 786440 | tf_op jit(solution)/shard_map/ppermute | solution.py:85

commit v5 on v4

--- a/solution.py
+++ b/solution.py
@@ -55,20 +55,22 @@
     local_heads = half // HEAD_SIZE
 
     n_users, n_pos = kv_store.shape[0], kv_store.shape[1]
-    ordered = kv_store.at[users].get(mode="promise_in_bounds", unique_indices=True).reshape(
+    ordered = jnp.take(kv_store, users, axis=0).reshape(
         n_users, n_pos, 2, n_blk, local_heads, HEAD_SIZE
     )
     ordered = jnp.transpose(ordered, (3, 0, 2, 4, 1, 5)).reshape(
         n_blk * n_users, 2, local_heads, n_pos, HEAD_SIZE
     )
+    mine = cands[0]
+    rows = mine.shape[0]
+    if n_blk == 2:
+        swap = [(0, 1), (1, 0)]
+        peer, ordered = lax.optimization_barrier((lax.ppermute(mine, "blk", swap), ordered))
     fetched = lax.all_to_all(
         ordered, ("blk", "store"), split_axis=0, concat_axis=3, tiled=True
     )
     keys = fetched[0, 0]
     values = fetched[0, 1]
-
-    mine = cands[0]
-    rows = mine.shape[0]
 
     def project(feats):
         proj = jnp.einsum("cd,dkh->ckh", feats, proj_weight, preferred_element_type=jnp.float32).transpose(1, 0, 2)
@@ -77,8 +79,6 @@
         return jnp.transpose(query, (1, 0, 2)), gate
 
     if n_blk == 2:
-        swap = [(0, 1), (1, 0)]
-        peer = lax.ppermute(mine, "blk", swap)
         query_own, gate_own = project(mine)
         query_peer, gate_peer = project(peer)
         sent = attend(query_peer, keys, values, count).astype(jnp.bfloat16)

time: 53.9 us -> 46 us (0.85)
  waiting for transfers between devices: 15.7 us -> 7.9 us
  other arithmetic: 5.48 us -> 7.2 us
  local copies, waits for them, and re-layouts: 14.9 us -> 13.5 us
    ppermute x1, waiting for transfers between devices: 9.77 us -> 0.01 us  [per_device(): lax.ppermute(mine, 'blk', swap)]
    reshape x2 -> x0, local copies, waits for them, and re-layouts: 4.01 us -> none  [per_device(): kv_store.at[users].get(mode='promise_in_bounds', unique_indices=True)]
    all_to_all x1, waiting for transfers between devices: 0.01 us -> 3.64 us  [per_device(): lax.all_to_all(ordered, ('blk', 'store'), split_axis=0, concat_axis=3, ti...]
    gather x1 -> x2, local copies, waits for them, and re-layouts: 3.88 us -> 6.52 us  [per_device(): jnp.take(kv_store, users, axis=0)]
    ppermute x1, waiting for transfers between devices: 5.92 us -> 4.26 us  [per_device(): back = lax.ppermute(jnp.stack([sent, gate_peer]), 'blk', swap)]
    all_to_all x1, starting transfers between devices: 5.3 us -> 3.69 us  [per_device(): lax.all_to_all(ordered, ('blk', 'store'), split_axis=0, concat_axis=3, ti...]
    select_n x1 -> x2, other arithmetic: 0.81 us -> 1.88 us  [per_device(): jnp.take(kv_store, users, axis=0)]
    ppermute x1, starting transfers between devices: 2.02 us -> 2.97 us  [per_device(): lax.ppermute(mine, 'blk', swap)]
  transfers between devices with their start and end apart: 3 -> 3, of which waited for: 2 -> 2; matrix products, arithmetic and copies ran while one was open for 19% -> 42% of each run, Pallas kernels for 0% -> 0%
where the time goes in v5:
time: 46 us; the launch traced here: 45.5 us
  local copies, waits for them, and re-layouts  13.5 us (29%)
  waiting for transfers between devices  7.9 us (17%)
  starting transfers between devices  7.2 us (16%)
  other arithmetic  7.2 us (16%)
  matrix products  6.94 us (15%)
  between operations  2.74 us (6%)
    gather x2, local copies, waits for them, and re-layouts, per_device(): jnp.take(kv_store, users, axis=0)  6.52 us
    dot_general x2, matrix products, one_block(): jnp.einsum('hck,hkd->chd', weights, value_block, preferred_element_type=j...  4.31 us
    ppermute x1, waiting for transfers between devices, per_device(): back = lax.ppermute(jnp.stack([sent, gate_peer]), 'blk', swap)  4.26 us
    all_to_all x1, starting transfers between devices, per_device(): lax.all_to_all(ordered, ('blk', 'store'), split_axis=0, concat_axis=3, ti...  3.69 us
    all_to_all x1, waiting for transfers between devices, per_device(): lax.all_to_all(ordered, ('blk', 'store'), split_axis=0, concat_axis=3, ti...  3.64 us
    ppermute x1, starting transfers between devices, per_device(): lax.ppermute(mine, 'blk', swap)  2.97 us
    dot_general x2, matrix products, project(): jnp.einsum('cd,dkh->ckh', feats, proj_weight, preferred_element_type=jnp....  2.64 us
    convert_element_type x2, other arithmetic, project(): gate = jax.nn.silu(proj[1]).astype(jnp.bfloat16)  2.06 us
  transfers between devices with their start and end apart: 3, of which 2 were waited for; matrix products, arithmetic and copies ran while one was open for 42% of the time, Pallas kernels for 0%

profile of v5, /device:TPU:0, one launch (start us, length us, event | category | flops | bytes accessed | tf_op | source)
XLA Modules:
  0.0 45.5 jit_solution(12959355790847841316)
XLA Ops:
  0.0 0.0 copy-start
  0.0 3.0 %collective-permute-start = (bf16[128,1024]{1,0:T(8,128)(2,1)}, bf16[128,1024]{1,0:T(8,128)(2,1)}, u32[]{:S(2)}, u32[]{:S(2)}) collective-permute-start(bf16[128,1024]{1,0:T(8,128)(2,1)} %bitcast.54), channel_id=1, source_target_pairs={{0,4},{4,0},{1,5},{5,1},{2,6},{6,2},{3,7},{7,3},{8,12},{12,8},{9,1... | collective-permute-start | bytes 786440 | tf_op jit(solution)/shard_map/ppermute | solution.py:68
  3.0 0.7 %compare_select_fusion = s32[4]{0:T(128)S(1)} fusion(s32[4]{0:T(128)} %param.10), kind=kLoop, calls=%fused_computation.44 | loop fusion | flops 12 | bytes 32 | tf_op jit(solution)/shard_map/jit(_take)/jit(_where)/select_n | solution.py:58
  3.6 0.7 %compare_and_fusion = pred[4]{0:T(512)(128)(4,1)S(1)} fusion(s32[4]{0:T(128)} %param.10), kind=kLoop, calls=%fused_computation.47 | loop fusion | flops 24 | bytes 20 | tf_op jit(solution)/shard_map/jit(_take)/and | solution.py:58
  4.3 4.8 %gather_fusion = bf16[4,64,2,1024]{3,2,1,0:T(2,128)(2,1)} fusion(bf16[4,64,2,1024]{3,2,1,0:T(2,128)(2,1)} %param.7, s32[1024]{0:T(1024)S(1)} %pad_clamp_fusion), kind=kCustom, calls=%fused_computation | custom fusion | bytes 2097168 | tf_op jit(solution)/shard_map/jit(_take)/gather | solution.py:58
  9.1 1.7 %gather.7 = bf16[4,64,2,2,4,128]{5,4,3,2,1,0:T(4,128)(2,1)S(1)} reshape(bf16[4,64,2,1024]{3,2,1,0:T(2,128)(2,1)} %gather_fusion) | data formatting | bytes 2097152 | tf_op jit(solution)/shard_map/jit(_take)/gather | solution.py:58
  10.8 0.0 copy-start.4
  10.8 1.2 %copy_select_fusion = bf16[4,64,2,2,4,128]{5,1,4,2,0,3:T(8,128)(2,1)} fusion(bf16[4,64,2,2,4,128]{5,4,3,2,1,0:T(4,128)(2,1)S(1)} %gather.7, pred[4]{0:T(512)(128)(4,1)S(1)} %compare_and_fusion), kind=kLoop, calls=%fused_computation.11 | loop fusion | flops 524288 | bytes 2097156 | tf_op jit(solution)/shard_map/jit(_take)/select_n | solution.py:58
  12.1 0.0 collective-permute-done
  12.1 0.0 copy-start.5
  12.1 0.0 copy-start.6
  12.1 3.7 %all-to-all-start = ((bf16[8,2,4,64,128]{4,3,2,1,0:T(8,128)(2,1)}), bf16[8,2,4,64,128]{4,3,2,1,0:T(8,128)(2,1)S(1)}, u32[]{:S(2)}, u32[]{:S(2)}) async-start(bf16[8,2,4,64,128]{4,3,2,1,0:T(8,128)(2,1)} %bitcast.2), calls=%async_computation | async-start | bytes 2097152 | tf_op jit(solution)/shard_map/all_to_all | solution.py:69
  15.8 0.0 copy-done
  15.8 0.0 copy-done.4
  15.8 1.2 %fusion.4 = f32[2,128,512]{2,1,0:T(8,128)} fusion(bf16[1024,2,512]{2,1,0:T(2,128)(2,1)S(1)} %copy-done, bf16[1,128,1024]{2,1,0:T(8,128)(2,1)S(1)} %copy-done.4), kind=kOutput, calls=%fused_computation.7 | convolution fusion | flops 268435456 | bytes 2883584 | tf_op jit(solution)/shard_map/cd,dkh->ckh/dot_general | solution.py:76
  17.0 0.0 copy-done.5
  17.0 0.6 %dynamic_slice.7 = s32[1]{0:T(128)} dynamic-slice(s32[4]{0:T(128)S(1)} %copy-done.5, s32[]{:T(128)S(6)} %select_n.50), dynamic_slice_sizes={1} | dynamic-slice | bytes 12 | tf_op jit(solution)/shard_map/jit(dynamic_index_in_dim)/dynamic_slice | solution.py:52
  19.6 0.0 copy-done.6
  19.6 0.6 %dynamic_slice.8 = s32[1]{0:T(128)} dynamic-slice(s32[4]{0:T(128)S(1)} %copy-done.6, s32[]{:T(128)S(6)} %select_n.51), dynamic_slice_sizes={1} | dynamic-slice | bytes 12 | tf_op jit(solution)/shard_map/jit(dynamic_index_in_dim)/dynamic_slice | solution.py:53
  20.8 1.0 %slice.60 = bf16[1,128,512]{2,1,0:T(8,128)(2,1)S(1)} slice(f32[2,128,512]{2,1,0:T(8,128)} %fusion.4), slice={[0:1], [0:128], [0:512]} | slice | bytes 262144 | tf_op jit(solution)/shard_map/slice | solution.py:77
  21.8 0.7 %convert_element_type.102 = bf16[128,4,128]{2,1,0:T(4,128)(2,1)} reshape(bf16[1,128,512]{2,1,0:T(8,128)(2,1)S(1)} %slice.60) | data formatting | bytes 262144 | tf_op jit(solution)/shard_map/convert_element_type | solution.py:77
  22.5 0.6 %fusion.30 = f32[512]{0:T(512)S(1)} fusion(s32[]{:T(128)} %bitcast.12), kind=kLoop, calls=%fused_computation.46 | loop fusion | flops 1024 | bytes 2052 | tf_op jit(solution)/shard_map/convert_element_type | solution.py:26
  23.1 1.0 %multiply_convert_fusion.1 = bf16[1,128,512]{2,1,0:T(8,128)(2,1)S(1)} fusion(f32[2,128,512]{2,1,0:T(8,128)} %fusion.4), kind=kLoop, calls=%fused_computation.37 | loop fusion | flops 327680 | bytes 393216 | tf_op jit(solution)/shard_map/convert_element_type | solution.py:78
  24.2 1.4 %fusion.7 = f32[2,128,512]{2,1,0:T(8,128)S(1)} fusion(bf16[1024,2,512]{2,1,0:T(2,128)(2,1)S(1)} %copy-done, bf16[128,1024]{1,0:T(8,128)(2,1)} %collective-permute-done), kind=kOutput, calls=%fused_computation.8 | convolution fusion | flops 268435456 | bytes 2883584 | tf_op jit(solution)/shard_map/cd,dkh->ckh/dot_general | solution.py:76
  25.6 0.0 copy-start.2
  25.6 0.8 %copy-done.2 = f32[2,128,512]{2,1,0:T(8,128)} copy-done((f32[2,128,512]{2,1,0:T(8,128)}, f32[2,128,512]{2,1,0:T(8,128)S(1)}, u32[]{:S(2)}) %copy-start.2) | copy-done | bytes 524312
  26.4 1.0 %multiply_convert_fusion.2 = bf16[1,128,512]{2,1,0:T(8,128)(2,1)S(1)} fusion(f32[2,128,512]{2,1,0:T(8,128)} %copy-done.2), kind=kLoop, calls=%fused_computation.38 | loop fusion | flops 327680 | bytes 393216 | tf_op jit(solution)/shard_map/convert_element_type | solution.py:78
  27.5 3.6 %all-to-all-done = bf16[8,2,4,64,128]{4,3,2,1,0:T(8,128)(2,1)S(1)} async-done(((bf16[8,2,4,64,128]{4,3,2,1,0:T(8,128)(2,1)}), bf16[8,2,4,64,128]{4,3,2,1,0:T(8,128)(2,1)S(1)}, u32[]{:S(2)}, u32[]{:S(2)}) %all-to-all-start) | async-done | bytes 1048608 | tf_op jit(solution)/shard_map/all_to_all | solution.py:69
  31.1 1.1 %copy.18 = bf16[1,2,4,8,64,128]{5,4,3,2,1,0:T(8,128)(2,1)} copy(bf16[1,2,4,8,64,128]{5,4,2,1,3,0:T(8,128)(2,1)S(1)} %bitcast.48) | data formatting | bytes 2097152 | tf_op jit(solution)/shard_map/all_to_all | solution.py:69
  32.2 0.0 copy-start.1
  32.2 2.7 %convolution_convert_fusion = bf16[4,128,128]{2,1,0:T(8,128)(2,1)} fusion(f32[]{:T(128)S(6)} %convert_element_type.104, f32[512]{0:T(512)S(1)} %fusion.30, bf16[1,2,4,512,128]{4,3,2,1,0:T(8,128)(2,1)} %bitcast.49, bf16[128,4,128]{2,1,0:T(4,128)(2,1)S(1)} %convert_element_type.108), kind=kOutput, calls=%fused_computation.9 | convolution fusion | flops 136380416 | bytes 1312772 | tf_op jit(solution)/shard_map/hck,hkd->chd/dot_general | solution.py:28
  34.8 1.0 %copy.31 = bf16[1,128,512]{2,1,0:T(8,128)(2,1)S(1)} copy(bf16[1,128,512]{1,2,0:T(8,128)(2,1)} %bitcast.53) | data formatting | bytes 262144 | tf_op jit(solution)/shard_map/convert_element_type | solution.py:84
  35.9 0.7 %pad_maximum_fusion = bf16[2,128,512]{2,1,0:T(8,128)(2,1)} fusion(bf16[1,128,512]{2,1,0:T(8,128)(2,1)S(1)} %multiply_convert_fusion.2, bf16[1,128,512]{2,1,0:T(8,128)(2,1)S(1)} %copy.31), kind=kLoop, calls=%fused_computation.31 | loop fusion | flops 131072 | bytes 524288 | tf_op jit(solution)/shard_map/stack | solution.py:85
  36.6 0.0 copy-start.3
  36.6 0.5 %collective-permute-start.1 = (bf16[2,128,512]{2,1,0:T(8,128)(2,1)}, bf16[2,128,512]{2,1,0:T(8,128)(2,1)}, u32[]{:S(2)}, u32[]{:S(2)}) collective-permute-start(bf16[2,128,512]{2,1,0:T(8,128)(2,1)} %pad_maximum_fusion), channel_id=1, source_target_pairs={{0,4},{4,0},{1,5},{5,1},{2,6},{6,2},{3,7},{7,3},{8,12},{12,8},{9,1... | collective-permute-start | bytes 786440 | tf_op jit(solution)/shard_map/ppermute | solution.py:85
  37.1 0.0 copy-done.1
  37.1 1.6 %convolution_convert_fusion.1 = bf16[4,128,128]{2,1,0:T(8,128)(2,1)S(1)} fusion(f32[]{:T(128)S(6)} %convert_element_type.104, f32[512]{0:T(512)S(1)} %fusion.30, bf16[1,2,4,512,128]{4,3,2,1,0:T(8,128)(2,1)S(1)} %bitcast.50, bf16[128,4,128]{2,1,0:T(4,128)(2,1)} %convert_element_type.102), kind=kOutput, calls=%fused_computation.10 | convolution fusion | flops 136380416 | bytes 1312772 | tf_op jit(solution)/shard_map/hck,hkd->chd/dot_general | solution.py:28
  38.8 0.1 copy.32
  38.9 0.1 copy.30
  39.0 4.3 %collective-permute-done.1 = bf16[2,128,512]{2,1,0:T(8,128)(2,1)} collective-permute-done((bf16[2,128,512]{2,1,0:T(8,128)(2,1)}, bf16[2,128,512]{2,1,0:T(8,128)(2,1)}, u32[]{:S(2)}, u32[]{:S(2)}) %collective-permute-start.1) | collective-permute-done | bytes 262176 | tf_op jit(solution)/shard_map/ppermute | solution.py:85
  43.3 1.0 %slice_bitcast_fusion.8 = (bf16[128,512]{1,0:T(8,128)(2,1)S(1)}, bf16[1,128,512]{2,1,0:T(8,128)(2,1)S(1)}, bf16[1,128,512]{2,1,0:T(8,128)(2,1)S(1)}) fusion(bf16[2,128,512]{2,1,0:T(8,128)(2,1)} %collective-permute-done.1), kind=kLoop, calls=%fused_computation.54 | loop fusion | bytes 655360 | tf_op jit(solution)/shard_map/squeeze | solution.py:88
  44.3 0.1 convert_reduce_fusion
  44.4 0.2 fusion.11
  44.6 0.0 copy-done.3
  44.6 0.9 %multiply_convert_fusion = bf16[1,128,1024]{2,1,0:T(8,128)(2,1)} fusion(bf16[1,128,512]{2,1,0:T(8,128)(2,1)S(1)} %get-tuple-element.11, bf16[1,128,512]{2,1,0:T(8,128)(2,1)S(1)} %copy.30, bf16[1,128,512]{2,1,0:T(8,128)(2,1)S(1)} %get-tuple-element.10, bf16[1,128,512]{2,1,0:T(8,128)(2,1)S(1)} %multiply_convert_fusion.1, f32[1024]{0:T(1024)S(1)} %copy-done.3, ...), kind=kLoop, calls=%fused_computation.20 | loop fusion | flops 3276800 | bytes 791553 | tf_op jit(solution)/shard_map/convert_element_type | solution.py:45
  (5 shorter events, 0.1 us)
Async XLA Ops:
  0.0 15.8 %copy-start = (bf16[1024,2,512]{2,1,0:T(2,128)(2,1)S(1)}, bf16[1024,2,512]{2,1,0:T(2,128)(2,1)}, u32[]{:S(2)}) copy-start(bf16[1024,2,512]{2,1,0:T(2,128)(2,1)} %param.8) | copy-start | bytes 6291460
  0.0 12.1 %collective-permute-start = (bf16[128,1024]{1,0:T(8,128)(2,1)}, bf16[128,1024]{1,0:T(8,128)(2,1)}, u32[]{:S(2)}, u32[]{:S(2)}) collective-permute-start(bf16[128,1024]{1,0:T(8,128)(2,1)} %bitcast.54), channel_id=1, source_target_pairs={{0,4},{4,0},{1,5},{5,1},{2,6},{6,2},{3,7},{7,3},{8,12},{12,8},{9,1... | collective-permute-start | bytes 786440 | tf_op jit(solution)/shard_map/ppermute | solution.py:68
  10.8 4.9 %copy-start.4 = (bf16[1,128,1024]{2,1,0:T(8,128)(2,1)S(1)}, bf16[1,128,1024]{2,1,0:T(8,128)(2,1)}, u32[]{:S(2)}) copy-start(bf16[1,128,1024]{2,1,0:T(8,128)(2,1)} %param.6) | copy-start | bytes 786436
  12.1 5.0 %copy-start.5 = (s32[4]{0:T(128)S(1)}, s32[4]{0:T(128)}, u32[]{:S(2)}) copy-start(s32[4]{0:T(128)} %param.10) | copy-start | bytes 52
  12.1 7.5 %copy-start.6 = (s32[4]{0:T(128)S(1)}, s32[4]{0:T(128)}, u32[]{:S(2)}) copy-start(s32[4]{0:T(128)} %param.11) | copy-start | bytes 52
  12.1 19.0 %all-to-all-start = ((bf16[8,2,4,64,128]{4,3,2,1,0:T(8,128)(2,1)}), bf16[8,2,4,64,128]{4,3,2,1,0:T(8,128)(2,1)S(1)}, u32[]{:S(2)}, u32[]{:S(2)}) async-start(bf16[8,2,4,64,128]{4,3,2,1,0:T(8,128)(2,1)} %bitcast.2), calls=%async_computation | async-start | bytes 2097152 | tf_op jit(solution)/shard_map/all_to_all | solution.py:69
  25.6 0.8 %copy-start.2 = (f32[2,128,512]{2,1,0:T(8,128)}, f32[2,128,512]{2,1,0:T(8,128)S(1)}, u32[]{:S(2)}) copy-start(f32[2,128,512]{2,1,0:T(8,128)S(1)} %fusion.7) | copy-start | bytes 1572868
  32.2 5.0 %copy-start.1 = (bf16[1,2,4,8,64,128]{5,4,3,2,1,0:T(8,128)(2,1)S(1)}, bf16[1,2,4,8,64,128]{5,4,3,2,1,0:T(8,128)(2,1)}, u32[]{:S(2)}) copy-start(bf16[1,2,4,8,64,128]{5,4,3,2,1,0:T(8,128)(2,1)} %copy.18) | copy-start | bytes 3145732
  36.6 8.0 %copy-start.3 = (f32[1024]{0:T(1024)S(1)}, f32[1024]{0:T(1024)}, u32[]{:S(2)}) copy-start(f32[1024]{0:T(1024)} %param.9) | copy-start | bytes 12292
  36.6 6.7 %collective-permute-start.1 = (bf16[2,128,512]{2,1,0:T(8,128)(2,1)}, bf16[2,128,512]{2,1,0:T(8,128)(2,1)}, u32[]{:S(2)}, u32[]{:S(2)}) collective-permute-start(bf16[2,128,512]{2,1,0:T(8,128)(2,1)} %pad_maximum_fusion), channel_id=1, source_target_pairs={{0,4},{4,0},{1,5},{5,1},{2,6},{6,2},{3,7},{7,3},{8,12},{12,8},{9,1... | collective-permute-start | bytes 786440 | tf_op jit(solution)/shard_map/ppermute | solution.py:85

commit v6 on v5

--- a/solution.py
+++ b/solution.py
@@ -2,6 +2,8 @@
 import jax.numpy as jnp
 from jax import lax
 from jax.sharding import PartitionSpec as P
+from jax.experimental import pallas as pl
+from jax.experimental.pallas import tpu as pltpu
 
 D = 1024
 HEADS = 8
@@ -45,6 +47,32 @@
     return (normed * gate.astype(jnp.float32)).astype(jnp.bfloat16)
 
 
+def take_users(kv_store, users):
+    n_users = users.shape[0]
+
+    def kernel(users_ref, kv_hbm, out_hbm, sems):
+        copies = [
+            pltpu.make_async_copy(kv_hbm.at[users_ref[s]], out_hbm.at[s], sems.at[s])
+            for s in range(n_users)
+        ]
+        for copy in copies:
+            copy.start()
+        for copy in copies:
+            copy.wait()
+
+    return pl.pallas_call(
+        kernel,
+        out_shape=jax.ShapeDtypeStruct((n_users,) + kv_store.shape[1:], kv_store.dtype),
+        grid_spec=pltpu.PrefetchScalarGridSpec(
+            num_scalar_prefetch=1,
+            grid=(1,),
+            in_specs=[pl.BlockSpec(memory_space=pl.ANY)],
+            out_specs=pl.BlockSpec(memory_space=pl.ANY),
+            scratch_shapes=[pltpu.SemaphoreType.DMA((n_users,))],
+        ),
+    )(users, kv_store)
+
+
 def per_device(cands, kv_store, proj_weight, norm_gain, users, lengths):
     n_blk = lax.axis_size("blk")
     blk = lax.axis_index("blk")
@@ -55,7 +83,7 @@
     local_heads = half // HEAD_SIZE
 
     n_users, n_pos = kv_store.shape[0], kv_store.shape[1]
-    ordered = jnp.take(kv_store, users, axis=0).reshape(
+    ordered = take_users(kv_store, users).reshape(
         n_users, n_pos, 2, n_blk, local_heads, HEAD_SIZE
     )
     ordered = jnp.transpose(ordered, (3, 0, 2, 4, 1, 5)).reshape(

time: 46 us -> 73.5 us (1.60)
  Pallas kernels: 0 us -> 33.6 us
  local copies, waits for them, and re-layouts: 13.5 us -> 10 us
  other arithmetic: 7.2 us -> 4.66 us
    pallas_call x0 -> x1, Pallas kernels: none -> 33.6 us  [take_users(): pl.pallas_call(kernel, out_shape=jax.ShapeDtypeStruct((n_users,) + kv_sto...]
    gather x2 -> x0, local copies, waits for them, and re-layouts: 6.52 us -> none  [per_device(): jnp.take(kv_store, users, axis=0)]
    reshape x0 -> x2, local copies, waits for them, and re-layouts: none -> 3 us  [per_device(): take_users(kv_store, users)]
    select_n x2 -> x0, other arithmetic: 1.88 us -> none  [per_device(): jnp.take(kv_store, users, axis=0)]
  transfers between devices with their start and end apart: 3 -> 3, of which waited for: 2 -> 2; matrix products, arithmetic and copies ran while one was open for 42% -> 18% of each run, Pallas kernels for 0% -> 46%
where the time goes in v6:
time: 73.5 us; the launch traced here: 73 us
  Pallas kernels  33.6 us (46%)
  local copies, waits for them, and re-layouts  10 us (14%)
  waiting for transfers between devices  7.9 us (11%)
  starting transfers between devices  7.2 us (10%)
  matrix products  6.95 us (9%)
  other arithmetic  4.66 us (6%)
  between operations  2.75 us (4%)
    pallas_call x1, Pallas kernels, take_users(): pl.pallas_call(kernel, out_shape=jax.ShapeDtypeStruct((n_users,) + kv_sto...  33.6 us
    dot_general x2, matrix products, one_block(): jnp.einsum('hck,hkd->chd', weights, value_block, preferred_element_type=j...  4.31 us
    ppermute x1, waiting for transfers between devices, per_device(): back = lax.ppermute(jnp.stack([sent, gate_peer]), 'blk', swap)  4.26 us
    all_to_all x1, starting transfers between devices, per_device(): lax.all_to_all(ordered, ('blk', 'store'), split_axis=0, concat_axis=3, ti...  3.69 us
    all_to_all x1, waiting for transfers between devices, per_device(): lax.all_to_all(ordered, ('blk', 'store'), split_axis=0, concat_axis=3, ti...  3.63 us
    reshape x2, local copies, waits for them, and re-layouts, per_device(): take_users(kv_store, users)  3 us
    ppermute x1, starting transfers between devices, per_device(): lax.ppermute(mine, 'blk', swap)  2.97 us
    dot_general x2, matrix products, project(): jnp.einsum('cd,dkh->ckh', feats, proj_weight, preferred_element_type=jnp....  2.64 us
  transfers between devices with their start and end apart: 3, of which 2 were waited for; matrix products, arithmetic and copies ran while one was open for 18% of the time, Pallas kernels for 46%

profile of v6, /device:TPU:0, one launch (start us, length us, event | category | flops | bytes accessed | tf_op | source)
XLA Modules:
  0.0 73.0 jit_solution(13688123265656633325)
XLA Ops:
  0.0 0.0 copy-start
  0.0 3.0 %collective-permute-start = (bf16[128,1024]{1,0:T(8,128)(2,1)}, bf16[128,1024]{1,0:T(8,128)(2,1)}, u32[]{:S(2)}, u32[]{:S(2)}) collective-permute-start(bf16[128,1024]{1,0:T(8,128)(2,1)} %bitcast.55), channel_id=1, source_target_pairs={{0,4},{4,0},{1,5},{5,1},{2,6},{6,2},{3,7},{7,3},{8,12},{12,8},{9,1... | collective-permute-start | bytes 786440 | tf_op jit(solution)/shard_map/ppermute | solution.py:96
  3.0 33.6 %shard_map.64 = bf16[4,64,2,1024]{3,2,1,0:T(2,128)(2,1)} custom-call(s32[4]{0:T(128)} %users_ref.1, bf16[4,64,2,1024]{3,2,1,0:T(2,128)(2,1)} %kv_hbm.1), custom_call_target="tpu_custom_call" | custom-call | tf_op jit(solution)/shard_map/pallas_call | solution.py:63
  36.5 1.7 %reshape.218 = bf16[4,64,2,2,4,128]{5,4,3,2,1,0:T(4,128)(2,1)S(1)} reshape(bf16[4,64,2,1024]{3,2,1,0:T(2,128)(2,1)} %shard_map.64) | data formatting | bytes 2097152 | tf_op jit(solution)/shard_map/reshape | solution.py:86
  38.3 0.0 copy-start.5
  38.3 1.3 %copy.16 = bf16[4,64,2,2,4,128]{5,1,4,2,0,3:T(8,128)(2,1)} copy(bf16[4,64,2,2,4,128]{5,4,3,2,1,0:T(4,128)(2,1)S(1)} %reshape.218) | data formatting | bytes 2097152 | tf_op jit(solution)/shard_map/reshape | solution.py:86
  39.6 0.0 collective-permute-done
  39.6 0.0 copy-start.4
  39.6 0.0 copy-start.6
  39.6 3.7 %all-to-all-start = ((bf16[8,2,4,64,128]{4,3,2,1,0:T(8,128)(2,1)}), bf16[8,2,4,64,128]{4,3,2,1,0:T(8,128)(2,1)S(1)}, u32[]{:S(2)}, u32[]{:S(2)}) async-start(bf16[8,2,4,64,128]{4,3,2,1,0:T(8,128)(2,1)} %bitcast.49), calls=%async_computation | async-start | bytes 2097152 | tf_op jit(solution)/shard_map/all_to_all | solution.py:97
  43.3 0.0 copy-done
  43.3 0.0 copy-done.5
  43.3 1.3 %fusion.4 = f32[2,128,512]{2,1,0:T(8,128)} fusion(bf16[1024,2,512]{2,1,0:T(2,128)(2,1)S(1)} %copy-done, bf16[1,128,1024]{2,1,0:T(8,128)(2,1)S(1)} %copy-done.5), kind=kOutput, calls=%fused_computation.6 | convolution fusion | flops 268435456 | bytes 2883584 | tf_op jit(solution)/shard_map/cd,dkh->ckh/dot_general | solution.py:104
  44.5 0.0 copy-done.4
  44.5 0.6 dynamic_slice.7
  47.1 0.0 copy-done.6
  47.1 0.6 dynamic_slice.8
  48.3 1.0 %slice.58 = bf16[1,128,512]{2,1,0:T(8,128)(2,1)S(1)} slice(f32[2,128,512]{2,1,0:T(8,128)} %fusion.4), slice={[0:1], [0:128], [0:512]} | slice | bytes 262144 | tf_op jit(solution)/shard_map/slice | solution.py:105
  49.3 0.7 convert_element_type.102
  50.0 0.6 fusion.30
  50.6 1.0 %multiply_convert_fusion.1 = bf16[1,128,512]{2,1,0:T(8,128)(2,1)S(1)} fusion(f32[2,128,512]{2,1,0:T(8,128)} %fusion.4), kind=kLoop, calls=%fused_computation.35 | loop fusion | flops 327680 | bytes 393216 | tf_op jit(solution)/shard_map/convert_element_type | solution.py:106
  51.7 1.4 %fusion.7 = f32[2,128,512]{2,1,0:T(8,128)S(1)} fusion(bf16[1024,2,512]{2,1,0:T(2,128)(2,1)S(1)} %copy-done, bf16[128,1024]{1,0:T(8,128)(2,1)} %collective-permute-done), kind=kOutput, calls=%fused_computation.7 | convolution fusion | flops 268435456 | bytes 2883584 | tf_op jit(solution)/shard_map/cd,dkh->ckh/dot_general | solution.py:104
  53.1 0.0 copy-start.2
  53.1 0.8 %copy-done.2 = f32[2,128,512]{2,1,0:T(8,128)} copy-done((f32[2,128,512]{2,1,0:T(8,128)}, f32[2,128,512]{2,1,0:T(8,128)S(1)}, u32[]{:S(2)}) %copy-start.2) | copy-done | bytes 524312
  53.9 1.0 %multiply_convert_fusion.2 = bf16[1,128,512]{2,1,0:T(8,128)(2,1)S(1)} fusion(f32[2,128,512]{2,1,0:T(8,128)} %copy-done.2), kind=kLoop, calls=%fused_computation.36 | loop fusion | flops 327680 | bytes 393216 | tf_op jit(solution)/shard_map/convert_element_type | solution.py:106
  55.0 3.6 %all-to-all-done = bf16[8,2,4,64,128]{4,3,2,1,0:T(8,128)(2,1)S(1)} async-done(((bf16[8,2,4,64,128]{4,3,2,1,0:T(8,128)(2,1)}), bf16[8,2,4,64,128]{4,3,2,1,0:T(8,128)(2,1)S(1)}, u32[]{:S(2)}, u32[]{:S(2)}) %all-to-all-start) | async-done | bytes 1048608 | tf_op jit(solution)/shard_map/all_to_all | solution.py:97
  58.6 1.1 %copy.17 = bf16[1,2,4,8,64,128]{5,4,3,2,1,0:T(8,128)(2,1)} copy(bf16[1,2,4,8,64,128]{5,4,2,1,3,0:T(8,128)(2,1)S(1)} %bitcast.48) | data formatting | bytes 2097152 | tf_op jit(solution)/shard_map/all_to_all | solution.py:97
  59.7 0.0 copy-start.1
  59.7 2.7 %convolution_convert_fusion = bf16[4,128,128]{2,1,0:T(8,128)(2,1)} fusion(f32[]{:T(128)S(6)} %convert_element_type.104, f32[512]{0:T(512)S(1)} %fusion.30, bf16[1,2,4,512,128]{4,3,2,1,0:T(8,128)(2,1)} %bitcast.50, bf16[128,4,128]{2,1,0:T(4,128)(2,1)S(1)} %convert_element_type.108), kind=kOutput, calls=%fused_computation.8 | convolution fusion | flops 136380416 | bytes 1312772 | tf_op jit(solution)/shard_map/hck,hkd->chd/dot_general | solution.py:30
  62.3 1.0 %copy.30 = bf16[1,128,512]{2,1,0:T(8,128)(2,1)S(1)} copy(bf16[1,128,512]{1,2,0:T(8,128)(2,1)} %bitcast.54) | data formatting | bytes 262144 | tf_op jit(solution)/shard_map/convert_element_type | solution.py:112
  63.4 0.7 pad_maximum_fusion
  64.1 0.0 copy-start.3
  64.1 0.5 collective-permute-start.1
  64.6 0.0 copy-done.1
  64.6 1.6 %convolution_convert_fusion.1 = bf16[4,128,128]{2,1,0:T(8,128)(2,1)S(1)} fusion(f32[]{:T(128)S(6)} %convert_element_type.104, f32[512]{0:T(512)S(1)} %fusion.30, bf16[1,2,4,512,128]{4,3,2,1,0:T(8,128)(2,1)S(1)} %bitcast.51, bf16[128,4,128]{2,1,0:T(4,128)(2,1)} %convert_element_type.102), kind=kOutput, calls=%fused_computation.9 | convolution fusion | flops 136380416 | bytes 1312772 | tf_op jit(solution)/shard_map/hck,hkd->chd/dot_general | solution.py:30
  66.3 0.1 copy.31
  66.4 0.1 copy.29
  66.5 4.3 %collective-permute-done.1 = bf16[2,128,512]{2,1,0:T(8,128)(2,1)} collective-permute-done((bf16[2,128,512]{2,1,0:T(8,128)(2,1)}, bf16[2,128,512]{2,1,0:T(8,128)(2,1)}, u32[]{:S(2)}, u32[]{:S(2)}) %collective-permute-start.1) | collective-permute-done | bytes 262176 | tf_op jit(solution)/shard_map/ppermute | solution.py:113
  70.8 1.0 %slice_bitcast_fusion.8 = (bf16[128,512]{1,0:T(8,128)(2,1)S(1)}, bf16[1,128,512]{2,1,0:T(8,128)(2,1)S(1)}, bf16[1,128,512]{2,1,0:T(8,128)(2,1)S(1)}) fusion(bf16[2,128,512]{2,1,0:T(8,128)(2,1)} %collective-permute-done.1), kind=kLoop, calls=%fused_computation.49 | loop fusion | bytes 655360 | tf_op jit(solution)/shard_map/squeeze | solution.py:116
  71.8 0.1 convert_reduce_fusion
  71.9 0.2 fusion.11
  72.1 0.0 copy-done.3
  72.1 0.9 %multiply_convert_fusion = bf16[1,128,1024]{2,1,0:T(8,128)(2,1)} fusion(bf16[1,128,512]{2,1,0:T(8,128)(2,1)S(1)} %get-tuple-element.11, bf16[1,128,512]{2,1,0:T(8,128)(2,1)S(1)} %copy.29, bf16[1,128,512]{2,1,0:T(8,128)(2,1)S(1)} %get-tuple-element.10, bf16[1,128,512]{2,1,0:T(8,128)(2,1)S(1)} %multiply_convert_fusion.1, f32[1024]{0:T(1024)S(1)} %copy-done.3, ...), kind=kLoop, calls=%fused_computation.18 | loop fusion | flops 3276800 | bytes 791553 | tf_op jit(solution)/shard_map/convert_element_type | solution.py:47
  (4 shorter events, 0.1 us)
Async XLA Ops:
  0.0 43.3 %copy-start = (bf16[1024,2,512]{2,1,0:T(2,128)(2,1)S(1)}, bf16[1024,2,512]{2,1,0:T(2,128)(2,1)}, u32[]{:S(2)}) copy-start(bf16[1024,2,512]{2,1,0:T(2,128)(2,1)} %param.8) | copy-start | bytes 6291460
  0.0 39.6 %collective-permute-start = (bf16[128,1024]{1,0:T(8,128)(2,1)}, bf16[128,1024]{1,0:T(8,128)(2,1)}, u32[]{:S(2)}, u32[]{:S(2)}) collective-permute-start(bf16[128,1024]{1,0:T(8,128)(2,1)} %bitcast.55), channel_id=1, source_target_pairs={{0,4},{4,0},{1,5},{5,1},{2,6},{6,2},{3,7},{7,3},{8,12},{12,8},{9,1... | collective-permute-start | bytes 786440 | tf_op jit(solution)/shard_map/ppermute | solution.py:96
  38.3 5.0 %copy-start.5 = (bf16[1,128,1024]{2,1,0:T(8,128)(2,1)S(1)}, bf16[1,128,1024]{2,1,0:T(8,128)(2,1)}, u32[]{:S(2)}) copy-start(bf16[1,128,1024]{2,1,0:T(8,128)(2,1)} %param.6) | copy-start | bytes 786436
  39.6 5.0 %copy-start.4 = (s32[4]{0:T(128)S(1)}, s32[4]{0:T(128)}, u32[]{:S(2)}) copy-start(s32[4]{0:T(128)} %users_ref.1) | copy-start | bytes 52
  39.6 7.5 %copy-start.6 = (s32[4]{0:T(128)S(1)}, s32[4]{0:T(128)}, u32[]{:S(2)}) copy-start(s32[4]{0:T(128)} %param.11) | copy-start | bytes 52
  39.6 19.0 %all-to-all-start = ((bf16[8,2,4,64,128]{4,3,2,1,0:T(8,128)(2,1)}), bf16[8,2,4,64,128]{4,3,2,1,0:T(8,128)(2,1)S(1)}, u32[]{:S(2)}, u32[]{:S(2)}) async-start(bf16[8,2,4,64,128]{4,3,2,1,0:T(8,128)(2,1)} %bitcast.49), calls=%async_computation | async-start | bytes 2097152 | tf_op jit(solution)/shard_map/all_to_all | solution.py:97
  53.1 0.8 %copy-start.2 = (f32[2,128,512]{2,1,0:T(8,128)}, f32[2,128,512]{2,1,0:T(8,128)S(1)}, u32[]{:S(2)}) copy-start(f32[2,128,512]{2,1,0:T(8,128)S(1)} %fusion.7) | copy-start | bytes 1572868
  59.7 5.0 %copy-start.1 = (bf16[1,2,4,8,64,128]{5,4,3,2,1,0:T(8,128)(2,1)S(1)}, bf16[1,2,4,8,64,128]{5,4,3,2,1,0:T(8,128)(2,1)}, u32[]{:S(2)}) copy-start(bf16[1,2,4,8,64,128]{5,4,3,2,1,0:T(8,128)(2,1)} %copy.17) | copy-start | bytes 3145732
  64.1 8.0 %copy-start.3 = (f32[1024]{0:T(1024)S(1)}, f32[1024]{0:T(1024)}, u32[]{:S(2)}) copy-start(f32[1024]{0:T(1024)} %param.9) | copy-start | bytes 12292
  64.1 6.7 %collective-permute-start.1 = (bf16[2,128,512]{2,1,0:T(8,128)(2,1)}, bf16[2,128,512]{2,1,0:T(8,128)(2,1)}, u32[]{:S(2)}, u32[]{:S(2)}) collective-permute-start(bf16[2,128,512]{2,1,0:T(8,128)(2,1)} %pad_maximum_fusion), channel_id=1, source_target_pairs={{0,4},{4,0},{1,5},{5,1},{2,6},{6,2},{3,7},{7,3},{8,12},{12,8},{9,1... | collective-permute-start | bytes 786440 | tf_op jit(solution)/shard_map/ppermute | solution.py:113

commit v7 on v3

--- a/solution.py
+++ b/solution.py
@@ -81,14 +81,15 @@
         peer = lax.ppermute(mine, "blk", swap)
         query_own, gate_own = project(mine)
         query_peer, gate_peer = project(peer)
+        gate_back = lax.ppermute(gate_peer, "blk", swap)
         sent = attend(query_peer, keys, values, count).astype(jnp.bfloat16)
-        back = lax.ppermute(jnp.stack([sent, gate_peer]), "blk", swap)
+        back = lax.ppermute(sent, "blk", swap)
         kept = attend(query_own, keys, values, count).astype(jnp.bfloat16)
         first = blk == 0
-        attended = jnp.where(first, jnp.concatenate([kept, back[0]], axis=1),
-                             jnp.concatenate([back[0], kept], axis=1))
-        gate_full = jnp.where(first, jnp.concatenate([gate_own, back[1]], axis=1),
-                              jnp.concatenate([back[1], gate_own], axis=1))
+        attended = jnp.where(first, jnp.concatenate([kept, back], axis=1),
+                             jnp.concatenate([back, kept], axis=1))
+        gate_full = jnp.where(first, jnp.concatenate([gate_own, gate_back], axis=1),
+                              jnp.concatenate([gate_back, gate_own], axis=1))
         return finish(attended, gate_full, norm_gain)[None]
 
     feats = lax.all_gather(mine, "blk", axis=0, tiled=True)

time: 42.5 us -> 41 us (0.965)
  waiting for transfers between devices: 5.95 us -> 4.4 us
    ppermute x1 -> x2, waiting for transfers between devices: 5.94 us -> 4.4 us  [the longest x1 4.39 us: per_device(): back = lax.ppermute(sent, 'blk', swap)]
    ppermute x1 -> x2, starting transfers between devices: 1.96 us -> 2.17 us  [the longest x1 1.96 us: per_device(): gate_back = lax.ppermute(gate_peer, 'blk', swap)]
  transfers between devices with their start and end apart: 3 -> 4, of which waited for: 1 -> 1; matrix products, arithmetic and copies ran while one was open for 47% -> 54% of each run, Pallas kernels for 0% -> 0%
where the time goes in v7:
time: 41 us; the launch traced here: 40.6 us
  local copies, waits for them, and re-layouts  13.5 us (33%)
  starting transfers between devices  9.37 us (23%)
  other arithmetic  5.87 us (14%)
  matrix products  4.61 us (11%)
  waiting for transfers between devices  4.4 us (11%)
  between operations  2.78 us (7%)
    unnamed x13, local copies, waits for them, and re-layouts  5.59 us
    ppermute x1, waiting for transfers between devices, per_device(): back = lax.ppermute(sent, 'blk', swap)  4.39 us
    all_to_all x1, starting transfers between devices, per_device(): lax.all_to_all(ordered, ('blk', 'store'), split_axis=0, concat_axis=3, ti...  4.24 us
    gather x2, local copies, waits for them, and re-layouts, per_device(): jnp.take(kv_store, users, axis=0)  3.37 us
    dot_general x2, matrix products, project(): jnp.einsum('cd,dkh->kch', feats, proj_weight, preferred_element_type=jnp....  3.16 us
    ppermute x1, starting transfers between devices, per_device(): peer = lax.ppermute(mine, 'blk', swap)  2.97 us
    convert_element_type x2, other arithmetic, project(): gate = jax.nn.silu(proj[1]).astype(jnp.bfloat16)  2.06 us
    ppermute x1, starting transfers between devices, per_device(): gate_back = lax.ppermute(gate_peer, 'blk', swap)  1.96 us
  transfers between devices with their start and end apart: 4, of which 1 were waited for; matrix products, arithmetic and copies ran while one was open for 54% of the time, Pallas kernels for 0%

profile of v7, /device:TPU:0, one launch (start us, length us, event | category | flops | bytes accessed | tf_op | source)
XLA Modules:
  0.0 40.6 jit_solution(14185034732738306895)
XLA Ops:
  0.0 0.0 copy-start
  0.0 3.0 %collective-permute-start = (bf16[128,1024]{1,0:T(8,128)(2,1)}, bf16[128,1024]{1,0:T(8,128)(2,1)}, u32[]{:S(2)}, u32[]{:S(2)}) collective-permute-start(bf16[128,1024]{1,0:T(8,128)(2,1)} %bitcast.64), channel_id=1, source_target_pairs={{0,4},{4,0},{1,5},{5,1},{2,6},{6,2},{3,7},{7,3},{8,12},{12,8},{9,1... | collective-permute-start | bytes 786440 | tf_op jit(solution)/shard_map/ppermute | solution.py:81
  3.0 0.7 %compare_and_fusion = pred[4]{0:T(512)(128)(4,1)S(1)} fusion(s32[4]{0:T(128)} %param.10), kind=kLoop, calls=%fused_computation.41 | loop fusion | flops 24 | bytes 20 | tf_op jit(solution)/shard_map/jit(_take)/and | solution.py:58
  3.6 0.7 %compare_select_fusion = s32[4]{0:T(128)S(1)} fusion(s32[4]{0:T(128)} %param.10), kind=kLoop, calls=%fused_computation.38 | loop fusion | flops 12 | bytes 32 | tf_op jit(solution)/shard_map/jit(_take)/jit(_where)/select_n | solution.py:58
  4.3 0.0 copy-done
  4.3 2.7 %gather_fusion = bf16[4,64,2,1024]{3,2,1,0:T(2,128)(2,1)S(1)} fusion(bf16[4,64,2,1024]{3,2,1,0:T(2,128)(2,1)S(1)} %copy-done, s32[1024]{0:T(1024)S(1)} %pad_clamp_fusion), kind=kCustom, calls=%fused_computation | custom fusion | bytes 2097168 | tf_op jit(solution)/shard_map/jit(_take)/gather | solution.py:58
  7.0 0.7 %gather.7 = bf16[4,64,2,2,4,128]{5,4,3,2,1,0:T(4,128)(2,1)S(1)} reshape(bf16[4,64,2,1024]{3,2,1,0:T(2,128)(2,1)S(1)} %gather_fusion) | data formatting | bytes 2097152 | tf_op jit(solution)/shard_map/jit(_take)/gather | solution.py:58
  7.7 1.3 %copy_select_fusion = bf16[4,64,2,2,4,128]{5,1,4,2,0,3:T(8,128)(2,1)} fusion(bf16[4,64,2,2,4,128]{5,4,3,2,1,0:T(4,128)(2,1)S(1)} %gather.7, pred[4]{0:T(512)(128)(4,1)S(1)} %compare_and_fusion), kind=kLoop, calls=%fused_computation.7 | loop fusion | flops 524288 | bytes 2097156 | tf_op jit(solution)/shard_map/jit(_take)/select_n | solution.py:58
  9.0 4.2 %all-to-all-start = ((bf16[8,2,4,64,128]{4,3,2,1,0:T(8,128)(2,1)}), bf16[8,2,4,64,128]{4,3,2,1,0:T(8,128)(2,1)}, u32[]{:S(2)}, u32[]{:S(2)}) async-start(bf16[8,2,4,64,128]{4,3,2,1,0:T(8,128)(2,1)} %bitcast.1), calls=%async_computation | async-start | bytes 2097152 | tf_op jit(solution)/shard_map/all_to_all | solution.py:64
  13.2 0.0 copy-start.2
  13.2 4.8 %copy.17 = bf16[1024,2,512]{0,2,1:T(8,128)(2,1)S(1)} copy(bf16[1024,2,512]{2,1,0:T(2,128)(2,1)} %param.8) | data formatting | bytes 4194304 | tf_op args[2]
  18.0 0.0 copy-done.2
  18.0 0.0 copy-start.4
  18.0 0.0 copy-start.5
  18.0 1.5 %convolution_bitcast_fusion.1 = f32[2,128,512]{1,2,0:T(8,128)} fusion(bf16[1024,2,512]{0,2,1:T(8,128)(2,1)S(1)} %copy.17, bf16[1,128,1024]{2,1,0:T(8,128)(2,1)S(1)} %copy-done.2), kind=kOutput, calls=%fused_computation.4 | convolution fusion | flops 268435456 | bytes 2883584 | tf_op jit(solution)/shard_map/cd,dkh->kch/dot_general | solution.py:74
  19.5 0.0 copy-done.4
  19.5 0.6 %dynamic_slice.7 = s32[1]{0:T(128)} dynamic-slice(s32[4]{0:T(128)S(1)} %copy-done.4, s32[]{:T(128)S(6)} %select_n.50), dynamic_slice_sizes={1} | dynamic-slice | bytes 12 | tf_op jit(solution)/shard_map/jit(dynamic_index_in_dim)/dynamic_slice | solution.py:52
  22.1 0.0 copy-done.5
  22.1 0.6 %dynamic_slice.8 = s32[1]{0:T(128)} dynamic-slice(s32[4]{0:T(128)S(1)} %copy-done.5, s32[]{:T(128)S(6)} %select_n.51), dynamic_slice_sizes={1} | dynamic-slice | bytes 12 | tf_op jit(solution)/shard_map/jit(dynamic_index_in_dim)/dynamic_slice | solution.py:53
  22.7 0.6 %fusion.16 = f32[512]{0:T(512)S(1)} fusion(s32[]{:T(128)} %bitcast.13), kind=kLoop, calls=%fused_computation.40 | loop fusion | flops 1024 | bytes 2052 | tf_op jit(solution)/shard_map/convert_element_type | solution.py:26
  24.0 1.0 %slice.49 = bf16[1,128,512]{1,2,0:T(8,128)(2,1)S(1)} slice(f32[2,128,512]{1,2,0:T(8,128)} %convolution_bitcast_fusion.1), slice={[0:1], [0:128], [0:512]} | slice | bytes 262144 | tf_op jit(solution)/shard_map/slice | solution.py:75
  24.9 0.1 copy.18
  25.1 1.0 %multiply_convert_fusion.2 = bf16[1,128,512]{1,2,0:T(8,128)(2,1)S(1)} fusion(f32[2,128,512]{1,2,0:T(8,128)} %convolution_bitcast_fusion.1), kind=kLoop, calls=%fused_computation.34 | loop fusion | flops 327680 | bytes 393216 | tf_op jit(solution)/shard_map/convert_element_type | solution.py:76
  26.1 0.0 collective-permute-done
  26.1 1.7 %convolution_bitcast_fusion = f32[2,128,512]{1,2,0:T(8,128)S(1)} fusion(bf16[1024,2,512]{0,2,1:T(8,128)(2,1)S(1)} %copy.17, bf16[128,1024]{1,0:T(8,128)(2,1)} %collective-permute-done), kind=kOutput, calls=%fused_computation.3 | convolution fusion | flops 268435456 | bytes 2883584 | tf_op jit(solution)/shard_map/cd,dkh->kch/dot_general | solution.py:74
  27.8 0.0 copy-start.1
  27.8 0.8 %copy-done.1 = f32[2,128,512]{1,2,0:T(8,128)} copy-done((f32[2,128,512]{1,2,0:T(8,128)}, f32[2,128,512]{1,2,0:T(8,128)S(1)}, u32[]{:S(2)}) %copy-start.1) | copy-done | bytes 524312
  28.6 0.1 copy.21
  28.7 1.0 %multiply_convert_fusion.1 = bf16[128,512]{0,1:T(8,128)(2,1)S(1)} fusion(f32[2,128,512]{1,2,0:T(8,128)} %copy-done.1), kind=kLoop, calls=%fused_computation.33 | loop fusion | flops 327680 | bytes 393216 | tf_op jit(solution)/shard_map/convert_element_type | solution.py:76
  29.8 2.0 %collective-permute-start.2 = (bf16[128,512]{0,1:T(8,128)(2,1)S(1)}, bf16[128,512]{0,1:T(8,128)(2,1)S(1)}, u32[]{:S(2)}, u32[]{:S(2)}) collective-permute-start(bf16[128,512]{0,1:T(8,128)(2,1)S(1)} %multiply_convert_fusion.1), channel_id=1, source_target_pairs={{0,4},{4,0},{1,5},{5,1},{2,6},{6,2},{3,7},{7,3},{8,12},{12,8},{9,1... | collective-permute-start | bytes 393224 | tf_op jit(solution)/shard_map/ppermute | solution.py:84
  31.7 0.0 all-to-all-done
  31.7 1.3 %copy.16 = bf16[1,2,4,8,64,128]{5,4,3,2,1,0:T(8,128)(2,1)S(1)} copy(bf16[1,2,4,8,64,128]{5,4,2,1,3,0:T(8,128)(2,1)} %bitcast.3) | data formatting | bytes 2097152 | tf_op jit(solution)/shard_map/all_to_all | solution.py:64
  33.0 0.7 %convolution_convert_fusion = bf16[4,128,128]{2,1,0:T(8,128)(2,1)S(1)} fusion(f32[]{:T(128)S(6)} %convert_element_type.96, f32[512]{0:T(512)S(1)} %fusion.16, bf16[1,2,4,512,128]{4,3,2,1,0:T(8,128)(2,1)S(1)} %bitcast.60, bf16[128,4,128]{2,0,1:T(8,128)(2,1)S(1)} %copy.21), kind=kOutput, calls=%fused_computation.5 | convolution fusion | flops 136380416 | bytes 1312772 | tf_op jit(solution)/shard_map/hck,hkd->chd/dot_general | solution.py:28
  33.8 0.0 copy-start.3
  33.8 0.2 collective-permute-start.1
  34.0 0.7 %convolution_convert_fusion.1 = bf16[4,128,128]{2,1,0:T(8,128)(2,1)S(1)} fusion(f32[]{:T(128)S(6)} %convert_element_type.96, f32[512]{0:T(512)S(1)} %fusion.16, bf16[1,2,4,512,128]{4,3,2,1,0:T(8,128)(2,1)S(1)} %bitcast.61, bf16[128,4,128]{2,0,1:T(8,128)(2,1)S(1)} %copy.18), kind=kOutput, calls=%fused_computation.6 | convolution fusion | flops 136380416 | bytes 1312772 | tf_op jit(solution)/shard_map/hck,hkd->chd/dot_general | solution.py:28
  34.7 4.4 %collective-permute-done.1 = bf16[128,512]{0,1:T(8,128)(2,1)S(1)} collective-permute-done((bf16[128,512]{0,1:T(8,128)(2,1)S(1)}, bf16[128,512]{0,1:T(8,128)(2,1)S(1)}, u32[]{:S(2)}, u32[]{:S(2)}) %collective-permute-start.1) | collective-permute-done | bytes 131104 | tf_op jit(solution)/shard_map/ppermute | solution.py:86
  39.1 0.2 convert_reduce_fusion
  39.3 0.2 fusion.1
  39.5 0.0 collective-permute-done.2
  39.5 0.0 copy-done.3
  39.5 0.2 multiply_convert_fusion
  39.7 0.9 %copy.23 = bf16[1,128,1024]{2,1,0:T(8,128)(2,1)} copy(bf16[1,128,1024]{1,2,0:T(8,128)(2,1)S(1)} %multiply_convert_fusion) | data formatting | bytes 524288 | tf_op jit(solution)/shard_map/convert_element_type | solution.py:45
  (4 shorter events, 0.0 us)
Async XLA Ops:
  0.0 4.3 %copy-start = (bf16[4,64,2,1024]{3,2,1,0:T(2,128)(2,1)S(1)}, bf16[4,64,2,1024]{3,2,1,0:T(2,128)(2,1)}, u32[]{:S(2)}) copy-start(bf16[4,64,2,1024]{3,2,1,0:T(2,128)(2,1)} %param.7) | copy-start | bytes 3145732
  0.0 26.1 %collective-permute-start = (bf16[128,1024]{1,0:T(8,128)(2,1)}, bf16[128,1024]{1,0:T(8,128)(2,1)}, u32[]{:S(2)}, u32[]{:S(2)}) collective-permute-start(bf16[128,1024]{1,0:T(8,128)(2,1)} %bitcast.64), channel_id=1, source_target_pairs={{0,4},{4,0},{1,5},{5,1},{2,6},{6,2},{3,7},{7,3},{8,12},{12,8},{9,1... | collective-permute-start | bytes 786440 | tf_op jit(solution)/shard_map/ppermute | solution.py:81
  9.0 22.8 %all-to-all-start = ((bf16[8,2,4,64,128]{4,3,2,1,0:T(8,128)(2,1)}), bf16[8,2,4,64,128]{4,3,2,1,0:T(8,128)(2,1)}, u32[]{:S(2)}, u32[]{:S(2)}) async-start(bf16[8,2,4,64,128]{4,3,2,1,0:T(8,128)(2,1)} %bitcast.1), calls=%async_computation | async-start | bytes 2097152 | tf_op jit(solution)/shard_map/all_to_all | solution.py:64
  13.2 4.8 %copy-start.2 = (bf16[1,128,1024]{2,1,0:T(8,128)(2,1)S(1)}, bf16[1,128,1024]{2,1,0:T(8,128)(2,1)}, u32[]{:S(2)}) copy-start(bf16[1,128,1024]{2,1,0:T(8,128)(2,1)} %param.6) | copy-start | bytes 786436
  18.0 1.5 %copy-start.4 = (s32[4]{0:T(128)S(1)}, s32[4]{0:T(128)}, u32[]{:S(2)}) copy-start(s32[4]{0:T(128)} %param.10) | copy-start | bytes 52
  18.0 4.0 %copy-start.5 = (s32[4]{0:T(128)S(1)}, s32[4]{0:T(128)}, u32[]{:S(2)}) copy-start(s32[4]{0:T(128)} %param.11) | copy-start | bytes 52
  27.8 0.8 %copy-start.1 = (f32[2,128,512]{1,2,0:T(8,128)}, f32[2,128,512]{1,2,0:T(8,128)S(1)}, u32[]{:S(2)}) copy-start(f32[2,128,512]{1,2,0:T(8,128)S(1)} %convolution_bitcast_fusion) | copy-start | bytes 1572868
  29.8 9.7 %collective-permute-start.2 = (bf16[128,512]{0,1:T(8,128)(2,1)S(1)}, bf16[128,512]{0,1:T(8,128)(2,1)S(1)}, u32[]{:S(2)}, u32[]{:S(2)}) collective-permute-start(bf16[128,512]{0,1:T(8,128)(2,1)S(1)} %multiply_convert_fusion.1), channel_id=1, source_target_pairs={{0,4},{4,0},{1,5},{5,1},{2,6},{6,2},{3,7},{7,3},{8,12},{12,8},{9,1... | collective-permute-start | bytes 393224 | tf_op jit(solution)/shard_map/ppermute | solution.py:84
  33.8 5.7 %copy-start.3 = (f32[1024]{0:T(1024)S(1)}, f32[1024]{0:T(1024)}, u32[]{:S(2)}) copy-start(f32[1024]{0:T(1024)} %param.9) | copy-start | bytes 12292
  33.8 5.3 %collective-permute-start.1 = (bf16[128,512]{0,1:T(8,128)(2,1)S(1)}, bf16[128,512]{0,1:T(8,128)(2,1)S(1)}, u32[]{:S(2)}, u32[]{:S(2)}) collective-permute-start(bf16[128,512]{0,1:T(8,128)(2,1)S(1)} %bitcast.66), channel_id=1, source_target_pairs={{0,4},{4,0},{1,5},{5,1},{2,6},{6,2},{3,7},{7,3},{8,12},{12,8},{9,1... | collective-permute-start | bytes 393224 | tf_op jit(solution)/shard_map/ppermute | solution.py:86

commit v8 on v7

--- a/solution.py
+++ b/solution.py
@@ -55,6 +55,7 @@
     local_heads = half // HEAD_SIZE
 
     n_users, n_pos = kv_store.shape[0], kv_store.shape[1]
+    count, kv_store = lax.optimization_barrier((count, kv_store))
     ordered = jnp.take(kv_store, users, axis=0).reshape(
         n_users, n_pos, 2, n_blk, local_heads, HEAD_SIZE
     )

time: 41 us -> 42.3 us (1.032)
  local copies, waits for them, and re-layouts: 13.5 us -> 14.8 us
    dynamic_slice x1, local copies, waits for them, and re-layouts: 0.59 us -> 1.24 us  [per_device(): count = lax.dynamic_index_in_dim(lengths, person, 0, keepdims=False)]
    dynamic_slice x1, local copies, waits for them, and re-layouts: 0.58 us -> 1.24 us  [per_device(): person = lax.dynamic_index_in_dim(users, slot, 0, keepdims=False)]
    ppermute x1, waiting for transfers between devices: 4.39 us -> 3.97 us  [per_device(): back = lax.ppermute(sent, 'blk', swap)]
    unnamed x13 -> x9, local copies, waits for them, and re-layouts: 5.59 us -> 5.58 us
  transfers between devices with their start and end apart: 4 -> 4, of which waited for: 1 -> 1; matrix products, arithmetic and copies ran while one was open for 54% -> 56% of each run, Pallas kernels for 0% -> 0%
where the time goes in v8:
time: 42.3 us; the launch traced here: 41.8 us
  local copies, waits for them, and re-layouts  14.8 us (35%)
  starting transfers between devices  9.77 us (23%)
  other arithmetic  5.87 us (14%)
  matrix products  4.62 us (11%)
  waiting for transfers between devices  4 us (9%)
  between operations  2.77 us (7%)
    unnamed x9, local copies, waits for them, and re-layouts  5.58 us
    all_to_all x1, starting transfers between devices, per_device(): lax.all_to_all(ordered, ('blk', 'store'), split_axis=0, concat_axis=3, ti...  4.24 us
    ppermute x1, waiting for transfers between devices, per_device(): back = lax.ppermute(sent, 'blk', swap)  3.97 us
    gather x2, local copies, waits for them, and re-layouts, per_device(): jnp.take(kv_store, users, axis=0)  3.37 us
    dot_general x2, matrix products, project(): jnp.einsum('cd,dkh->kch', feats, proj_weight, preferred_element_type=jnp....  3.17 us
    ppermute x1, starting transfers between devices, per_device(): peer = lax.ppermute(mine, 'blk', swap)  2.97 us
    convert_element_type x2, other arithmetic, project(): gate = jax.nn.silu(proj[1]).astype(jnp.bfloat16)  2.06 us
    ppermute x1, starting transfers between devices, per_device(): gate_back = lax.ppermute(gate_peer, 'blk', swap)  1.96 us
  transfers between devices with their start and end apart: 4, of which 1 were waited for; matrix products, arithmetic and copies ran while one was open for 56% of the time, Pallas kernels for 0%

profile of v8, /device:TPU:0, one launch (start us, length us, event | category | flops | bytes accessed | tf_op | source)
XLA Modules:
  0.0 41.8 jit_solution(8973143083884687073)
XLA Ops:
  0.0 0.0 copy-start
  0.0 3.0 %collective-permute-start = (bf16[128,1024]{1,0:T(8,128)(2,1)}, bf16[128,1024]{1,0:T(8,128)(2,1)}, u32[]{:S(2)}, u32[]{:S(2)}) collective-permute-start(bf16[128,1024]{1,0:T(8,128)(2,1)} %bitcast.64), channel_id=1, source_target_pairs={{0,4},{4,0},{1,5},{5,1},{2,6},{6,2},{3,7},{7,3},{8,12},{12,8},{9,1... | collective-permute-start | bytes 786440 | tf_op jit(solution)/shard_map/ppermute | solution.py:82
  3.0 1.2 %dynamic_slice.7 = s32[1]{0:T(128)} dynamic-slice(s32[4]{0:T(128)} %param.10, s32[]{:T(128)S(6)} %select_n.49), dynamic_slice_sizes={1} | dynamic-slice | bytes 12 | tf_op jit(solution)/shard_map/jit(dynamic_index_in_dim)/dynamic_slice | solution.py:52
  5.5 0.7 %compare_and_fusion = pred[4]{0:T(512)(128)(4,1)S(1)} fusion(s32[4]{0:T(128)} %param.10), kind=kLoop, calls=%fused_computation.41 | loop fusion | flops 24 | bytes 20 | tf_op jit(solution)/shard_map/jit(_take)/and | solution.py:59
  6.2 0.7 %compare_select_fusion = s32[4]{0:T(128)S(1)} fusion(s32[4]{0:T(128)} %param.10), kind=kLoop, calls=%fused_computation.38 | loop fusion | flops 12 | bytes 32 | tf_op jit(solution)/shard_map/jit(_take)/jit(_where)/select_n | solution.py:59
  7.5 1.2 %dynamic_slice.8 = s32[1]{0:T(128)} dynamic-slice(s32[4]{0:T(128)} %param.11, s32[]{:T(128)S(6)} %select_n.50), dynamic_slice_sizes={1} | dynamic-slice | bytes 12 | tf_op jit(solution)/shard_map/jit(dynamic_index_in_dim)/dynamic_slice | solution.py:53
  8.7 0.0 copy-done
  8.7 2.7 %gather_fusion = bf16[4,64,2,1024]{3,2,1,0:T(2,128)(2,1)S(1)} fusion(bf16[4,64,2,1024]{3,2,1,0:T(2,128)(2,1)S(1)} %copy-done, s32[1024]{0:T(1024)S(1)} %pad_clamp_fusion), kind=kCustom, calls=%fused_computation | custom fusion | bytes 2097168 | tf_op jit(solution)/shard_map/jit(_take)/gather | solution.py:59
  11.4 0.7 %gather.7 = bf16[4,64,2,2,4,128]{5,4,3,2,1,0:T(4,128)(2,1)S(1)} reshape(bf16[4,64,2,1024]{3,2,1,0:T(2,128)(2,1)S(1)} %gather_fusion) | data formatting | bytes 2097152 | tf_op jit(solution)/shard_map/jit(_take)/gather | solution.py:59
  12.1 1.3 %copy_select_fusion = bf16[4,64,2,2,4,128]{5,1,4,2,0,3:T(8,128)(2,1)} fusion(bf16[4,64,2,2,4,128]{5,4,3,2,1,0:T(4,128)(2,1)S(1)} %gather.7, pred[4]{0:T(512)(128)(4,1)S(1)} %compare_and_fusion), kind=kLoop, calls=%fused_computation.7 | loop fusion | flops 524288 | bytes 2097156 | tf_op jit(solution)/shard_map/jit(_take)/select_n | solution.py:59
  13.4 4.2 %all-to-all-start = ((bf16[8,2,4,64,128]{4,3,2,1,0:T(8,128)(2,1)}), bf16[8,2,4,64,128]{4,3,2,1,0:T(8,128)(2,1)}, u32[]{:S(2)}, u32[]{:S(2)}) async-start(bf16[8,2,4,64,128]{4,3,2,1,0:T(8,128)(2,1)} %bitcast.3), calls=%async_computation | async-start | bytes 2097152 | tf_op jit(solution)/shard_map/all_to_all | solution.py:65
  17.6 0.0 copy-start.2
  17.6 4.8 %copy.17 = bf16[1024,2,512]{0,2,1:T(8,128)(2,1)S(1)} copy(bf16[1024,2,512]{2,1,0:T(2,128)(2,1)} %param.8) | data formatting | bytes 4194304 | tf_op args[2]
  22.4 0.0 copy-done.2
  22.4 1.5 %convolution_bitcast_fusion.1 = f32[2,128,512]{1,2,0:T(8,128)} fusion(bf16[1024,2,512]{0,2,1:T(8,128)(2,1)S(1)} %copy.17, bf16[1,128,1024]{2,1,0:T(8,128)(2,1)S(1)} %copy-done.2), kind=kOutput, calls=%fused_computation.4 | convolution fusion | flops 268435456 | bytes 2883584 | tf_op jit(solution)/shard_map/cd,dkh->kch/dot_general | solution.py:75
  23.9 0.6 %fusion.16 = f32[512]{0:T(512)S(1)} fusion(s32[]{:T(128)} %bitcast.1), kind=kLoop, calls=%fused_computation.40 | loop fusion | flops 1024 | bytes 2052 | tf_op jit(solution)/shard_map/convert_element_type | solution.py:26
  25.2 1.0 %slice.49 = bf16[1,128,512]{1,2,0:T(8,128)(2,1)S(1)} slice(f32[2,128,512]{1,2,0:T(8,128)} %convolution_bitcast_fusion.1), slice={[0:1], [0:128], [0:512]} | slice | bytes 262144 | tf_op jit(solution)/shard_map/slice | solution.py:76
  26.2 0.1 copy.18
  26.3 1.0 %multiply_convert_fusion.2 = bf16[1,128,512]{1,2,0:T(8,128)(2,1)S(1)} fusion(f32[2,128,512]{1,2,0:T(8,128)} %convolution_bitcast_fusion.1), kind=kLoop, calls=%fused_computation.34 | loop fusion | flops 327680 | bytes 393216 | tf_op jit(solution)/shard_map/convert_element_type | solution.py:77
  27.4 0.0 collective-permute-done
  27.4 1.7 %convolution_bitcast_fusion = f32[2,128,512]{1,2,0:T(8,128)S(1)} fusion(bf16[1024,2,512]{0,2,1:T(8,128)(2,1)S(1)} %copy.17, bf16[128,1024]{1,0:T(8,128)(2,1)} %collective-permute-done), kind=kOutput, calls=%fused_computation.3 | convolution fusion | flops 268435456 | bytes 2883584 | tf_op jit(solution)/shard_map/cd,dkh->kch/dot_general | solution.py:75
  29.1 0.0 copy-start.1
  29.1 0.8 %copy-done.1 = f32[2,128,512]{1,2,0:T(8,128)} copy-done((f32[2,128,512]{1,2,0:T(8,128)}, f32[2,128,512]{1,2,0:T(8,128)S(1)}, u32[]{:S(2)}) %copy-start.1) | copy-done | bytes 524312
  29.9 0.1 copy.21
  30.0 1.0 %multiply_convert_fusion.1 = bf16[128,512]{0,1:T(8,128)(2,1)S(1)} fusion(f32[2,128,512]{1,2,0:T(8,128)} %copy-done.1), kind=kLoop, calls=%fused_computation.33 | loop fusion | flops 327680 | bytes 393216 | tf_op jit(solution)/shard_map/convert_element_type | solution.py:77
  31.0 2.0 %collective-permute-start.2 = (bf16[128,512]{0,1:T(8,128)(2,1)S(1)}, bf16[128,512]{0,1:T(8,128)(2,1)S(1)}, u32[]{:S(2)}, u32[]{:S(2)}) collective-permute-start(bf16[128,512]{0,1:T(8,128)(2,1)S(1)} %multiply_convert_fusion.1), channel_id=1, source_target_pairs={{0,4},{4,0},{1,5},{5,1},{2,6},{6,2},{3,7},{7,3},{8,12},{12,8},{9,1... | collective-permute-start | bytes 393224 | tf_op jit(solution)/shard_map/ppermute | solution.py:85
  33.0 0.0 all-to-all-done
  33.0 1.3 %copy.16 = bf16[1,2,4,8,64,128]{5,4,3,2,1,0:T(8,128)(2,1)S(1)} copy(bf16[1,2,4,8,64,128]{5,4,2,1,3,0:T(8,128)(2,1)} %bitcast.5) | data formatting | bytes 2097152 | tf_op jit(solution)/shard_map/all_to_all | solution.py:65
  34.4 0.7 %convolution_convert_fusion = bf16[4,128,128]{2,1,0:T(8,128)(2,1)S(1)} fusion(f32[]{:T(128)S(6)} %convert_element_type.96, f32[512]{0:T(512)S(1)} %fusion.16, bf16[1,2,4,512,128]{4,3,2,1,0:T(8,128)(2,1)S(1)} %bitcast.60, bf16[128,4,128]{2,0,1:T(8,128)(2,1)S(1)} %copy.21), kind=kOutput, calls=%fused_computation.5 | convolution fusion | flops 136380416 | bytes 1312772 | tf_op jit(solution)/shard_map/hck,hkd->chd/dot_general | solution.py:28
  35.1 0.0 copy-start.3
  35.1 0.6 %collective-permute-start.1 = (bf16[128,512]{0,1:T(8,128)(2,1)S(1)}, bf16[128,512]{0,1:T(8,128)(2,1)S(1)}, u32[]{:S(2)}, u32[]{:S(2)}) collective-permute-start(bf16[128,512]{0,1:T(8,128)(2,1)S(1)} %bitcast.66), channel_id=1, source_target_pairs={{0,4},{4,0},{1,5},{5,1},{2,6},{6,2},{3,7},{7,3},{8,12},{12,8},{9,1... | collective-permute-start | bytes 393224 | tf_op jit(solution)/shard_map/ppermute | solution.py:87
  35.7 0.7 %convolution_convert_fusion.1 = bf16[4,128,128]{2,1,0:T(8,128)(2,1)S(1)} fusion(f32[]{:T(128)S(6)} %convert_element_type.96, f32[512]{0:T(512)S(1)} %fusion.16, bf16[1,2,4,512,128]{4,3,2,1,0:T(8,128)(2,1)S(1)} %bitcast.61, bf16[128,4,128]{2,0,1:T(8,128)(2,1)S(1)} %copy.18), kind=kOutput, calls=%fused_computation.6 | convolution fusion | flops 136380416 | bytes 1312772 | tf_op jit(solution)/shard_map/hck,hkd->chd/dot_general | solution.py:28
  36.4 4.0 %collective-permute-done.1 = bf16[128,512]{0,1:T(8,128)(2,1)S(1)} collective-permute-done((bf16[128,512]{0,1:T(8,128)(2,1)S(1)}, bf16[128,512]{0,1:T(8,128)(2,1)S(1)}, u32[]{:S(2)}, u32[]{:S(2)}) %collective-permute-start.1) | collective-permute-done | bytes 131104 | tf_op jit(solution)/shard_map/ppermute | solution.py:87
  40.4 0.2 convert_reduce_fusion
  40.6 0.2 fusion.1
  40.8 0.0 collective-permute-done.2
  40.8 0.0 copy-done.3
  40.8 0.2 multiply_convert_fusion
  41.0 0.9 %copy.23 = bf16[1,128,1024]{2,1,0:T(8,128)(2,1)} copy(bf16[1,128,1024]{1,2,0:T(8,128)(2,1)S(1)} %multiply_convert_fusion) | data formatting | bytes 524288 | tf_op jit(solution)/shard_map/convert_element_type | solution.py:45
  (4 shorter events, 0.0 us)
Async XLA Ops:
  0.0 8.7 %copy-start = (bf16[4,64,2,1024]{3,2,1,0:T(2,128)(2,1)S(1)}, bf16[4,64,2,1024]{3,2,1,0:T(2,128)(2,1)}, u32[]{:S(2)}) copy-start(bf16[4,64,2,1024]{3,2,1,0:T(2,128)(2,1)} %param.7) | copy-start | bytes 3145732
  0.0 27.4 %collective-permute-start = (bf16[128,1024]{1,0:T(8,128)(2,1)}, bf16[128,1024]{1,0:T(8,128)(2,1)}, u32[]{:S(2)}, u32[]{:S(2)}) collective-permute-start(bf16[128,1024]{1,0:T(8,128)(2,1)} %bitcast.64), channel_id=1, source_target_pairs={{0,4},{4,0},{1,5},{5,1},{2,6},{6,2},{3,7},{7,3},{8,12},{12,8},{9,1... | collective-permute-start | bytes 786440 | tf_op jit(solution)/shard_map/ppermute | solution.py:82
  13.4 19.7 %all-to-all-start = ((bf16[8,2,4,64,128]{4,3,2,1,0:T(8,128)(2,1)}), bf16[8,2,4,64,128]{4,3,2,1,0:T(8,128)(2,1)}, u32[]{:S(2)}, u32[]{:S(2)}) async-start(bf16[8,2,4,64,128]{4,3,2,1,0:T(8,128)(2,1)} %bitcast.3), calls=%async_computation | async-start | bytes 2097152 | tf_op jit(solution)/shard_map/all_to_all | solution.py:65
  17.6 4.8 %copy-start.2 = (bf16[1,128,1024]{2,1,0:T(8,128)(2,1)S(1)}, bf16[1,128,1024]{2,1,0:T(8,128)(2,1)}, u32[]{:S(2)}) copy-start(bf16[1,128,1024]{2,1,0:T(8,128)(2,1)} %param.6) | copy-start | bytes 786436
  29.1 0.8 %copy-start.1 = (f32[2,128,512]{1,2,0:T(8,128)}, f32[2,128,512]{1,2,0:T(8,128)S(1)}, u32[]{:S(2)}) copy-start(f32[2,128,512]{1,2,0:T(8,128)S(1)} %convolution_bitcast_fusion) | copy-start | bytes 1572868
  31.0 9.7 %collective-permute-start.2 = (bf16[128,512]{0,1:T(8,128)(2,1)S(1)}, bf16[128,512]{0,1:T(8,128)(2,1)S(1)}, u32[]{:S(2)}, u32[]{:S(2)}) collective-permute-start(bf16[128,512]{0,1:T(8,128)(2,1)S(1)} %multiply_convert_fusion.1), channel_id=1, source_target_pairs={{0,4},{4,0},{1,5},{5,1},{2,6},{6,2},{3,7},{7,3},{8,12},{12,8},{9,1... | collective-permute-start | bytes 393224 | tf_op jit(solution)/shard_map/ppermute | solution.py:85
  35.1 5.7 %copy-start.3 = (f32[1024]{0:T(1024)S(1)}, f32[1024]{0:T(1024)}, u32[]{:S(2)}) copy-start(f32[1024]{0:T(1024)} %param.9) | copy-start | bytes 12292
  35.1 5.3 %collective-permute-start.1 = (bf16[128,512]{0,1:T(8,128)(2,1)S(1)}, bf16[128,512]{0,1:T(8,128)(2,1)S(1)}, u32[]{:S(2)}, u32[]{:S(2)}) collective-permute-start(bf16[128,512]{0,1:T(8,128)(2,1)S(1)} %bitcast.66), channel_id=1, source_target_pairs={{0,4},{4,0},{1,5},{5,1},{2,6},{6,2},{3,7},{7,3},{8,12},{12,8},{9,1... | collective-permute-start | bytes 393224 | tf_op jit(solution)/shard_map/ppermute | solution.py:87

commit v9 on v7

--- a/solution.py
+++ b/solution.py
@@ -71,7 +71,11 @@
     rows = mine.shape[0]
 
     def project(feats):
-        proj = jnp.einsum("cd,dkh->kch", feats, proj_weight, preferred_element_type=jnp.float32)
+        proj = jnp.dot(
+            feats, proj_weight.reshape(proj_weight.shape[0], 2 * half),
+            preferred_element_type=jnp.float32,
+        ).reshape(feats.shape[0], 2, half)
+        proj = jnp.transpose(proj, (1, 0, 2))
         query = proj[0].astype(jnp.bfloat16).reshape(-1, local_heads, HEAD_SIZE)
         gate = jax.nn.silu(proj[1]).astype(jnp.bfloat16)
         return jnp.transpose(query, (1, 0, 2)), gate

time: 41 us -> 41.2 us (level)
  other arithmetic: 5.87 us -> 6.49 us
  local copies, waits for them, and re-layouts: 13.5 us -> 12.9 us
    dot_general x0 -> x1, local copies, waits for them, and re-layouts: none -> 2.9 us  [project(): jnp.dot(feats, proj_weight.reshape(proj_weight.shape[0], 2 * half), prefe...]
    unnamed x13 -> x15, local copies, waits for them, and re-layouts: 5.59 us -> 2.75 us
    convert_element_type x1, other arithmetic: 0.22 us -> 0.87 us  [finish(): return (normed * gate.astype(jnp.float32)).astype(jnp.bfloat16)]
    convert_element_type x1 -> x2, local copies, waits for them, and re-layouts: 0.85 us -> 0.23 us  [the longest x1 0.11 us: per_device(): sent = attend(query_peer, keys, values, count).astype(jnp.bfloat16)]
  transfers between devices with their start and end apart: 4 -> 4, of which waited for: 1 -> 1; matrix products, arithmetic and copies ran while one was open for 54% -> 55% of each run, Pallas kernels for 0% -> 0%
where the time goes in v9:
time: 41.2 us; the launch traced here: 40.7 us
  local copies, waits for them, and re-layouts  12.9 us (31%)
  starting transfers between devices  9.51 us (23%)
  other arithmetic  6.49 us (16%)
  matrix products  4.86 us (12%)
  waiting for transfers between devices  4.17 us (10%)
  between operations  2.81 us (7%)
    all_to_all x1, starting transfers between devices, per_device(): lax.all_to_all(ordered, ('blk', 'store'), split_axis=0, concat_axis=3, ti...  4.37 us
    ppermute x1, waiting for transfers between devices, per_device(): back = lax.ppermute(sent, 'blk', swap)  4.16 us
    dot_general x2, matrix products, project(): jnp.dot(feats, proj_weight.reshape(proj_weight.shape[0], 2 * half), prefe...  3.4 us
    gather x2, local copies, waits for them, and re-layouts, per_device(): jnp.take(kv_store, users, axis=0)  3.37 us
    ppermute x1, starting transfers between devices, per_device(): peer = lax.ppermute(mine, 'blk', swap)  2.97 us
    dot_general x1, local copies, waits for them, and re-layouts, project(): jnp.dot(feats, proj_weight.reshape(proj_weight.shape[0], 2 * half), prefe...  2.9 us
    unnamed x15, local copies, waits for them, and re-layouts  2.75 us
    convert_element_type x2, other arithmetic, project(): gate = jax.nn.silu(proj[1]).astype(jnp.bfloat16)  2.06 us
  transfers between devices with their start and end apart: 4, of which 1 were waited for; matrix products, arithmetic and copies ran while one was open for 55% of the time, Pallas kernels for 0%

profile of v9, /device:TPU:0, one launch (start us, length us, event | category | flops | bytes accessed | tf_op | source)
XLA Modules:
  0.0 40.7 jit_solution(18245201785850864384)
XLA Ops:
  0.0 0.0 copy-start
  0.0 3.0 %collective-permute-start = (bf16[128,1024]{1,0:T(8,128)(2,1)}, bf16[128,1024]{1,0:T(8,128)(2,1)}, u32[]{:S(2)}, u32[]{:S(2)}) collective-permute-start(bf16[128,1024]{1,0:T(8,128)(2,1)} %bitcast.68), channel_id=1, source_target_pairs={{0,4},{4,0},{1,5},{5,1},{2,6},{6,2},{3,7},{7,3},{8,12},{12,8},{9,1... | collective-permute-start | bytes 786440 | tf_op jit(solution)/shard_map/ppermute | solution.py:85
  3.0 0.7 %compare_select_fusion = s32[4]{0:T(128)S(1)} fusion(s32[4]{0:T(128)} %param.10), kind=kLoop, calls=%fused_computation.40 | loop fusion | flops 12 | bytes 32 | tf_op jit(solution)/shard_map/jit(_take)/jit(_where)/select_n | solution.py:58
  3.6 0.7 %compare_and_fusion = pred[4]{0:T(512)(128)(4,1)S(1)} fusion(s32[4]{0:T(128)} %param.10), kind=kLoop, calls=%fused_computation.43 | loop fusion | flops 24 | bytes 20 | tf_op jit(solution)/shard_map/jit(_take)/and | solution.py:58
  4.3 0.0 copy-done
  4.3 2.7 %gather_fusion = bf16[4,64,2,1024]{3,2,1,0:T(2,128)(2,1)S(1)} fusion(bf16[4,64,2,1024]{3,2,1,0:T(2,128)(2,1)S(1)} %copy-done, s32[1024]{0:T(1024)S(1)} %pad_clamp_fusion), kind=kCustom, calls=%fused_computation | custom fusion | bytes 2097168 | tf_op jit(solution)/shard_map/jit(_take)/gather | solution.py:58
  7.0 0.7 %gather.7 = bf16[4,64,2,2,4,128]{5,4,3,2,1,0:T(4,128)(2,1)S(1)} reshape(bf16[4,64,2,1024]{3,2,1,0:T(2,128)(2,1)S(1)} %gather_fusion) | data formatting | bytes 2097152 | tf_op jit(solution)/shard_map/jit(_take)/gather | solution.py:58
  7.7 1.2 %copy_select_fusion = bf16[4,64,2,2,4,128]{5,1,4,2,0,3:T(8,128)(2,1)} fusion(bf16[4,64,2,2,4,128]{5,4,3,2,1,0:T(4,128)(2,1)S(1)} %gather.7, pred[4]{0:T(512)(128)(4,1)S(1)} %compare_and_fusion), kind=kLoop, calls=%fused_computation.7 | loop fusion | flops 524288 | bytes 2097156 | tf_op jit(solution)/shard_map/jit(_take)/select_n | solution.py:58
  8.9 0.0 copy-start.1
  8.9 4.4 %all-to-all-start = ((bf16[8,2,4,64,128]{4,3,2,1,0:T(8,128)(2,1)}), bf16[8,2,4,64,128]{4,3,2,1,0:T(8,128)(2,1)}, u32[]{:S(2)}, u32[]{:S(2)}) async-start(bf16[8,2,4,64,128]{4,3,2,1,0:T(8,128)(2,1)} %bitcast.1), calls=%async_computation | async-start | bytes 2097152 | tf_op jit(solution)/shard_map/all_to_all | solution.py:64
  13.3 0.0 copy-done.1
  13.3 1.9 %copy.31 = bf16[128,8,2,512]{3,1,2,0:T(8,128)(2,1)} copy(bf16[128,8,2,512]{3,2,1,0:T(2,128)(2,1)S(1)} %bitcast.62) | data formatting | bytes 4194304
  15.2 0.0 copy-start.3
  15.3 2.9 %copy.18 = bf16[1024,1024]{1,0:T(8,128)(2,1)S(1)} copy(bf16[1024,1024]{0,1:T(8,128)(2,1)} %bitcast.61) | data formatting | bytes 4194304 | tf_op jit(solution)/shard_map/dot_general | solution.py:74
  18.2 0.0 copy-start.5
  18.2 0.0 copy-start.6
  18.2 0.0 copy-done.3
  18.2 1.6 %convolution_bitcast_fusion.1 = f32[2,128,512]{2,1,0:T(8,128)} fusion(bf16[2,512,1024]{2,1,0:T(8,128)(2,1)S(1)} %bitcast.59, bf16[1,128,1024]{2,1,0:T(8,128)(2,1)S(1)} %copy-done.3), kind=kOutput, calls=%fused_computation.4 | convolution fusion | flops 268435456 | bytes 2883584 | tf_op jit(solution)/shard_map/dot_general | solution.py:74
  19.8 0.0 copy-done.5
  19.8 0.6 %dynamic_slice.7 = s32[1]{0:T(128)} dynamic-slice(s32[4]{0:T(128)S(1)} %copy-done.5, s32[]{:T(128)S(6)} %select_n.50), dynamic_slice_sizes={1} | dynamic-slice | bytes 12 | tf_op jit(solution)/shard_map/jit(dynamic_index_in_dim)/dynamic_slice | solution.py:52
  22.3 0.0 copy-done.6
  22.4 0.6 %dynamic_slice.8 = s32[1]{0:T(128)} dynamic-slice(s32[4]{0:T(128)S(1)} %copy-done.6, s32[]{:T(128)S(6)} %select_n.51), dynamic_slice_sizes={1} | dynamic-slice | bytes 12 | tf_op jit(solution)/shard_map/jit(dynamic_index_in_dim)/dynamic_slice | solution.py:53
  22.9 0.6 %fusion.20 = f32[512]{0:T(512)S(1)} fusion(s32[]{:T(128)} %bitcast.14), kind=kLoop, calls=%fused_computation.42 | loop fusion | flops 1024 | bytes 2052 | tf_op jit(solution)/shard_map/convert_element_type | solution.py:26
  24.2 1.0 %slice.49 = bf16[1,128,512]{2,1,0:T(8,128)(2,1)S(1)} slice(f32[2,128,512]{2,1,0:T(8,128)} %convolution_bitcast_fusion.1), slice={[0:1], [0:128], [0:512]} | slice | bytes 262144 | tf_op jit(solution)/shard_map/slice | solution.py:79
  25.3 1.0 %multiply_convert_fusion.2 = bf16[1,128,512]{2,1,0:T(8,128)(2,1)S(1)} fusion(f32[2,128,512]{2,1,0:T(8,128)} %convolution_bitcast_fusion.1), kind=kLoop, calls=%fused_computation.34 | loop fusion | flops 327680 | bytes 393216 | tf_op jit(solution)/shard_map/convert_element_type | solution.py:80
  26.3 0.0 collective-permute-done
  26.3 1.8 %convolution_bitcast_fusion = f32[2,128,512]{2,1,0:T(8,128)S(1)} fusion(bf16[2,512,1024]{2,1,0:T(8,128)(2,1)S(1)} %bitcast.60, bf16[128,1024]{1,0:T(8,128)(2,1)} %collective-permute-done), kind=kOutput, calls=%fused_computation.3 | convolution fusion | flops 268435456 | bytes 2883584 | tf_op jit(solution)/shard_map/dot_general | solution.py:74
  28.1 0.0 copy-start.2
  28.1 0.8 %copy-done.2 = f32[2,128,512]{2,1,0:T(8,128)} copy-done((f32[2,128,512]{2,1,0:T(8,128)}, f32[2,128,512]{2,1,0:T(8,128)S(1)}, u32[]{:S(2)}) %copy-start.2) | copy-done | bytes 524312
  28.9 1.0 %multiply_convert_fusion.1 = bf16[128,512]{1,0:T(8,128)(2,1)S(1)} fusion(f32[2,128,512]{2,1,0:T(8,128)} %copy-done.2), kind=kLoop, calls=%fused_computation.33 | loop fusion | flops 327680 | bytes 393216 | tf_op jit(solution)/shard_map/convert_element_type | solution.py:80
  30.0 2.0 %collective-permute-start.2 = (bf16[128,512]{1,0:T(8,128)(2,1)S(1)}, bf16[128,512]{1,0:T(8,128)(2,1)S(1)}, u32[]{:S(2)}, u32[]{:S(2)}) collective-permute-start(bf16[128,512]{1,0:T(8,128)(2,1)S(1)} %multiply_convert_fusion.1), channel_id=1, source_target_pairs={{0,4},{4,0},{1,5},{5,1},{2,6},{6,2},{3,7},{7,3},{8,12},{12,8},{9,1... | collective-permute-start | bytes 393224 | tf_op jit(solution)/shard_map/ppermute | solution.py:88
  31.9 0.0 all-to-all-done
  31.9 1.3 %copy.17 = bf16[1,2,4,8,64,128]{5,4,3,2,1,0:T(8,128)(2,1)S(1)} copy(bf16[1,2,4,8,64,128]{5,4,2,1,3,0:T(8,128)(2,1)} %bitcast.3) | data formatting | bytes 2097152 | tf_op jit(solution)/shard_map/all_to_all | solution.py:64
  33.3 0.7 %convolution_convert_fusion = bf16[4,128,128]{2,1,0:T(8,128)(2,1)S(1)} fusion(f32[]{:T(128)S(6)} %convert_element_type.96, f32[512]{0:T(512)S(1)} %fusion.20, bf16[1,2,4,512,128]{4,3,2,1,0:T(8,128)(2,1)S(1)} %bitcast.64, bf16[128,4,128]{2,1,0:T(4,128)(2,1)S(1)} %convert_element_type.100), kind=kOutput, calls=%fused_computation.5 | convolution fusion | flops 136380416 | bytes 1312772 | tf_op jit(solution)/shard_map/hck,hkd->chd/dot_general | solution.py:28
  34.0 0.1 copy.29
  34.1 0.0 copy-start.4
  34.1 0.2 collective-permute-start.1
  34.3 0.7 %convolution_convert_fusion.1 = bf16[4,128,128]{2,1,0:T(8,128)(2,1)S(1)} fusion(f32[]{:T(128)S(6)} %convert_element_type.96, f32[512]{0:T(512)S(1)} %fusion.20, bf16[1,2,4,512,128]{4,3,2,1,0:T(8,128)(2,1)S(1)} %bitcast.65, bf16[128,4,128]{2,1,0:T(4,128)(2,1)S(1)} %convert_element_type.94), kind=kOutput, calls=%fused_computation.6 | convolution fusion | flops 136380416 | bytes 1312772 | tf_op jit(solution)/shard_map/hck,hkd->chd/dot_general | solution.py:28
  35.1 0.1 copy.30
  35.2 0.1 copy.28
  35.3 4.2 %collective-permute-done.1 = bf16[128,512]{1,0:T(8,128)(2,1)S(1)} collective-permute-done((bf16[128,512]{1,0:T(8,128)(2,1)S(1)}, bf16[128,512]{1,0:T(8,128)(2,1)S(1)}, u32[]{:S(2)}, u32[]{:S(2)}) %collective-permute-start.1) | collective-permute-done | bytes 131104 | tf_op jit(solution)/shard_map/ppermute | solution.py:90
  39.5 0.1 convert_reduce_fusion
  39.6 0.2 fusion.1
  39.8 0.0 collective-permute-done.2
  39.8 0.0 copy-done.4
  39.8 0.9 %multiply_convert_fusion = bf16[1,128,1024]{2,1,0:T(8,128)(2,1)} fusion(bf16[1,128,512]{2,1,0:T(8,128)(2,1)S(1)} %bitcast.63, bf16[1,128,512]{2,1,0:T(8,128)(2,1)S(1)} %copy.28, bf16[1,128,512]{2,1,0:T(8,128)(2,1)S(1)} %bitcast.70, bf16[1,128,512]{2,1,0:T(8,128)(2,1)S(1)} %multiply_convert_fusion.2, f32[1024]{0:T(1024)S(1)} %copy-done.4, ...), kind=kLoop, calls=%fused_computation.16 | loop fusion | flops 3276800 | bytes 791553 | tf_op jit(solution)/shard_map/convert_element_type | solution.py:45
  (6 shorter events, 0.1 us)
Async XLA Ops:
  0.0 4.3 %copy-start = (bf16[4,64,2,1024]{3,2,1,0:T(2,128)(2,1)S(1)}, bf16[4,64,2,1024]{3,2,1,0:T(2,128)(2,1)}, u32[]{:S(2)}) copy-start(bf16[4,64,2,1024]{3,2,1,0:T(2,128)(2,1)} %param.7) | copy-start | bytes 3145732
  0.0 26.3 %collective-permute-start = (bf16[128,1024]{1,0:T(8,128)(2,1)}, bf16[128,1024]{1,0:T(8,128)(2,1)}, u32[]{:S(2)}, u32[]{:S(2)}) collective-permute-start(bf16[128,1024]{1,0:T(8,128)(2,1)} %bitcast.68), channel_id=1, source_target_pairs={{0,4},{4,0},{1,5},{5,1},{2,6},{6,2},{3,7},{7,3},{8,12},{12,8},{9,1... | collective-permute-start | bytes 786440 | tf_op jit(solution)/shard_map/ppermute | solution.py:85
  8.9 4.4 %copy-start.1 = (bf16[1024,2,512]{2,1,0:T(2,128)(2,1)S(1)}, bf16[1024,2,512]{2,1,0:T(2,128)(2,1)}, u32[]{:S(2)}) copy-start(bf16[1024,2,512]{2,1,0:T(2,128)(2,1)} %param.8) | copy-start | bytes 6291460
  8.9 23.0 %all-to-all-start = ((bf16[8,2,4,64,128]{4,3,2,1,0:T(8,128)(2,1)}), bf16[8,2,4,64,128]{4,3,2,1,0:T(8,128)(2,1)}, u32[]{:S(2)}, u32[]{:S(2)}) async-start(bf16[8,2,4,64,128]{4,3,2,1,0:T(8,128)(2,1)} %bitcast.1), calls=%async_computation | async-start | bytes 2097152 | tf_op jit(solution)/shard_map/all_to_all | solution.py:64
  15.2 2.9 %copy-start.3 = (bf16[1,128,1024]{2,1,0:T(8,128)(2,1)S(1)}, bf16[1,128,1024]{2,1,0:T(8,128)(2,1)}, u32[]{:S(2)}) copy-start(bf16[1,128,1024]{2,1,0:T(8,128)(2,1)} %param.6) | copy-start | bytes 786436
  18.2 1.7 %copy-start.5 = (s32[4]{0:T(128)S(1)}, s32[4]{0:T(128)}, u32[]{:S(2)}) copy-start(s32[4]{0:T(128)} %param.10) | copy-start | bytes 52
  18.2 4.2 %copy-start.6 = (s32[4]{0:T(128)S(1)}, s32[4]{0:T(128)}, u32[]{:S(2)}) copy-start(s32[4]{0:T(128)} %param.11) | copy-start | bytes 52
  28.1 0.8 %copy-start.2 = (f32[2,128,512]{2,1,0:T(8,128)}, f32[2,128,512]{2,1,0:T(8,128)S(1)}, u32[]{:S(2)}) copy-start(f32[2,128,512]{2,1,0:T(8,128)S(1)} %convolution_bitcast_fusion) | copy-start | bytes 1572868
  30.0 9.9 %collective-permute-start.2 = (bf16[128,512]{1,0:T(8,128)(2,1)S(1)}, bf16[128,512]{1,0:T(8,128)(2,1)S(1)}, u32[]{:S(2)}, u32[]{:S(2)}) collective-permute-start(bf16[128,512]{1,0:T(8,128)(2,1)S(1)} %multiply_convert_fusion.1), channel_id=1, source_target_pairs={{0,4},{4,0},{1,5},{5,1},{2,6},{6,2},{3,7},{7,3},{8,12},{12,8},{9,1... | collective-permute-start | bytes 393224 | tf_op jit(solution)/shard_map/ppermute | solution.py:88
  34.1 5.7 %copy-start.4 = (f32[1024]{0:T(1024)S(1)}, f32[1024]{0:T(1024)}, u32[]{:S(2)}) copy-start(f32[1024]{0:T(1024)} %param.9) | copy-start | bytes 12292
  34.1 5.3 %collective-permute-start.1 = (bf16[128,512]{1,0:T(8,128)(2,1)S(1)}, bf16[128,512]{1,0:T(8,128)(2,1)S(1)}, u32[]{:S(2)}, u32[]{:S(2)}) collective-permute-start(bf16[128,512]{1,0:T(8,128)(2,1)S(1)} %copy.29), channel_id=1, source_target_pairs={{0,4},{4,0},{1,5},{5,1},{2,6},{6,2},{3,7},{7,3},{8,12},{12,8},{9,1... | collective-permute-start | bytes 393224 | tf_op jit(solution)/shard_map/ppermute | solution.py:90

commit v10 on v7

--- a/solution.py
+++ b/solution.py
@@ -71,9 +71,10 @@
     rows = mine.shape[0]
 
     def project(feats):
-        proj = jnp.einsum("cd,dkh->kch", feats, proj_weight, preferred_element_type=jnp.float32)
-        query = proj[0].astype(jnp.bfloat16).reshape(-1, local_heads, HEAD_SIZE)
-        gate = jax.nn.silu(proj[1]).astype(jnp.bfloat16)
+        query = jnp.dot(feats, proj_weight[:, 0, :], preferred_element_type=jnp.float32)
+        query = query.astype(jnp.bfloat16).reshape(-1, local_heads, HEAD_SIZE)
+        gate = jnp.dot(feats, proj_weight[:, 1, :], preferred_element_type=jnp.float32)
+        gate = jax.nn.silu(gate).astype(jnp.bfloat16)
         return jnp.transpose(query, (1, 0, 2)), gate
 
     if n_blk == 2:

time: 41 us -> 42.5 us (1.037)
  matrix products: 4.61 us -> 8.82 us
  local copies, waits for them, and re-layouts: 13.5 us -> 11.2 us
    unnamed x13 -> x18, local copies, waits for them, and re-layouts: 5.59 us -> 0.04 us
    dot_general x2 -> x4, matrix products: 3.16 us -> 7.37 us  [the longest x2 3.97 us: project(): jnp.dot(feats, proj_weight[:, 0, :], preferred_element_type=jnp.float32)]
    slice x2 -> x1, local copies, waits for them, and re-layouts: 0.98 us -> 4.17 us  [project(): proj_weight[:, 1, :]]
    convert_element_type x2 -> x0, other arithmetic: 2.06 us -> none  [project(): gate = jax.nn.silu(proj[1]).astype(jnp.bfloat16)]
    select_n x2, other arithmetic: 1.93 us -> 3.24 us  [per_device(): jnp.take(kv_store, users, axis=0)]
    convert_element_type x3 -> x2, local copies, waits for them, and re-layouts: 1.11 us -> 0.23 us  [the longest x1 0.11 us: per_device(): sent = attend(query_peer, keys, values, count).astype(jnp.bfloat16)]
    gather x2, local copies, waits for them, and re-layouts: 3.37 us -> 4.13 us  [per_device(): jnp.take(kv_store, users, axis=0)]
    convert_element_type x1, other arithmetic: 0.22 us -> 0.87 us  [finish(): return (normed * gate.astype(jnp.float32)).astype(jnp.bfloat16)]
  transfers between devices with their start and end apart: 4 -> 4, of which waited for: 1 -> 1; matrix products, arithmetic and copies ran while one was open for 54% -> 59% of each run, Pallas kernels for 0% -> 0%
where the time goes in v10:
time: 42.5 us; the launch traced here: 42.1 us
  local copies, waits for them, and re-layouts  11.2 us (26%)
  starting transfers between devices  9.38 us (22%)
  matrix products  8.82 us (21%)
  other arithmetic  5.76 us (14%)
  waiting for transfers between devices  4.16 us (10%)
  between operations  2.8 us (7%)
    all_to_all x1, starting transfers between devices, per_device(): lax.all_to_all(ordered, ('blk', 'store'), split_axis=0, concat_axis=3, ti...  4.24 us
    slice x1, local copies, waits for them, and re-layouts, project(): proj_weight[:, 1, :]  4.17 us
    ppermute x1, waiting for transfers between devices, per_device(): back = lax.ppermute(sent, 'blk', swap)  4.15 us
    gather x2, local copies, waits for them, and re-layouts, per_device(): jnp.take(kv_store, users, axis=0)  4.13 us
    dot_general x2, matrix products, project(): jnp.dot(feats, proj_weight[:, 0, :], preferred_element_type=jnp.float32)  3.97 us
    dot_general x2, matrix products, project(): jnp.dot(feats, proj_weight[:, 1, :], preferred_element_type=jnp.float32)  3.4 us
    select_n x2, other arithmetic, per_device(): jnp.take(kv_store, users, axis=0)  3.24 us
    ppermute x1, starting transfers between devices, per_device(): peer = lax.ppermute(mine, 'blk', swap)  2.97 us
  transfers between devices with their start and end apart: 4, of which 1 were waited for; matrix products, arithmetic and copies ran while one was open for 59% of the time, Pallas kernels for 0%

profile of v10, /device:TPU:0, one launch (start us, length us, event | category | flops | bytes accessed | tf_op | source)
XLA Modules:
  0.0 42.1 jit_solution(13377265231186017087)
XLA Ops:
  0.0 0.0 copy-start
  0.0 3.0 %collective-permute-start = (bf16[128,1024]{1,0:T(8,128)(2,1)}, bf16[128,1024]{1,0:T(8,128)(2,1)}, u32[]{:S(2)}, u32[]{:S(2)}) collective-permute-start(bf16[128,1024]{1,0:T(8,128)(2,1)} %bitcast.80), channel_id=1, source_target_pairs={{0,4},{4,0},{1,5},{5,1},{2,6},{6,2},{3,7},{7,3},{8,12},{12,8},{9,1... | collective-permute-start | bytes 786440 | tf_op jit(solution)/shard_map/ppermute | solution.py:82
  3.0 0.7 %compare_and_fusion = pred[4]{0:T(512)(128)(4,1)S(1)} fusion(s32[4]{0:T(128)} %param.10), kind=kLoop, calls=%fused_computation.45 | loop fusion | flops 24 | bytes 20 | tf_op jit(solution)/shard_map/jit(_take)/and | solution.py:58
  3.6 0.7 %compare_select_fusion = s32[4]{0:T(128)S(1)} fusion(s32[4]{0:T(128)} %param.10), kind=kLoop, calls=%fused_computation.42 | loop fusion | flops 12 | bytes 32 | tf_op jit(solution)/shard_map/jit(_take)/jit(_where)/select_n | solution.py:58
  4.3 0.0 copy-done
  4.3 2.7 %gather_fusion = bf16[4,64,2,1024]{3,2,1,0:T(2,128)(2,1)S(1)} fusion(bf16[4,64,2,1024]{3,2,1,0:T(2,128)(2,1)S(1)} %copy-done, s32[1024]{0:T(1024)S(1)} %pad_clamp_fusion), kind=kCustom, calls=%fused_computation | custom fusion | bytes 2097168 | tf_op jit(solution)/shard_map/jit(_take)/gather | solution.py:58
  7.0 1.5 %gather.7 = bf16[4,64,2,2,4,128]{5,4,3,2,1,0:T(4,128)(2,1)} reshape(bf16[4,64,2,1024]{3,2,1,0:T(2,128)(2,1)S(1)} %gather_fusion) | data formatting | bytes 2097152 | tf_op jit(solution)/shard_map/jit(_take)/gather | solution.py:58
  8.4 0.0 copy-start.6
  8.4 0.0 copy-start.1
  8.4 2.6 %copy_select_fusion = bf16[4,64,2,2,4,128]{5,1,4,2,0,3:T(8,128)(2,1)} fusion(bf16[4,64,2,2,4,128]{5,4,3,2,1,0:T(4,128)(2,1)} %gather.7, pred[4]{0:T(512)(128)(4,1)S(1)} %compare_and_fusion), kind=kLoop, calls=%fused_computation.11 | loop fusion | flops 524288 | bytes 2097156 | tf_op jit(solution)/shard_map/jit(_take)/select_n | solution.py:58
  11.0 4.2 %all-to-all-start = ((bf16[8,2,4,64,128]{4,3,2,1,0:T(8,128)(2,1)}), bf16[8,2,4,64,128]{4,3,2,1,0:T(8,128)(2,1)}, u32[]{:S(2)}, u32[]{:S(2)}) async-start(bf16[8,2,4,64,128]{4,3,2,1,0:T(8,128)(2,1)} %bitcast.72), calls=%async_computation | async-start | bytes 2097152 | tf_op jit(solution)/shard_map/all_to_all | solution.py:64
  15.3 0.0 copy-done.6
  15.3 0.6 %dynamic_slice.7 = s32[1]{0:T(128)} dynamic-slice(s32[4]{0:T(128)S(1)} %copy-done.6, s32[]{:T(128)S(6)} %select_n.50), dynamic_slice_sizes={1} | dynamic-slice | bytes 12 | tf_op jit(solution)/shard_map/jit(dynamic_index_in_dim)/dynamic_slice | solution.py:52
  17.2 0.0 copy-done.1
  17.2 0.0 copy-start.7
  17.2 0.0 copy-start.5
  17.2 4.2 %fusion.26 = (bf16[1024,1,512]{2,1,0:T(2,128)(2,1)}, bf16[1024,1,512]{2,1,0:T(2,128)(2,1)}) fusion(bf16[1024,2,512]{2,1,0:T(2,128)(2,1)S(1)} %copy-done.1), kind=kLoop, calls=%fused_computation.54 | loop fusion | bytes 4194304 | tf_op jit(solution)/shard_map/slice | solution.py:76
  22.0 0.0 copy-done.7
  22.1 0.6 %dynamic_slice.8 = s32[1]{0:T(128)} dynamic-slice(s32[4]{0:T(128)S(1)} %copy-done.7, s32[]{:T(128)S(6)} %select_n.51), dynamic_slice_sizes={1} | dynamic-slice | bytes 12 | tf_op jit(solution)/shard_map/jit(dynamic_index_in_dim)/dynamic_slice | solution.py:53
  22.7 0.0 copy-done.5
  22.7 0.0 copy-start.3
  22.7 2.7 %fusion = bf16[16,4,8,128]{3,2,1,0:T(8,128)(2,1)} fusion(bf16[1024,1,512]{2,1,0:T(2,128)(2,1)} %get-tuple-element.6, bf16[1,128,1024]{2,1,0:T(8,128)(2,1)S(1)} %copy-done.5), kind=kOutput, calls=%fused_computation.7 | convolution fusion | flops 134283264 | bytes 1441792 | tf_op jit(solution)/shard_map/dot_general | solution.py:74
  25.4 0.6 %fusion.19 = f32[512]{0:T(512)S(1)} fusion(s32[]{:T(128)} %bitcast.11), kind=kLoop, calls=%fused_computation.44 | loop fusion | flops 1024 | bytes 2052 | tf_op jit(solution)/shard_map/convert_element_type | solution.py:26
  26.7 0.0 copy-start.2
  26.7 2.1 %fusion.14 = bf16[1,128,512]{2,1,0:T(8,128)(2,1)S(1)} fusion(bf16[1024,1,512]{2,1,0:T(2,128)(2,1)} %get-tuple-element.5, bf16[1,128,1024]{2,1,0:T(8,128)(2,1)S(1)} %copy-done.5), kind=kOutput, calls=%fused_computation.36 | convolution fusion | flops 134545408 | bytes 1441792 | tf_op jit(solution)/shard_map/dot_general | solution.py:76
  28.8 0.0 collective-permute-done
  28.8 0.0 copy-done.3
  28.8 1.3 %multiply_convert_fusion.1 = bf16[128,512]{1,0:T(8,128)(2,1)S(1)} fusion(bf16[128,1024]{1,0:T(8,128)(2,1)} %collective-permute-done, bf16[1024,1,512]{2,1,0:T(2,128)(2,1)S(1)} %copy-done.3), kind=kOutput, calls=%fused_computation.34 | convolution fusion | flops 134545408 | bytes 1441792 | tf_op jit(solution)/shard_map/dot_general | solution.py:76
  30.1 2.0 %collective-permute-start.2 = (bf16[128,512]{1,0:T(8,128)(2,1)S(1)}, bf16[128,512]{1,0:T(8,128)(2,1)S(1)}, u32[]{:S(2)}, u32[]{:S(2)}) collective-permute-start(bf16[128,512]{1,0:T(8,128)(2,1)S(1)} %multiply_convert_fusion.1), channel_id=1, source_target_pairs={{0,4},{4,0},{1,5},{5,1},{2,6},{6,2},{3,7},{7,3},{8,12},{12,8},{9,1... | collective-permute-start | bytes 393224 | tf_op jit(solution)/shard_map/ppermute | solution.py:85
  32.1 0.0 copy-done.2
  32.1 1.3 %fusion.1 = bf16[16,4,8,128]{3,2,1,0:T(8,128)(2,1)S(1)} fusion(bf16[128,1024]{1,0:T(8,128)(2,1)} %collective-permute-done, bf16[1024,1,512]{2,1,0:T(2,128)(2,1)S(1)} %copy-done.2), kind=kOutput, calls=%fused_computation.8 | convolution fusion | flops 134283264 | bytes 1441792 | tf_op jit(solution)/shard_map/dot_general | solution.py:74
  33.3 0.0 all-to-all-done
  33.4 1.3 %copy.30 = bf16[1,2,4,8,64,128]{5,4,3,2,1,0:T(8,128)(2,1)S(1)} copy(bf16[1,2,4,8,64,128]{5,4,2,1,3,0:T(8,128)(2,1)} %bitcast.3) | data formatting | bytes 2097152 | tf_op jit(solution)/shard_map/all_to_all | solution.py:64
  34.7 0.0 copy-start.8
  34.7 0.7 %convolution_convert_fusion = bf16[4,128,128]{2,1,0:T(8,128)(2,1)S(1)} fusion(f32[]{:T(128)S(6)} %convert_element_type.91, f32[512]{0:T(512)S(1)} %fusion.19, bf16[1,2,4,512,128]{4,3,2,1,0:T(8,128)(2,1)S(1)} %bitcast.74, bf16[16,4,8,128]{3,2,1,0:T(8,128)(2,1)S(1)} %fusion.1), kind=kOutput, calls=%fused_computation.3 | convolution fusion | flops 136380416 | bytes 1312772 | tf_op jit(solution)/shard_map/hck,hkd->chd/dot_general | solution.py:28
  35.4 0.1 copy.36
  35.5 0.0 copy-start.4
  35.6 0.2 collective-permute-start.1
  35.8 0.0 copy-done.8
  35.8 0.7 %convolution_convert_fusion.1 = bf16[4,128,128]{2,1,0:T(8,128)(2,1)S(1)} fusion(f32[]{:T(128)S(6)} %convert_element_type.91, f32[512]{0:T(512)S(1)} %fusion.19, bf16[1,2,4,512,128]{4,3,2,1,0:T(8,128)(2,1)S(1)} %bitcast.75, bf16[16,4,8,128]{3,2,1,0:T(8,128)(2,1)S(1)} %copy-done.8), kind=kOutput, calls=%fused_computation.4 | convolution fusion | flops 136380416 | bytes 1312772 | tf_op jit(solution)/shard_map/hck,hkd->chd/dot_general | solution.py:28
  36.5 0.1 copy.39
  36.6 0.1 copy.37
  36.7 4.2 %collective-permute-done.1 = bf16[128,512]{1,0:T(8,128)(2,1)S(1)} collective-permute-done((bf16[128,512]{1,0:T(8,128)(2,1)S(1)}, bf16[128,512]{1,0:T(8,128)(2,1)S(1)}, u32[]{:S(2)}, u32[]{:S(2)}) %collective-permute-start.1) | collective-permute-done | bytes 131104 | tf_op jit(solution)/shard_map/ppermute | solution.py:87
  40.9 0.1 convert_reduce_fusion
  41.0 0.2 fusion.3
  41.2 0.0 collective-permute-done.2
  41.3 0.0 copy-done.4
  41.3 0.9 %multiply_convert_fusion = bf16[1,128,1024]{2,1,0:T(8,128)(2,1)} fusion(bf16[1,128,512]{2,1,0:T(8,128)(2,1)S(1)} %bitcast.73, bf16[1,128,512]{2,1,0:T(8,128)(2,1)S(1)} %copy.37, bf16[1,128,512]{2,1,0:T(8,128)(2,1)S(1)} %bitcast.79, bf16[1,128,512]{2,1,0:T(8,128)(2,1)S(1)} %fusion.14, f32[1024]{0:T(1024)S(1)} %copy-done.4, f32[128]{0:T(128)S(1)} %add_rsqrt_fusion, ...), kind=kLoop, calls=%fused_computation.20 | loop fusion | flops 3276800 | bytes 791553 | tf_op jit(solution)/shard_map/convert_element_type | solution.py:45
  (3 shorter events, 0.0 us)
Async XLA Ops:
  0.0 4.3 %copy-start = (bf16[4,64,2,1024]{3,2,1,0:T(2,128)(2,1)S(1)}, bf16[4,64,2,1024]{3,2,1,0:T(2,128)(2,1)}, u32[]{:S(2)}) copy-start(bf16[4,64,2,1024]{3,2,1,0:T(2,128)(2,1)} %param.7) | copy-start | bytes 3145732
  0.0 28.8 %collective-permute-start = (bf16[128,1024]{1,0:T(8,128)(2,1)}, bf16[128,1024]{1,0:T(8,128)(2,1)}, u32[]{:S(2)}, u32[]{:S(2)}) collective-permute-start(bf16[128,1024]{1,0:T(8,128)(2,1)} %bitcast.80), channel_id=1, source_target_pairs={{0,4},{4,0},{1,5},{5,1},{2,6},{6,2},{3,7},{7,3},{8,12},{12,8},{9,1... | collective-permute-start | bytes 786440 | tf_op jit(solution)/shard_map/ppermute | solution.py:82
  8.4 6.8 %copy-start.6 = (s32[4]{0:T(128)S(1)}, s32[4]{0:T(128)}, u32[]{:S(2)}) copy-start(s32[4]{0:T(128)} %param.10) | copy-start | bytes 52
  8.4 8.7 %copy-start.1 = (bf16[1024,2,512]{2,1,0:T(2,128)(2,1)S(1)}, bf16[1024,2,512]{2,1,0:T(2,128)(2,1)}, u32[]{:S(2)}) copy-start(bf16[1024,2,512]{2,1,0:T(2,128)(2,1)} %param.8) | copy-start | bytes 6291460
  11.0 22.3 %all-to-all-start = ((bf16[8,2,4,64,128]{4,3,2,1,0:T(8,128)(2,1)}), bf16[8,2,4,64,128]{4,3,2,1,0:T(8,128)(2,1)}, u32[]{:S(2)}, u32[]{:S(2)}) async-start(bf16[8,2,4,64,128]{4,3,2,1,0:T(8,128)(2,1)} %bitcast.72), calls=%async_computation | async-start | bytes 2097152 | tf_op jit(solution)/shard_map/all_to_all | solution.py:64
  17.2 4.9 %copy-start.7 = (s32[4]{0:T(128)S(1)}, s32[4]{0:T(128)}, u32[]{:S(2)}) copy-start(s32[4]{0:T(128)} %param.11) | copy-start | bytes 52
  17.2 5.5 %copy-start.5 = (bf16[1,128,1024]{2,1,0:T(8,128)(2,1)S(1)}, bf16[1,128,1024]{2,1,0:T(8,128)(2,1)}, u32[]{:S(2)}) copy-start(bf16[1,128,1024]{2,1,0:T(8,128)(2,1)} %param.6) | copy-start | bytes 786436
  22.7 6.1 %copy-start.3 = (bf16[1024,1,512]{2,1,0:T(2,128)(2,1)S(1)}, bf16[1024,1,512]{2,1,0:T(2,128)(2,1)}, u32[]{:S(2)}) copy-start(bf16[1024,1,512]{2,1,0:T(2,128)(2,1)} %get-tuple-element.5) | copy-start | bytes 3145732
  26.7 5.4 %copy-start.2 = (bf16[1024,1,512]{2,1,0:T(2,128)(2,1)S(1)}, bf16[1024,1,512]{2,1,0:T(2,128)(2,1)}, u32[]{:S(2)}) copy-start(bf16[1024,1,512]{2,1,0:T(2,128)(2,1)} %get-tuple-element.6) | copy-start | bytes 3145732
  30.1 11.1 %collective-permute-start.2 = (bf16[128,512]{1,0:T(8,128)(2,1)S(1)}, bf16[128,512]{1,0:T(8,128)(2,1)S(1)}, u32[]{:S(2)}, u32[]{:S(2)}) collective-permute-start(bf16[128,512]{1,0:T(8,128)(2,1)S(1)} %multiply_convert_fusion.1), channel_id=1, source_target_pairs={{0,4},{4,0},{1,5},{5,1},{2,6},{6,2},{3,7},{7,3},{8,12},{12,8},{9,1... | collective-permute-start | bytes 393224 | tf_op jit(solution)/shard_map/ppermute | solution.py:85
  34.7 1.1 %copy-start.8 = (bf16[16,4,8,128]{3,2,1,0:T(8,128)(2,1)S(1)}, bf16[16,4,8,128]{3,2,1,0:T(8,128)(2,1)}, u32[]{:S(2)}) copy-start(bf16[16,4,8,128]{3,2,1,0:T(8,128)(2,1)} %fusion) | copy-start | bytes 393220
  35.5 5.7 %copy-start.4 = (f32[1024]{0:T(1024)S(1)}, f32[1024]{0:T(1024)}, u32[]{:S(2)}) copy-start(f32[1024]{0:T(1024)} %param.9) | copy-start | bytes 12292
  35.6 5.3 %collective-permute-start.1 = (bf16[128,512]{1,0:T(8,128)(2,1)S(1)}, bf16[128,512]{1,0:T(8,128)(2,1)S(1)}, u32[]{:S(2)}, u32[]{:S(2)}) collective-permute-start(bf16[128,512]{1,0:T(8,128)(2,1)S(1)} %copy.36), channel_id=1, source_target_pairs={{0,4},{4,0},{1,5},{5,1},{2,6},{6,2},{3,7},{7,3},{8,12},{12,8},{9,1... | collective-permute-start | bytes 393224 | tf_op jit(solution)/shard_map/ppermute | solution.py:87

commit v11 on v7

--- a/solution.py
+++ b/solution.py
@@ -55,7 +55,10 @@
     local_heads = half // HEAD_SIZE
 
     n_users, n_pos = kv_store.shape[0], kv_store.shape[1]
-    ordered = jnp.take(kv_store, users, axis=0).reshape(
+    chosen = jnp.concatenate(
+        [lax.dynamic_index_in_dim(kv_store, users[s], 0) for s in range(users.shape[0])]
+    )
+    ordered = chosen.reshape(
         n_users, n_pos, 2, n_blk, local_heads, HEAD_SIZE
     )
     ordered = jnp.transpose(ordered, (3, 0, 2, 4, 1, 5)).reshape(

time: 41 us -> 47.8 us (1.17)
  between operations: 2.78 us -> 10 us
  starting transfers between devices: 9.37 us -> 8.7 us
  other arithmetic: 5.87 us -> 5.23 us
  waiting for transfers between devices: 4.4 us -> 4.92 us
    gather x2 -> x0, local copies, waits for them, and re-layouts: 3.37 us -> none  [per_device(): jnp.take(kv_store, users, axis=0)]
    reshape x0 -> x2, local copies, waits for them, and re-layouts: none -> 1.97 us  [per_device(): ordered = chosen.reshape(n_users, n_pos, 2, n_blk, local_heads, HEAD_SIZE)]
    concatenate x0 -> x1, other arithmetic: none -> 1.96 us  [per_device(): jnp.concatenate([lax.dynamic_index_in_dim(kv_store, users[s], 0) for s in...]
    select_n x2 -> x0, other arithmetic: 1.93 us -> none  [per_device(): jnp.take(kv_store, users, axis=0)]
    slice x0 -> x1, local copies, waits for them, and re-layouts: none -> 1.51 us  [per_device(): users[s]]
    dynamic_slice x1, local copies, waits for them, and re-layouts: 0.58 us -> 1.93 us  [per_device(): lax.dynamic_index_in_dim(kv_store, users[s], 0)]
    all_to_all x1, local copies, waits for them, and re-layouts: 1.31 us -> 0.08 us  [per_device(): lax.all_to_all(ordered, ('blk', 'store'), split_axis=0, concat_axis=3, ti...]
    all_to_all x1, starting transfers between devices: 4.24 us -> 3.56 us  [per_device(): lax.all_to_all(ordered, ('blk', 'store'), split_axis=0, concat_axis=3, ti...]
  transfers between devices with their start and end apart: 4 -> 4, of which waited for: 1 -> 1; matrix products, arithmetic and copies ran while one was open for 54% -> 46% of each run, Pallas kernels for 0% -> 0%
where the time goes in v11:
time: 47.8 us; the launch traced here: 47.3 us
  local copies, waits for them, and re-layouts  13.8 us (29%)
  between operations  10 us (21%)
  starting transfers between devices  8.7 us (18%)
  other arithmetic  5.23 us (11%)
  waiting for transfers between devices  4.92 us (10%)
  matrix products  4.63 us (10%)
    unnamed x9, local copies, waits for them, and re-layouts  5.59 us
    ppermute x1, waiting for transfers between devices, per_device(): back = lax.ppermute(sent, 'blk', swap)  4.91 us
    all_to_all x1, starting transfers between devices, per_device(): lax.all_to_all(ordered, ('blk', 'store'), split_axis=0, concat_axis=3, ti...  3.56 us
    dot_general x2, matrix products, project(): jnp.einsum('cd,dkh->kch', feats, proj_weight, preferred_element_type=jnp....  3.17 us
    ppermute x1, starting transfers between devices, per_device(): peer = lax.ppermute(mine, 'blk', swap)  2.97 us
    convert_element_type x2, other arithmetic, project(): gate = jax.nn.silu(proj[1]).astype(jnp.bfloat16)  2.06 us
    ppermute x1, starting transfers between devices, per_device(): gate_back = lax.ppermute(gate_peer, 'blk', swap)  1.99 us
    reshape x2, local copies, waits for them, and re-layouts, per_device(): ordered = chosen.reshape(n_users, n_pos, 2, n_blk, local_heads, HEAD_SIZE)  1.97 us
  transfers between devices with their start and end apart: 4, of which 1 were waited for; matrix products, arithmetic and copies ran while one was open for 46% of the time, Pallas kernels for 0%

profile of v11, /device:TPU:0, one launch (start us, length us, event | category | flops | bytes accessed | tf_op | source)
XLA Modules:
  0.0 47.3 jit_solution(13406378997958957575)
XLA Ops:
  0.0 3.0 %collective-permute-start = (bf16[128,1024]{1,0:T(8,128)(2,1)}, bf16[128,1024]{1,0:T(8,128)(2,1)}, u32[]{:S(2)}, u32[]{:S(2)}) collective-permute-start(bf16[128,1024]{1,0:T(8,128)(2,1)} %bitcast.69), channel_id=1, source_target_pairs={{0,4},{4,0},{1,5},{5,1},{2,6},{6,2},{3,7},{7,3},{8,12},{12,8},{9,1... | collective-permute-start | bytes 786440 | tf_op jit(solution)/shard_map/ppermute | solution.py:84
  3.0 1.5 %fusion.21 = (s32[1]{0:T(128)}, s32[1]{0:T(128)}, s32[1]{0:T(128)}, s32[1]{0:T(128)}, s32[1]{0:T(128)}) fusion(s32[4]{0:T(128)} %param.10, s32[]{:T(128)S(6)} %select_n.55), kind=kLoop, calls=%fused_computation.48 | loop fusion | bytes 44 | tf_op jit(solution)/shard_map/slice | solution.py:59
  11.8 1.9 %constant_dynamic-slice_fusion.3 = (bf16[1,64,2,1024]{3,2,1,0:T(2,128)(2,1)S(1)}, bf16[1,64,2,1024]{3,2,1,0:T(2,128)(2,1)S(1)}, bf16[1,64,2,1024]{3,2,1,0:T(2,128)(2,1)S(1)}, bf16[1,64,2,1024]{3,2,1,0:T(2,128)(2,1)S(1)}) fusion(bf16[4,64,2,1024]{3,2,1,0:T(2,128)(2,1)} %param.7, s32[]{:T(128)S(6)} %select_n.51, s32[]{:T(128)S(6)} %select_n.52, ...), kind=kLoop, calls=%fused_computation.41 | loop fusion | bytes 2097168 | tf_op jit(solution)/shard_map/jit(dynamic_index_in_dim)/dynamic_slice | solution.py:59
  13.8 2.0 %pad_maximum_fusion = bf16[4,64,2,1024]{3,2,1,0:T(2,128)(2,1)S(1)} fusion(bf16[1,64,2,1024]{3,2,1,0:T(2,128)(2,1)S(1)} %get-tuple-element.7, bf16[1,64,2,1024]{3,2,1,0:T(2,128)(2,1)S(1)} %get-tuple-element.8, bf16[1,64,2,1024]{3,2,1,0:T(2,128)(2,1)S(1)} %get-tuple-element.6, bf16[1,64,2,1024]{3,2,1,0:T(2,128)(2,1)S(1)} %get-tuple-element.5), kind=kLoop, calls=%fused_computation.6 | loop fusion | flops 1572864 | bytes 2097152 | tf_op jit(solution)/shard_map/concatenate | solution.py:58
  15.7 0.7 %reshape.216 = bf16[4,64,2,2,4,128]{5,4,3,2,1,0:T(4,128)(2,1)S(1)} reshape(bf16[4,64,2,1024]{3,2,1,0:T(2,128)(2,1)S(1)} %pad_maximum_fusion) | data formatting | bytes 2097152 | tf_op jit(solution)/shard_map/reshape | solution.py:61
  16.5 1.3 %copy.15 = bf16[4,64,2,2,4,128]{5,1,4,2,0,3:T(8,128)(2,1)} copy(bf16[4,64,2,2,4,128]{5,4,3,2,1,0:T(4,128)(2,1)S(1)} %reshape.216) | data formatting | bytes 2097152 | tf_op jit(solution)/shard_map/reshape | solution.py:61
  17.7 3.6 %all-to-all-start = ((bf16[8,2,4,64,128]{4,3,2,1,0:T(8,128)(2,1)}), bf16[8,2,4,64,128]{4,3,2,1,0:T(8,128)(2,1)S(1)}, u32[]{:S(2)}, u32[]{:S(2)}) async-start(bf16[8,2,4,64,128]{4,3,2,1,0:T(8,128)(2,1)} %bitcast.5), calls=%async_computation | async-start | bytes 2097152 | tf_op jit(solution)/shard_map/all_to_all | solution.py:67
  21.3 0.0 copy-start.1
  21.3 4.8 %copy.17 = bf16[1024,2,512]{0,2,1:T(8,128)(2,1)S(1)} copy(bf16[1024,2,512]{2,1,0:T(2,128)(2,1)} %param.8) | data formatting | bytes 4194304 | tf_op args[2]
  26.1 0.0 copy-done.1
  26.1 0.0 copy-start.3
  26.1 1.5 %convolution_bitcast_fusion.1 = f32[2,128,512]{1,2,0:T(8,128)} fusion(bf16[1024,2,512]{0,2,1:T(8,128)(2,1)S(1)} %copy.17, bf16[1,128,1024]{2,1,0:T(8,128)(2,1)S(1)} %copy-done.1), kind=kOutput, calls=%fused_computation.3 | convolution fusion | flops 268435456 | bytes 2883584 | tf_op jit(solution)/shard_map/cd,dkh->kch/dot_general | solution.py:77
  29.5 0.0 copy-done.3
  29.5 0.6 %dynamic_slice.25 = s32[1]{0:T(128)} dynamic-slice(s32[4]{0:T(128)S(1)} %copy-done.3, s32[]{:T(128)S(6)} %select_n.56), dynamic_slice_sizes={1} | dynamic-slice | bytes 12 | tf_op jit(solution)/shard_map/jit(dynamic_index_in_dim)/dynamic_slice | solution.py:53
  30.1 0.6 %fusion.16 = f32[512]{0:T(512)S(1)} fusion(s32[]{:T(128)} %bitcast.17), kind=kLoop, calls=%fused_computation.37 | loop fusion | flops 1024 | bytes 2052 | tf_op jit(solution)/shard_map/convert_element_type | solution.py:26
  31.4 1.0 %slice.63 = bf16[1,128,512]{1,2,0:T(8,128)(2,1)S(1)} slice(f32[2,128,512]{1,2,0:T(8,128)} %convolution_bitcast_fusion.1), slice={[0:1], [0:128], [0:512]} | slice | bytes 262144 | tf_op jit(solution)/shard_map/slice | solution.py:78
  32.3 0.1 copy.18
  32.5 1.0 %multiply_convert_fusion.2 = bf16[1,128,512]{1,2,0:T(8,128)(2,1)S(1)} fusion(f32[2,128,512]{1,2,0:T(8,128)} %convolution_bitcast_fusion.1), kind=kLoop, calls=%fused_computation.33 | loop fusion | flops 327680 | bytes 393216 | tf_op jit(solution)/shard_map/convert_element_type | solution.py:79
  33.5 0.0 collective-permute-done
  33.5 1.7 %convolution_bitcast_fusion = f32[2,128,512]{1,2,0:T(8,128)S(1)} fusion(bf16[1024,2,512]{0,2,1:T(8,128)(2,1)S(1)} %copy.17, bf16[128,1024]{1,0:T(8,128)(2,1)} %collective-permute-done), kind=kOutput, calls=%fused_computation.2 | convolution fusion | flops 268435456 | bytes 2883584 | tf_op jit(solution)/shard_map/cd,dkh->kch/dot_general | solution.py:77
  35.2 0.0 copy-start
  35.2 0.8 %copy-done = f32[2,128,512]{1,2,0:T(8,128)} copy-done((f32[2,128,512]{1,2,0:T(8,128)}, f32[2,128,512]{1,2,0:T(8,128)S(1)}, u32[]{:S(2)}) %copy-start) | copy-done | bytes 524312
  36.0 0.1 copy.21
  36.1 1.0 %multiply_convert_fusion.1 = bf16[128,512]{0,1:T(8,128)(2,1)S(1)} fusion(f32[2,128,512]{1,2,0:T(8,128)} %copy-done), kind=kLoop, calls=%fused_computation.32 | loop fusion | flops 327680 | bytes 393216 | tf_op jit(solution)/shard_map/convert_element_type | solution.py:79
  37.2 2.0 %collective-permute-start.2 = (bf16[128,512]{0,1:T(8,128)(2,1)S(1)}, bf16[128,512]{0,1:T(8,128)(2,1)S(1)}, u32[]{:S(2)}, u32[]{:S(2)}) collective-permute-start(bf16[128,512]{0,1:T(8,128)(2,1)S(1)} %multiply_convert_fusion.1), channel_id=1, source_target_pairs={{0,4},{4,0},{1,5},{5,1},{2,6},{6,2},{3,7},{7,3},{8,12},{12,8},{9,1... | collective-permute-start | bytes 393224 | tf_op jit(solution)/shard_map/ppermute | solution.py:87
  39.2 0.0 all-to-all-done
  39.2 0.1 copy.16
  39.3 0.7 %convolution_convert_fusion = bf16[4,128,128]{2,1,0:T(8,128)(2,1)S(1)} fusion(f32[]{:T(128)S(6)} %convert_element_type.96, f32[512]{0:T(512)S(1)} %fusion.16, bf16[1,2,4,512,128]{4,3,2,1,0:T(8,128)(2,1)S(1)} %bitcast.65, bf16[128,4,128]{2,0,1:T(8,128)(2,1)S(1)} %copy.21), kind=kOutput, calls=%fused_computation.4 | convolution fusion | flops 136380416 | bytes 1312772 | tf_op jit(solution)/shard_map/hck,hkd->chd/dot_general | solution.py:28
  40.0 0.0 copy-start.2
  40.0 0.2 collective-permute-start.1
  40.2 0.7 %convolution_convert_fusion.1 = bf16[4,128,128]{2,1,0:T(8,128)(2,1)S(1)} fusion(f32[]{:T(128)S(6)} %convert_element_type.96, f32[512]{0:T(512)S(1)} %fusion.16, bf16[1,2,4,512,128]{4,3,2,1,0:T(8,128)(2,1)S(1)} %bitcast.66, bf16[128,4,128]{2,0,1:T(8,128)(2,1)S(1)} %copy.18), kind=kOutput, calls=%fused_computation.5 | convolution fusion | flops 136380416 | bytes 1312772 | tf_op jit(solution)/shard_map/hck,hkd->chd/dot_general | solution.py:28
  40.9 4.9 %collective-permute-done.1 = bf16[128,512]{0,1:T(8,128)(2,1)S(1)} collective-permute-done((bf16[128,512]{0,1:T(8,128)(2,1)S(1)}, bf16[128,512]{0,1:T(8,128)(2,1)S(1)}, u32[]{:S(2)}, u32[]{:S(2)}) %collective-permute-start.1) | collective-permute-done | bytes 131104 | tf_op jit(solution)/shard_map/ppermute | solution.py:89
  45.8 0.2 convert_reduce_fusion
  46.0 0.2 fusion.1
  46.2 0.0 collective-permute-done.2
  46.2 0.0 copy-done.2
  46.2 0.2 multiply_convert_fusion
  46.4 0.9 %copy.23 = bf16[1,128,1024]{2,1,0:T(8,128)(2,1)} copy(bf16[1,128,1024]{1,2,0:T(8,128)(2,1)S(1)} %multiply_convert_fusion) | data formatting | bytes 524288 | tf_op jit(solution)/shard_map/convert_element_type | solution.py:45
  (3 shorter events, 0.0 us)
Async XLA Ops:
  0.0 33.5 %collective-permute-start = (bf16[128,1024]{1,0:T(8,128)(2,1)}, bf16[128,1024]{1,0:T(8,128)(2,1)}, u32[]{:S(2)}, u32[]{:S(2)}) collective-permute-start(bf16[128,1024]{1,0:T(8,128)(2,1)} %bitcast.69), channel_id=1, source_target_pairs={{0,4},{4,0},{1,5},{5,1},{2,6},{6,2},{3,7},{7,3},{8,12},{12,8},{9,1... | collective-permute-start | bytes 786440 | tf_op jit(solution)/shard_map/ppermute | solution.py:84
  17.7 21.5 %all-to-all-start = ((bf16[8,2,4,64,128]{4,3,2,1,0:T(8,128)(2,1)}), bf16[8,2,4,64,128]{4,3,2,1,0:T(8,128)(2,1)S(1)}, u32[]{:S(2)}, u32[]{:S(2)}) async-start(bf16[8,2,4,64,128]{4,3,2,1,0:T(8,128)(2,1)} %bitcast.5), calls=%async_computation | async-start | bytes 2097152 | tf_op jit(solution)/shard_map/all_to_all | solution.py:67
  21.3 4.8 %copy-start.1 = (bf16[1,128,1024]{2,1,0:T(8,128)(2,1)S(1)}, bf16[1,128,1024]{2,1,0:T(8,128)(2,1)}, u32[]{:S(2)}) copy-start(bf16[1,128,1024]{2,1,0:T(8,128)(2,1)} %param.6) | copy-start | bytes 786436
  26.1 3.4 %copy-start.3 = (s32[4]{0:T(128)S(1)}, s32[4]{0:T(128)}, u32[]{:S(2)}) copy-start(s32[4]{0:T(128)} %param.11) | copy-start | bytes 52
  35.2 0.8 %copy-start = (f32[2,128,512]{1,2,0:T(8,128)}, f32[2,128,512]{1,2,0:T(8,128)S(1)}, u32[]{:S(2)}) copy-start(f32[2,128,512]{1,2,0:T(8,128)S(1)} %convolution_bitcast_fusion) | copy-start | bytes 1572868
  37.2 9.0 %collective-permute-start.2 = (bf16[128,512]{0,1:T(8,128)(2,1)S(1)}, bf16[128,512]{0,1:T(8,128)(2,1)S(1)}, u32[]{:S(2)}, u32[]{:S(2)}) collective-permute-start(bf16[128,512]{0,1:T(8,128)(2,1)S(1)} %multiply_convert_fusion.1), channel_id=1, source_target_pairs={{0,4},{4,0},{1,5},{5,1},{2,6},{6,2},{3,7},{7,3},{8,12},{12,8},{9,1... | collective-permute-start | bytes 393224 | tf_op jit(solution)/shard_map/ppermute | solution.py:87
  40.0 6.2 %copy-start.2 = (f32[1024]{0:T(1024)S(1)}, f32[1024]{0:T(1024)}, u32[]{:S(2)}) copy-start(f32[1024]{0:T(1024)} %param.9) | copy-start | bytes 12292
  40.0 5.8 %collective-permute-start.1 = (bf16[128,512]{0,1:T(8,128)(2,1)S(1)}, bf16[128,512]{0,1:T(8,128)(2,1)S(1)}, u32[]{:S(2)}, u32[]{:S(2)}) collective-permute-start(bf16[128,512]{0,1:T(8,128)(2,1)S(1)} %bitcast.71), channel_id=1, source_target_pairs={{0,4},{4,0},{1,5},{5,1},{2,6},{6,2},{3,7},{7,3},{8,12},{12,8},{9,1... | collective-permute-start | bytes 393224 | tf_op jit(solution)/shard_map/ppermute | solution.py:89

commit v12 on v7

--- a/solution.py
+++ b/solution.py
@@ -73,17 +73,18 @@
     def project(feats):
         proj = jnp.einsum("cd,dkh->kch", feats, proj_weight, preferred_element_type=jnp.float32)
         query = proj[0].astype(jnp.bfloat16).reshape(-1, local_heads, HEAD_SIZE)
-        gate = jax.nn.silu(proj[1]).astype(jnp.bfloat16)
-        return jnp.transpose(query, (1, 0, 2)), gate
+        return jnp.transpose(query, (1, 0, 2)), proj[1]
 
     if n_blk == 2:
         swap = [(0, 1), (1, 0)]
         peer = lax.ppermute(mine, "blk", swap)
         query_own, gate_own = project(mine)
         query_peer, gate_peer = project(peer)
-        gate_back = lax.ppermute(gate_peer, "blk", swap)
+        gate_back = lax.ppermute(jax.nn.silu(gate_peer).astype(jnp.bfloat16), "blk", swap)
         sent = attend(query_peer, keys, values, count).astype(jnp.bfloat16)
         back = lax.ppermute(sent, "blk", swap)
+        query_own, gate_own, _ = lax.optimization_barrier((query_own, gate_own, sent))
+        gate_own = jax.nn.silu(gate_own).astype(jnp.bfloat16)
         kept = attend(query_own, keys, values, count).astype(jnp.bfloat16)
         first = blk == 0
         attended = jnp.where(first, jnp.concatenate([kept, back], axis=1),
@@ -94,6 +95,7 @@
 
     feats = lax.all_gather(mine, "blk", axis=0, tiled=True)
     query, gate = project(feats)
+    gate = jax.nn.silu(gate).astype(jnp.bfloat16)
     attended = attend(query, keys, values, count).astype(jnp.bfloat16)
     both = jnp.stack([attended, gate]).reshape(2, n_blk, rows, half)
     own = lax.all_to_all(both, "blk", split_axis=1, concat_axis=3, tiled=True)

time: 41 us -> 41 us (level)
  local copies, waits for them, and re-layouts: 13.5 us -> 14.5 us
  other arithmetic: 5.87 us -> 4.92 us
    convert_element_type x2 -> x1, other arithmetic: 2.06 us -> 1.03 us  [per_device(): jax.nn.silu(gate_peer).astype(jnp.bfloat16)]
    squeeze x0 -> x1, local copies, waits for them, and re-layouts: none -> 0.97 us  [project(): return (jnp.transpose(query, (1, 0, 2)), proj[1])]
  transfers between devices with their start and end apart: 4 -> 4, of which waited for: 1 -> 1; matrix products, arithmetic and copies ran while one was open for 54% -> 55% of each run, Pallas kernels for 0% -> 0%
where the time goes in v12:
time: 41 us; the launch traced here: 40.5 us
  local copies, waits for them, and re-layouts  14.5 us (35%)
  starting transfers between devices  9.37 us (23%)
  other arithmetic  4.92 us (12%)
  matrix products  4.61 us (11%)
  waiting for transfers between devices  4.31 us (11%)
  between operations  2.78 us (7%)
    unnamed x13, local copies, waits for them, and re-layouts  5.59 us
    ppermute x1, waiting for transfers between devices, per_device(): back = lax.ppermute(sent, 'blk', swap)  4.3 us
    all_to_all x1, starting transfers between devices, per_device(): lax.all_to_all(ordered, ('blk', 'store'), split_axis=0, concat_axis=3, ti...  4.24 us
    gather x2, local copies, waits for them, and re-layouts, per_device(): jnp.take(kv_store, users, axis=0)  3.37 us
    dot_general x2, matrix products, project(): jnp.einsum('cd,dkh->kch', feats, proj_weight, preferred_element_type=jnp....  3.16 us
    ppermute x1, starting transfers between devices, per_device(): peer = lax.ppermute(mine, 'blk', swap)  2.97 us
    ppermute x1, starting transfers between devices, per_device(): lax.ppermute(jax.nn.silu(gate_peer).astype(jnp.bfloat16), 'blk', swap)  1.96 us
    select_n x2, other arithmetic, per_device(): jnp.take(kv_store, users, axis=0)  1.93 us
  transfers between devices with their start and end apart: 4, of which 1 were waited for; matrix products, arithmetic and copies ran while one was open for 55% of the time, Pallas kernels for 0%

profile of v12, /device:TPU:0, one launch (start us, length us, event | category | flops | bytes accessed | tf_op | source)
XLA Modules:
  0.0 40.5 jit_solution(8194489412673169876)
XLA Ops:
  0.0 0.0 copy-start
  0.0 3.0 %collective-permute-start = (bf16[128,1024]{1,0:T(8,128)(2,1)}, bf16[128,1024]{1,0:T(8,128)(2,1)}, u32[]{:S(2)}, u32[]{:S(2)}) collective-permute-start(bf16[128,1024]{1,0:T(8,128)(2,1)} %bitcast.66), channel_id=1, source_target_pairs={{0,4},{4,0},{1,5},{5,1},{2,6},{6,2},{3,7},{7,3},{8,12},{12,8},{9,1... | collective-permute-start | bytes 786440 | tf_op jit(solution)/shard_map/ppermute | solution.py:80
  3.0 0.7 %compare_and_fusion = pred[4]{0:T(512)(128)(4,1)S(1)} fusion(s32[4]{0:T(128)} %param.10), kind=kLoop, calls=%fused_computation.42 | loop fusion | flops 24 | bytes 20 | tf_op jit(solution)/shard_map/jit(_take)/and | solution.py:58
  3.6 0.7 %compare_select_fusion = s32[4]{0:T(128)S(1)} fusion(s32[4]{0:T(128)} %param.10), kind=kLoop, calls=%fused_computation.39 | loop fusion | flops 12 | bytes 32 | tf_op jit(solution)/shard_map/jit(_take)/jit(_where)/select_n | solution.py:58
  4.3 0.0 copy-done
  4.3 2.7 %gather_fusion = bf16[4,64,2,1024]{3,2,1,0:T(2,128)(2,1)S(1)} fusion(bf16[4,64,2,1024]{3,2,1,0:T(2,128)(2,1)S(1)} %copy-done, s32[1024]{0:T(1024)S(1)} %pad_clamp_fusion), kind=kCustom, calls=%fused_computation | custom fusion | bytes 2097168 | tf_op jit(solution)/shard_map/jit(_take)/gather | solution.py:58
  7.0 0.7 %gather.7 = bf16[4,64,2,2,4,128]{5,4,3,2,1,0:T(4,128)(2,1)S(1)} reshape(bf16[4,64,2,1024]{3,2,1,0:T(2,128)(2,1)S(1)} %gather_fusion) | data formatting | bytes 2097152 | tf_op jit(solution)/shard_map/jit(_take)/gather | solution.py:58
  7.7 1.3 %copy_select_fusion = bf16[4,64,2,2,4,128]{5,1,4,2,0,3:T(8,128)(2,1)} fusion(bf16[4,64,2,2,4,128]{5,4,3,2,1,0:T(4,128)(2,1)S(1)} %gather.7, pred[4]{0:T(512)(128)(4,1)S(1)} %compare_and_fusion), kind=kLoop, calls=%fused_computation.7 | loop fusion | flops 524288 | bytes 2097156 | tf_op jit(solution)/shard_map/jit(_take)/select_n | solution.py:58
  9.0 4.2 %all-to-all-start = ((bf16[8,2,4,64,128]{4,3,2,1,0:T(8,128)(2,1)}), bf16[8,2,4,64,128]{4,3,2,1,0:T(8,128)(2,1)}, u32[]{:S(2)}, u32[]{:S(2)}) async-start(bf16[8,2,4,64,128]{4,3,2,1,0:T(8,128)(2,1)} %bitcast.1), calls=%async_computation | async-start | bytes 2097152 | tf_op jit(solution)/shard_map/all_to_all | solution.py:64
  13.2 0.0 copy-start.2
  13.2 4.8 %copy.17 = bf16[1024,2,512]{0,2,1:T(8,128)(2,1)S(1)} copy(bf16[1024,2,512]{2,1,0:T(2,128)(2,1)} %param.8) | data formatting | bytes 4194304 | tf_op args[2]
  18.0 0.0 copy-done.2
  18.0 0.0 copy-start.4
  18.0 0.0 copy-start.5
  18.0 1.5 %convolution_bitcast_fusion.1 = f32[2,128,512]{1,2,0:T(8,128)} fusion(bf16[1024,2,512]{0,2,1:T(8,128)(2,1)S(1)} %copy.17, bf16[1,128,1024]{2,1,0:T(8,128)(2,1)S(1)} %copy-done.2), kind=kOutput, calls=%fused_computation.4 | convolution fusion | flops 268435456 | bytes 2883584 | tf_op jit(solution)/shard_map/cd,dkh->kch/dot_general | solution.py:74
  19.5 0.0 copy-done.4
  19.5 0.6 %dynamic_slice.7 = s32[1]{0:T(128)} dynamic-slice(s32[4]{0:T(128)S(1)} %copy-done.4, s32[]{:T(128)S(6)} %select_n.50), dynamic_slice_sizes={1} | dynamic-slice | bytes 12 | tf_op jit(solution)/shard_map/jit(dynamic_index_in_dim)/dynamic_slice | solution.py:52
  22.1 0.0 copy-done.5
  22.1 0.6 %dynamic_slice.8 = s32[1]{0:T(128)} dynamic-slice(s32[4]{0:T(128)S(1)} %copy-done.5, s32[]{:T(128)S(6)} %select_n.51), dynamic_slice_sizes={1} | dynamic-slice | bytes 12 | tf_op jit(solution)/shard_map/jit(dynamic_index_in_dim)/dynamic_slice | solution.py:53
  22.7 0.6 %fusion.15 = f32[512]{0:T(512)S(1)} fusion(s32[]{:T(128)} %bitcast.18), kind=kLoop, calls=%fused_computation.41 | loop fusion | flops 1024 | bytes 2052 | tf_op jit(solution)/shard_map/convert_element_type | solution.py:26
  24.0 1.0 %slice.49 = bf16[1,128,512]{1,2,0:T(8,128)(2,1)S(1)} slice(f32[2,128,512]{1,2,0:T(8,128)} %convolution_bitcast_fusion.1), slice={[0:1], [0:128], [0:512]} | slice | bytes 262144 | tf_op jit(solution)/shard_map/slice | solution.py:75
  24.9 0.1 copy.18
  25.1 1.0 %slice_bitcast_fusion.9 = f32[128,512]{0,1:T(8,128)S(1)} fusion(f32[2,128,512]{1,2,0:T(8,128)} %convolution_bitcast_fusion.1), kind=kLoop, calls=%fused_computation.27 | loop fusion | bytes 524288 | tf_op jit(solution)/shard_map/squeeze | solution.py:76
  26.0 0.0 collective-permute-done
  26.1 1.7 %convolution_bitcast_fusion = f32[2,128,512]{1,2,0:T(8,128)S(1)} fusion(bf16[1024,2,512]{0,2,1:T(8,128)(2,1)S(1)} %copy.17, bf16[128,1024]{1,0:T(8,128)(2,1)} %collective-permute-done), kind=kOutput, calls=%fused_computation.3 | convolution fusion | flops 268435456 | bytes 2883584 | tf_op jit(solution)/shard_map/cd,dkh->kch/dot_general | solution.py:74
  27.7 0.0 copy-start.1
  27.7 0.8 %copy-done.1 = f32[2,128,512]{1,2,0:T(8,128)} copy-done((f32[2,128,512]{1,2,0:T(8,128)}, f32[2,128,512]{1,2,0:T(8,128)S(1)}, u32[]{:S(2)}) %copy-start.1) | copy-done | bytes 524312
  28.5 0.1 copy.20
  28.7 1.0 %multiply_convert_fusion.1 = bf16[128,512]{0,1:T(8,128)(2,1)S(1)} fusion(f32[2,128,512]{1,2,0:T(8,128)} %copy-done.1), kind=kLoop, calls=%fused_computation.34 | loop fusion | flops 327680 | bytes 393216 | tf_op jit(solution)/shard_map/convert_element_type | solution.py:83
  29.7 2.0 %collective-permute-start.2 = (bf16[128,512]{0,1:T(8,128)(2,1)S(1)}, bf16[128,512]{0,1:T(8,128)(2,1)S(1)}, u32[]{:S(2)}, u32[]{:S(2)}) collective-permute-start(bf16[128,512]{0,1:T(8,128)(2,1)S(1)} %multiply_convert_fusion.1), channel_id=1, source_target_pairs={{0,4},{4,0},{1,5},{5,1},{2,6},{6,2},{3,7},{7,3},{8,12},{12,8},{9,1... | collective-permute-start | bytes 393224 | tf_op jit(solution)/shard_map/ppermute | solution.py:83
  31.7 0.0 all-to-all-done
  31.7 1.3 %copy.16 = bf16[1,2,4,8,64,128]{5,4,3,2,1,0:T(8,128)(2,1)S(1)} copy(bf16[1,2,4,8,64,128]{5,4,2,1,3,0:T(8,128)(2,1)} %bitcast.3) | data formatting | bytes 2097152 | tf_op jit(solution)/shard_map/all_to_all | solution.py:64
  33.0 0.7 %convolution_convert_fusion.1 = bf16[4,128,128]{2,1,0:T(8,128)(2,1)S(1)} fusion(f32[]{:T(128)S(6)} %convert_element_type.96, f32[512]{0:T(512)S(1)} %fusion.15, bf16[1,2,4,512,128]{4,3,2,1,0:T(8,128)(2,1)S(1)} %bitcast.62, bf16[128,4,128]{2,0,1:T(8,128)(2,1)S(1)} %copy.20), kind=kOutput, calls=%fused_computation.6 | convolution fusion | flops 136380416 | bytes 1312772 | tf_op jit(solution)/shard_map/hck,hkd->chd/dot_general | solution.py:28
  33.7 0.2 collective-permute-start.1
  33.9 0.0 copy-start.3
  33.9 0.7 %convolution_convert_fusion = bf16[4,128,128]{2,1,0:T(8,128)(2,1)S(1)} fusion(bf16[4,128,128]{2,1,0:T(8,128)(2,1)S(1)} %bitcast.67, f32[]{:T(128)S(6)} %convert_element_type.96, f32[512]{0:T(512)S(1)} %fusion.15, bf16[1,2,4,512,128]{4,3,2,1,0:T(8,128)(2,1)S(1)} %bitcast.63), kind=kOutput, calls=%fused_computation.5 | convolution fusion | flops 136380416 | bytes 1312772 | tf_op jit(solution)/shard_map/hck,hkd->chd/dot_general | solution.py:28
  34.7 0.1 fusion.14
  34.7 4.3 %collective-permute-done.1 = bf16[128,512]{0,1:T(8,128)(2,1)S(1)} collective-permute-done((bf16[128,512]{0,1:T(8,128)(2,1)S(1)}, bf16[128,512]{0,1:T(8,128)(2,1)S(1)}, u32[]{:S(2)}, u32[]{:S(2)}) %collective-permute-start.1) | collective-permute-done | bytes 131104 | tf_op jit(solution)/shard_map/ppermute | solution.py:85
  39.1 0.2 convert_reduce_fusion
  39.2 0.2 fusion.1
  39.4 0.0 collective-permute-done.2
  39.4 0.0 copy-done.3
  39.4 0.2 multiply_convert_fusion
  39.6 0.9 %copy.23 = bf16[1,128,1024]{2,1,0:T(8,128)(2,1)} copy(bf16[1,128,1024]{1,2,0:T(8,128)(2,1)S(1)} %multiply_convert_fusion) | data formatting | bytes 524288 | tf_op jit(solution)/shard_map/convert_element_type | solution.py:45
  (4 shorter events, 0.0 us)
Async XLA Ops:
  0.0 4.3 %copy-start = (bf16[4,64,2,1024]{3,2,1,0:T(2,128)(2,1)S(1)}, bf16[4,64,2,1024]{3,2,1,0:T(2,128)(2,1)}, u32[]{:S(2)}) copy-start(bf16[4,64,2,1024]{3,2,1,0:T(2,128)(2,1)} %param.7) | copy-start | bytes 3145732
  0.0 26.0 %collective-permute-start = (bf16[128,1024]{1,0:T(8,128)(2,1)}, bf16[128,1024]{1,0:T(8,128)(2,1)}, u32[]{:S(2)}, u32[]{:S(2)}) collective-permute-start(bf16[128,1024]{1,0:T(8,128)(2,1)} %bitcast.66), channel_id=1, source_target_pairs={{0,4},{4,0},{1,5},{5,1},{2,6},{6,2},{3,7},{7,3},{8,12},{12,8},{9,1... | collective-permute-start | bytes 786440 | tf_op jit(solution)/shard_map/ppermute | solution.py:80
  9.0 22.7 %all-to-all-start = ((bf16[8,2,4,64,128]{4,3,2,1,0:T(8,128)(2,1)}), bf16[8,2,4,64,128]{4,3,2,1,0:T(8,128)(2,1)}, u32[]{:S(2)}, u32[]{:S(2)}) async-start(bf16[8,2,4,64,128]{4,3,2,1,0:T(8,128)(2,1)} %bitcast.1), calls=%async_computation | async-start | bytes 2097152 | tf_op jit(solution)/shard_map/all_to_all | solution.py:64
  13.2 4.8 %copy-start.2 = (bf16[1,128,1024]{2,1,0:T(8,128)(2,1)S(1)}, bf16[1,128,1024]{2,1,0:T(8,128)(2,1)}, u32[]{:S(2)}) copy-start(bf16[1,128,1024]{2,1,0:T(8,128)(2,1)} %param.6) | copy-start | bytes 786436
  18.0 1.5 %copy-start.4 = (s32[4]{0:T(128)S(1)}, s32[4]{0:T(128)}, u32[]{:S(2)}) copy-start(s32[4]{0:T(128)} %param.10) | copy-start | bytes 52
  18.0 4.0 %copy-start.5 = (s32[4]{0:T(128)S(1)}, s32[4]{0:T(128)}, u32[]{:S(2)}) copy-start(s32[4]{0:T(128)} %param.11) | copy-start | bytes 52
  27.7 0.8 %copy-start.1 = (f32[2,128,512]{1,2,0:T(8,128)}, f32[2,128,512]{1,2,0:T(8,128)S(1)}, u32[]{:S(2)}) copy-start(f32[2,128,512]{1,2,0:T(8,128)S(1)} %convolution_bitcast_fusion) | copy-start | bytes 1572868
  29.7 9.7 %collective-permute-start.2 = (bf16[128,512]{0,1:T(8,128)(2,1)S(1)}, bf16[128,512]{0,1:T(8,128)(2,1)S(1)}, u32[]{:S(2)}, u32[]{:S(2)}) collective-permute-start(bf16[128,512]{0,1:T(8,128)(2,1)S(1)} %multiply_convert_fusion.1), channel_id=1, source_target_pairs={{0,4},{4,0},{1,5},{5,1},{2,6},{6,2},{3,7},{7,3},{8,12},{12,8},{9,1... | collective-permute-start | bytes 393224 | tf_op jit(solution)/shard_map/ppermute | solution.py:83
  33.7 5.3 %collective-permute-start.1 = (bf16[128,512]{0,1:T(8,128)(2,1)S(1)}, bf16[128,512]{0,1:T(8,128)(2,1)S(1)}, u32[]{:S(2)}, u32[]{:S(2)}) collective-permute-start(bf16[128,512]{0,1:T(8,128)(2,1)S(1)} %bitcast.69), channel_id=1, source_target_pairs={{0,4},{4,0},{1,5},{5,1},{2,6},{6,2},{3,7},{7,3},{8,12},{12,8},{9,1... | collective-permute-start | bytes 393224 | tf_op jit(solution)/shard_map/ppermute | solution.py:85
  33.9 5.5 %copy-start.3 = (f32[1024]{0:T(1024)S(1)}, f32[1024]{0:T(1024)}, u32[]{:S(2)}) copy-start(f32[1024]{0:T(1024)} %param.9) | copy-start | bytes 12292

commit v13 on v7

--- a/solution.py
+++ b/solution.py
@@ -55,7 +55,7 @@
     local_heads = half // HEAD_SIZE
 
     n_users, n_pos = kv_store.shape[0], kv_store.shape[1]
-    ordered = jnp.take(kv_store, users, axis=0).reshape(
+    ordered = kv_store.at[users].get(mode="promise_in_bounds", unique_indices=True).reshape(
         n_users, n_pos, 2, n_blk, local_heads, HEAD_SIZE
     )
     ordered = jnp.transpose(ordered, (3, 0, 2, 4, 1, 5)).reshape(

time: 41 us -> 40.4 us (0.985)
  other arithmetic: 5.87 us -> 3.94 us
  local copies, waits for them, and re-layouts: 13.5 us -> 14.8 us
    reshape x0 -> x2, local copies, waits for them, and re-layouts: none -> 2.02 us  [per_device(): kv_store.at[users].get(mode='promise_in_bounds', unique_indices=True)]
    select_n x2 -> x1, other arithmetic: 1.93 us -> 0.66 us  [per_device(): kv_store.at[users].get(mode='promise_in_bounds', unique_indices=True)]
    gather x2 -> x1, local copies, waits for them, and re-layouts: 3.37 us -> 2.66 us  [per_device(): kv_store.at[users].get(mode='promise_in_bounds', unique_indices=True)]
    and x1 -> x0, other arithmetic: 0.66 us -> none  [per_device(): jnp.take(kv_store, users, axis=0)]
where the time goes in v13:
time: 40.4 us; the launch traced here: 39.9 us
  local copies, waits for them, and re-layouts  14.8 us (37%)
  starting transfers between devices  9.37 us (23%)
  matrix products  4.61 us (11%)
  waiting for transfers between devices  4.4 us (11%)
  other arithmetic  3.94 us (10%)
  between operations  2.78 us (7%)
    unnamed x13, local copies, waits for them, and re-layouts  5.59 us
    ppermute x1, waiting for transfers between devices, per_device(): back = lax.ppermute(sent, 'blk', swap)  4.4 us
    all_to_all x1, starting transfers between devices, per_device(): lax.all_to_all(ordered, ('blk', 'store'), split_axis=0, concat_axis=3, ti...  4.24 us
    dot_general x2, matrix products, project(): jnp.einsum('cd,dkh->kch', feats, proj_weight, preferred_element_type=jnp....  3.16 us
    ppermute x1, starting transfers between devices, per_device(): peer = lax.ppermute(mine, 'blk', swap)  2.97 us
    gather x1, local copies, waits for them, and re-layouts, per_device(): kv_store.at[users].get(mode='promise_in_bounds', unique_indices=True)  2.66 us
    convert_element_type x2, other arithmetic, project(): gate = jax.nn.silu(proj[1]).astype(jnp.bfloat16)  2.06 us
    reshape x2, local copies, waits for them, and re-layouts, per_device(): kv_store.at[users].get(mode='promise_in_bounds', unique_indices=True)  2.02 us
  transfers between devices with their start and end apart: 4, of which 1 were waited for; matrix products, arithmetic and copies ran while one was open for 54% of the time, Pallas kernels for 0%

profile of v13, /device:TPU:0, one launch (start us, length us, event | category | flops | bytes accessed | tf_op | source)
XLA Modules:
  0.0 39.9 jit_solution(4784147675228688799)
XLA Ops:
  0.0 0.0 copy-start
  0.0 3.0 %collective-permute-start = (bf16[128,1024]{1,0:T(8,128)(2,1)}, bf16[128,1024]{1,0:T(8,128)(2,1)}, u32[]{:S(2)}, u32[]{:S(2)}) collective-permute-start(bf16[128,1024]{1,0:T(8,128)(2,1)} %bitcast.64), channel_id=1, source_target_pairs={{0,4},{4,0},{1,5},{5,1},{2,6},{6,2},{3,7},{7,3},{8,12},{12,8},{9,1... | collective-permute-start | bytes 786440 | tf_op jit(solution)/shard_map/ppermute | solution.py:81
  3.0 0.7 %compare_select_fusion = s32[4]{0:T(128)S(1)} fusion(s32[4]{0:T(128)} %param.10), kind=kLoop, calls=%fused_computation.37 | loop fusion | flops 12 | bytes 32 | tf_op jit(solution)/shard_map/select_n | solution.py:58
  3.6 0.0 copy-done
  3.6 2.7 %gather_fusion = bf16[4,64,2,1024]{3,2,1,0:T(2,128)(2,1)S(1)} fusion(bf16[4,64,2,1024]{3,2,1,0:T(2,128)(2,1)S(1)} %copy-done, s32[1024]{0:T(1024)S(1)} %pad_clamp_fusion), kind=kCustom, calls=%fused_computation | custom fusion | bytes 2097168 | tf_op jit(solution)/shard_map/gather | solution.py:58
  6.3 0.7 %reshape.216 = bf16[4,64,2,2,4,128]{5,4,3,2,1,0:T(4,128)(2,1)S(1)} reshape(bf16[4,64,2,1024]{3,2,1,0:T(2,128)(2,1)S(1)} %gather_fusion) | data formatting | bytes 2097152 | tf_op jit(solution)/shard_map/reshape | solution.py:58
  7.0 1.3 %copy.15 = bf16[4,64,2,2,4,128]{5,1,4,2,0,3:T(8,128)(2,1)} copy(bf16[4,64,2,2,4,128]{5,4,3,2,1,0:T(4,128)(2,1)S(1)} %reshape.216) | data formatting | bytes 2097152 | tf_op jit(solution)/shard_map/reshape | solution.py:58
  8.3 4.2 %all-to-all-start = ((bf16[8,2,4,64,128]{4,3,2,1,0:T(8,128)(2,1)}), bf16[8,2,4,64,128]{4,3,2,1,0:T(8,128)(2,1)}, u32[]{:S(2)}, u32[]{:S(2)}) async-start(bf16[8,2,4,64,128]{4,3,2,1,0:T(8,128)(2,1)} %bitcast.1), calls=%async_computation | async-start | bytes 2097152 | tf_op jit(solution)/shard_map/all_to_all | solution.py:64
  12.6 0.0 copy-start.2
  12.6 4.8 %copy.17 = bf16[1024,2,512]{0,2,1:T(8,128)(2,1)S(1)} copy(bf16[1024,2,512]{2,1,0:T(2,128)(2,1)} %param.8) | data formatting | bytes 4194304 | tf_op args[2]
  17.4 0.0 copy-done.2
  17.4 0.0 copy-start.4
  17.4 0.0 copy-start.5
  17.4 1.5 %convolution_bitcast_fusion.1 = f32[2,128,512]{1,2,0:T(8,128)} fusion(bf16[1024,2,512]{0,2,1:T(8,128)(2,1)S(1)} %copy.17, bf16[1,128,1024]{2,1,0:T(8,128)(2,1)S(1)} %copy-done.2), kind=kOutput, calls=%fused_computation.4 | convolution fusion | flops 268435456 | bytes 2883584 | tf_op jit(solution)/shard_map/cd,dkh->kch/dot_general | solution.py:74
  18.9 0.0 copy-done.4
  18.9 0.6 %dynamic_slice.7 = s32[1]{0:T(128)} dynamic-slice(s32[4]{0:T(128)S(1)} %copy-done.4, s32[]{:T(128)S(6)} %select_n.42), dynamic_slice_sizes={1} | dynamic-slice | bytes 12 | tf_op jit(solution)/shard_map/jit(dynamic_index_in_dim)/dynamic_slice | solution.py:52
  21.4 0.0 copy-done.5
  21.4 0.6 %dynamic_slice.8 = s32[1]{0:T(128)} dynamic-slice(s32[4]{0:T(128)S(1)} %copy-done.5, s32[]{:T(128)S(6)} %select_n.43), dynamic_slice_sizes={1} | dynamic-slice | bytes 12 | tf_op jit(solution)/shard_map/jit(dynamic_index_in_dim)/dynamic_slice | solution.py:53
  22.0 0.6 %fusion.16 = f32[512]{0:T(512)S(1)} fusion(s32[]{:T(128)} %bitcast.13), kind=kLoop, calls=%fused_computation.39 | loop fusion | flops 1024 | bytes 2052 | tf_op jit(solution)/shard_map/convert_element_type | solution.py:26
  23.3 1.0 %slice.49 = bf16[1,128,512]{1,2,0:T(8,128)(2,1)S(1)} slice(f32[2,128,512]{1,2,0:T(8,128)} %convolution_bitcast_fusion.1), slice={[0:1], [0:128], [0:512]} | slice | bytes 262144 | tf_op jit(solution)/shard_map/slice | solution.py:75
  24.3 0.1 copy.18
  24.4 1.0 %multiply_convert_fusion.2 = bf16[1,128,512]{1,2,0:T(8,128)(2,1)S(1)} fusion(f32[2,128,512]{1,2,0:T(8,128)} %convolution_bitcast_fusion.1), kind=kLoop, calls=%fused_computation.33 | loop fusion | flops 327680 | bytes 393216 | tf_op jit(solution)/shard_map/convert_element_type | solution.py:76
  25.5 0.0 collective-permute-done
  25.5 1.7 %convolution_bitcast_fusion = f32[2,128,512]{1,2,0:T(8,128)S(1)} fusion(bf16[1024,2,512]{0,2,1:T(8,128)(2,1)S(1)} %copy.17, bf16[128,1024]{1,0:T(8,128)(2,1)} %collective-permute-done), kind=kOutput, calls=%fused_computation.3 | convolution fusion | flops 268435456 | bytes 2883584 | tf_op jit(solution)/shard_map/cd,dkh->kch/dot_general | solution.py:74
  27.2 0.0 copy-start.1
  27.2 0.8 %copy-done.1 = f32[2,128,512]{1,2,0:T(8,128)} copy-done((f32[2,128,512]{1,2,0:T(8,128)}, f32[2,128,512]{1,2,0:T(8,128)S(1)}, u32[]{:S(2)}) %copy-start.1) | copy-done | bytes 524312
  28.0 0.1 copy.21
  28.1 1.0 %multiply_convert_fusion.1 = bf16[128,512]{0,1:T(8,128)(2,1)S(1)} fusion(f32[2,128,512]{1,2,0:T(8,128)} %copy-done.1), kind=kLoop, calls=%fused_computation.32 | loop fusion | flops 327680 | bytes 393216 | tf_op jit(solution)/shard_map/convert_element_type | solution.py:76
  29.1 2.0 %collective-permute-start.2 = (bf16[128,512]{0,1:T(8,128)(2,1)S(1)}, bf16[128,512]{0,1:T(8,128)(2,1)S(1)}, u32[]{:S(2)}, u32[]{:S(2)}) collective-permute-start(bf16[128,512]{0,1:T(8,128)(2,1)S(1)} %multiply_convert_fusion.1), channel_id=1, source_target_pairs={{0,4},{4,0},{1,5},{5,1},{2,6},{6,2},{3,7},{7,3},{8,12},{12,8},{9,1... | collective-permute-start | bytes 393224 | tf_op jit(solution)/shard_map/ppermute | solution.py:84
  31.1 0.0 all-to-all-done
  31.1 1.3 %copy.16 = bf16[1,2,4,8,64,128]{5,4,3,2,1,0:T(8,128)(2,1)S(1)} copy(bf16[1,2,4,8,64,128]{5,4,2,1,3,0:T(8,128)(2,1)} %bitcast.3) | data formatting | bytes 2097152 | tf_op jit(solution)/shard_map/all_to_all | solution.py:64
  32.4 0.7 %convolution_convert_fusion = bf16[4,128,128]{2,1,0:T(8,128)(2,1)S(1)} fusion(f32[]{:T(128)S(6)} %convert_element_type.96, f32[512]{0:T(512)S(1)} %fusion.16, bf16[1,2,4,512,128]{4,3,2,1,0:T(8,128)(2,1)S(1)} %bitcast.60, bf16[128,4,128]{2,0,1:T(8,128)(2,1)S(1)} %copy.21), kind=kOutput, calls=%fused_computation.5 | convolution fusion | flops 136380416 | bytes 1312772 | tf_op jit(solution)/shard_map/hck,hkd->chd/dot_general | solution.py:28
  33.2 0.0 copy-start.3
  33.2 0.2 collective-permute-start.1
  33.4 0.7 %convolution_convert_fusion.1 = bf16[4,128,128]{2,1,0:T(8,128)(2,1)S(1)} fusion(f32[]{:T(128)S(6)} %convert_element_type.96, f32[512]{0:T(512)S(1)} %fusion.16, bf16[1,2,4,512,128]{4,3,2,1,0:T(8,128)(2,1)S(1)} %bitcast.61, bf16[128,4,128]{2,0,1:T(8,128)(2,1)S(1)} %copy.18), kind=kOutput, calls=%fused_computation.6 | convolution fusion | flops 136380416 | bytes 1312772 | tf_op jit(solution)/shard_map/hck,hkd->chd/dot_general | solution.py:28
  34.1 4.4 %collective-permute-done.1 = bf16[128,512]{0,1:T(8,128)(2,1)S(1)} collective-permute-done((bf16[128,512]{0,1:T(8,128)(2,1)S(1)}, bf16[128,512]{0,1:T(8,128)(2,1)S(1)}, u32[]{:S(2)}, u32[]{:S(2)}) %collective-permute-start.1) | collective-permute-done | bytes 131104 | tf_op jit(solution)/shard_map/ppermute | solution.py:86
  38.5 0.2 convert_reduce_fusion
  38.7 0.2 fusion.1
  38.8 0.0 collective-permute-done.2
  38.9 0.0 copy-done.3
  38.9 0.2 multiply_convert_fusion
  39.1 0.9 %copy.23 = bf16[1,128,1024]{2,1,0:T(8,128)(2,1)} copy(bf16[1,128,1024]{1,2,0:T(8,128)(2,1)S(1)} %multiply_convert_fusion) | data formatting | bytes 524288 | tf_op jit(solution)/shard_map/convert_element_type | solution.py:45
  (4 shorter events, 0.0 us)
Async XLA Ops:
  0.0 3.6 %copy-start = (bf16[4,64,2,1024]{3,2,1,0:T(2,128)(2,1)S(1)}, bf16[4,64,2,1024]{3,2,1,0:T(2,128)(2,1)}, u32[]{:S(2)}) copy-start(bf16[4,64,2,1024]{3,2,1,0:T(2,128)(2,1)} %param.7) | copy-start | bytes 3145732
  0.0 25.5 %collective-permute-start = (bf16[128,1024]{1,0:T(8,128)(2,1)}, bf16[128,1024]{1,0:T(8,128)(2,1)}, u32[]{:S(2)}, u32[]{:S(2)}) collective-permute-start(bf16[128,1024]{1,0:T(8,128)(2,1)} %bitcast.64), channel_id=1, source_target_pairs={{0,4},{4,0},{1,5},{5,1},{2,6},{6,2},{3,7},{7,3},{8,12},{12,8},{9,1... | collective-permute-start | bytes 786440 | tf_op jit(solution)/shard_map/ppermute | solution.py:81
  8.3 22.8 %all-to-all-start = ((bf16[8,2,4,64,128]{4,3,2,1,0:T(8,128)(2,1)}), bf16[8,2,4,64,128]{4,3,2,1,0:T(8,128)(2,1)}, u32[]{:S(2)}, u32[]{:S(2)}) async-start(bf16[8,2,4,64,128]{4,3,2,1,0:T(8,128)(2,1)} %bitcast.1), calls=%async_computation | async-start | bytes 2097152 | tf_op jit(solution)/shard_map/all_to_all | solution.py:64
  12.6 4.8 %copy-start.2 = (bf16[1,128,1024]{2,1,0:T(8,128)(2,1)S(1)}, bf16[1,128,1024]{2,1,0:T(8,128)(2,1)}, u32[]{:S(2)}) copy-start(bf16[1,128,1024]{2,1,0:T(8,128)(2,1)} %param.6) | copy-start | bytes 786436
  17.4 1.5 %copy-start.4 = (s32[4]{0:T(128)S(1)}, s32[4]{0:T(128)}, u32[]{:S(2)}) copy-start(s32[4]{0:T(128)} %param.10) | copy-start | bytes 52
  17.4 4.0 %copy-start.5 = (s32[4]{0:T(128)S(1)}, s32[4]{0:T(128)}, u32[]{:S(2)}) copy-start(s32[4]{0:T(128)} %param.11) | copy-start | bytes 52
  27.2 0.8 %copy-start.1 = (f32[2,128,512]{1,2,0:T(8,128)}, f32[2,128,512]{1,2,0:T(8,128)S(1)}, u32[]{:S(2)}) copy-start(f32[2,128,512]{1,2,0:T(8,128)S(1)} %convolution_bitcast_fusion) | copy-start | bytes 1572868
  29.1 9.7 %collective-permute-start.2 = (bf16[128,512]{0,1:T(8,128)(2,1)S(1)}, bf16[128,512]{0,1:T(8,128)(2,1)S(1)}, u32[]{:S(2)}, u32[]{:S(2)}) collective-permute-start(bf16[128,512]{0,1:T(8,128)(2,1)S(1)} %multiply_convert_fusion.1), channel_id=1, source_target_pairs={{0,4},{4,0},{1,5},{5,1},{2,6},{6,2},{3,7},{7,3},{8,12},{12,8},{9,1... | collective-permute-start | bytes 393224 | tf_op jit(solution)/shard_map/ppermute | solution.py:84
  33.2 5.7 %copy-start.3 = (f32[1024]{0:T(1024)S(1)}, f32[1024]{0:T(1024)}, u32[]{:S(2)}) copy-start(f32[1024]{0:T(1024)} %param.9) | copy-start | bytes 12292
  33.2 5.3 %collective-permute-start.1 = (bf16[128,512]{0,1:T(8,128)(2,1)S(1)}, bf16[128,512]{0,1:T(8,128)(2,1)S(1)}, u32[]{:S(2)}, u32[]{:S(2)}) collective-permute-start(bf16[128,512]{0,1:T(8,128)(2,1)S(1)} %bitcast.66), channel_id=1, source_target_pairs={{0,4},{4,0},{1,5},{5,1},{2,6},{6,2},{3,7},{7,3},{8,12},{12,8},{9,1... | collective-permute-start | bytes 393224 | tf_op jit(solution)/shard_map/ppermute | solution.py:86

commit v14 on v13

--- a/solution.py
+++ b/solution.py
@@ -49,8 +49,9 @@
     n_blk = lax.axis_size("blk")
     blk = lax.axis_index("blk")
     slot = lax.axis_index("store")
-    person = lax.dynamic_index_in_dim(users, slot, 0, keepdims=False)
-    count = lax.dynamic_index_in_dim(lengths, person, 0, keepdims=False)
+    ids = jnp.arange(users.shape[0], dtype=jnp.int32)
+    chosen = (ids[:, None] == slot) & (users[:, None] == ids[None, :])
+    count = jnp.sum(jnp.where(chosen, lengths[None, :], 0))
     half = proj_weight.shape[2]
     local_heads = half // HEAD_SIZE
 

time: 40.4 us -> 38 us (0.941)
  between operations: 2.78 us -> 0.84 us
  local copies, waits for them, and re-layouts: 14.8 us -> 13.7 us
  other arithmetic: 3.94 us -> 4.65 us
    dynamic_slice x2 -> x0, local copies, waits for them, and re-layouts: 1.17 us -> none  [the longest x1 0.59 us: per_device(): count = lax.dynamic_index_in_dim(lengths, person, 0, keepdims=False)]
    reduce_sum x0 -> x1, other arithmetic: none -> 0.7 us  [per_device(): count = jnp.sum(jnp.where(chosen, lengths[None, :], 0))]
  transfers between devices with their start and end apart: 4 -> 4, of which waited for: 1 -> 1; matrix products, arithmetic and copies ran while one was open for 54% -> 56% of each run, Pallas kernels for 0% -> 0%
where the time goes in v14:
time: 38 us; the launch traced here: 37.5 us
  local copies, waits for them, and re-layouts  13.7 us (36%)
  starting transfers between devices  9.38 us (25%)
  other arithmetic  4.65 us (12%)
  matrix products  4.61 us (12%)
  waiting for transfers between devices  4.4 us (12%)
  between operations  0.84 us (2%)
    unnamed x13, local copies, waits for them, and re-layouts  5.58 us
    ppermute x1, waiting for transfers between devices, per_device(): back = lax.ppermute(sent, 'blk', swap)  4.39 us
    all_to_all x1, starting transfers between devices, per_device(): lax.all_to_all(ordered, ('blk', 'store'), split_axis=0, concat_axis=3, ti...  4.24 us
    dot_general x2, matrix products, project(): jnp.einsum('cd,dkh->kch', feats, proj_weight, preferred_element_type=jnp....  3.16 us
    ppermute x1, starting transfers between devices, per_device(): peer = lax.ppermute(mine, 'blk', swap)  2.97 us
    gather x1, local copies, waits for them, and re-layouts, per_device(): kv_store.at[users].get(mode='promise_in_bounds', unique_indices=True)  2.66 us
    convert_element_type x2, other arithmetic, project(): gate = jax.nn.silu(proj[1]).astype(jnp.bfloat16)  2.06 us
    reshape x2, local copies, waits for them, and re-layouts, per_device(): kv_store.at[users].get(mode='promise_in_bounds', unique_indices=True)  2.02 us
  transfers between devices with their start and end apart: 4, of which 1 were waited for; matrix products, arithmetic and copies ran while one was open for 56% of the time, Pallas kernels for 0%

profile of v14, /device:TPU:0, one launch (start us, length us, event | category | flops | bytes accessed | tf_op | source)
XLA Modules:
  0.0 37.5 jit_solution(3667509022913474181)
XLA Ops:
  0.0 0.0 copy-start
  0.0 3.0 %collective-permute-start = (bf16[128,1024]{1,0:T(8,128)(2,1)}, bf16[128,1024]{1,0:T(8,128)(2,1)}, u32[]{:S(2)}, u32[]{:S(2)}) collective-permute-start(bf16[128,1024]{1,0:T(8,128)(2,1)} %bitcast.62), channel_id=1, source_target_pairs={{0,4},{4,0},{1,5},{5,1},{2,6},{6,2},{3,7},{7,3},{8,12},{12,8},{9,1... | collective-permute-start | bytes 786440 | tf_op jit(solution)/shard_map/ppermute | solution.py:82
  3.0 0.7 %compare_select_fusion = s32[4]{0:T(128)S(1)} fusion(s32[4]{0:T(128)} %param.10), kind=kLoop, calls=%fused_computation.37 | loop fusion | flops 12 | bytes 32 | tf_op jit(solution)/shard_map/select_n | solution.py:59
  3.6 0.0 copy-done
  3.6 2.7 %gather_fusion = bf16[4,64,2,1024]{3,2,1,0:T(2,128)(2,1)S(1)} fusion(bf16[4,64,2,1024]{3,2,1,0:T(2,128)(2,1)S(1)} %copy-done, s32[1024]{0:T(1024)S(1)} %pad_clamp_fusion), kind=kCustom, calls=%fused_computation | custom fusion | bytes 2097168 | tf_op jit(solution)/shard_map/gather | solution.py:59
  6.3 0.7 %reshape.223 = bf16[4,64,2,2,4,128]{5,4,3,2,1,0:T(4,128)(2,1)S(1)} reshape(bf16[4,64,2,1024]{3,2,1,0:T(2,128)(2,1)S(1)} %gather_fusion) | data formatting | bytes 2097152 | tf_op jit(solution)/shard_map/reshape | solution.py:59
  7.0 1.3 %copy.24 = bf16[4,64,2,2,4,128]{5,1,4,2,0,3:T(8,128)(2,1)} copy(bf16[4,64,2,2,4,128]{5,4,3,2,1,0:T(4,128)(2,1)S(1)} %reshape.223) | data formatting | bytes 2097152 | tf_op jit(solution)/shard_map/reshape | solution.py:59
  8.3 4.2 %all-to-all-start = ((bf16[8,2,4,64,128]{4,3,2,1,0:T(8,128)(2,1)}), bf16[8,2,4,64,128]{4,3,2,1,0:T(8,128)(2,1)}, u32[]{:S(2)}, u32[]{:S(2)}) async-start(bf16[8,2,4,64,128]{4,3,2,1,0:T(8,128)(2,1)} %bitcast.1), calls=%async_computation | async-start | bytes 2097152 | tf_op jit(solution)/shard_map/all_to_all | solution.py:65
  12.6 0.0 copy-start.2
  12.6 4.8 %copy.26 = bf16[1024,2,512]{0,2,1:T(8,128)(2,1)S(1)} copy(bf16[1024,2,512]{2,1,0:T(2,128)(2,1)} %param.8) | data formatting | bytes 4194304 | tf_op args[2]
  17.4 0.0 copy-done.2
  17.4 0.0 copy-start.4
  17.4 0.0 copy-start.5
  17.4 1.5 %convolution_bitcast_fusion.1 = f32[2,128,512]{1,2,0:T(8,128)} fusion(bf16[1024,2,512]{0,2,1:T(8,128)(2,1)S(1)} %copy.26, bf16[1,128,1024]{2,1,0:T(8,128)(2,1)S(1)} %copy-done.2), kind=kOutput, calls=%fused_computation.4 | convolution fusion | flops 268435456 | bytes 2883584 | tf_op jit(solution)/shard_map/cd,dkh->kch/dot_general | solution.py:75
  18.9 0.0 copy-done.4
  18.9 0.0 copy-done.5
  18.9 0.7 %select_reduce_fusion = s32[]{:T(128)} fusion(s32[4]{0:T(128)S(1)} %copy-done.4, s32[4]{0:T(128)S(1)} %copy-done.5, pred[4]{0:T(512)(128)(4,1)S(1)} %iota_compare_fusion.2), kind=kLoop, calls=%fused_computation.38 | loop fusion | flops 63 | bytes 40 | tf_op jit(solution)/shard_map/reduce_sum | solution.py:54
  19.6 0.6 %fusion.16 = f32[512]{0:T(512)S(1)} fusion(s32[]{:T(128)} %select_reduce_fusion), kind=kLoop, calls=%fused_computation.41 | loop fusion | flops 1024 | bytes 2052 | tf_op jit(solution)/shard_map/convert_element_type | solution.py:26
  20.9 1.0 %slice.49 = bf16[1,128,512]{1,2,0:T(8,128)(2,1)S(1)} slice(f32[2,128,512]{1,2,0:T(8,128)} %convolution_bitcast_fusion.1), slice={[0:1], [0:128], [0:512]} | slice | bytes 262144 | tf_op jit(solution)/shard_map/slice | solution.py:76
  21.9 0.1 copy.27
  22.0 1.0 %multiply_convert_fusion.2 = bf16[1,128,512]{1,2,0:T(8,128)(2,1)S(1)} fusion(f32[2,128,512]{1,2,0:T(8,128)} %convolution_bitcast_fusion.1), kind=kLoop, calls=%fused_computation.33 | loop fusion | flops 327680 | bytes 393216 | tf_op jit(solution)/shard_map/convert_element_type | solution.py:77
  23.1 0.0 collective-permute-done
  23.1 1.7 %convolution_bitcast_fusion = f32[2,128,512]{1,2,0:T(8,128)S(1)} fusion(bf16[1024,2,512]{0,2,1:T(8,128)(2,1)S(1)} %copy.26, bf16[128,1024]{1,0:T(8,128)(2,1)} %collective-permute-done), kind=kOutput, calls=%fused_computation.3 | convolution fusion | flops 268435456 | bytes 2883584 | tf_op jit(solution)/shard_map/cd,dkh->kch/dot_general | solution.py:75
  24.8 0.0 copy-start.1
  24.8 0.8 %copy-done.1 = f32[2,128,512]{1,2,0:T(8,128)} copy-done((f32[2,128,512]{1,2,0:T(8,128)}, f32[2,128,512]{1,2,0:T(8,128)S(1)}, u32[]{:S(2)}) %copy-start.1) | copy-done | bytes 524312
  25.6 0.1 copy.30
  25.7 1.0 %multiply_convert_fusion.1 = bf16[128,512]{0,1:T(8,128)(2,1)S(1)} fusion(f32[2,128,512]{1,2,0:T(8,128)} %copy-done.1), kind=kLoop, calls=%fused_computation.32 | loop fusion | flops 327680 | bytes 393216 | tf_op jit(solution)/shard_map/convert_element_type | solution.py:77
  26.7 2.0 %collective-permute-start.2 = (bf16[128,512]{0,1:T(8,128)(2,1)S(1)}, bf16[128,512]{0,1:T(8,128)(2,1)S(1)}, u32[]{:S(2)}, u32[]{:S(2)}) collective-permute-start(bf16[128,512]{0,1:T(8,128)(2,1)S(1)} %multiply_convert_fusion.1), channel_id=1, source_target_pairs={{0,4},{4,0},{1,5},{5,1},{2,6},{6,2},{3,7},{7,3},{8,12},{12,8},{9,1... | collective-permute-start | bytes 393224 | tf_op jit(solution)/shard_map/ppermute | solution.py:85
  28.7 0.0 all-to-all-done
  28.7 1.3 %copy.25 = bf16[1,2,4,8,64,128]{5,4,3,2,1,0:T(8,128)(2,1)S(1)} copy(bf16[1,2,4,8,64,128]{5,4,2,1,3,0:T(8,128)(2,1)} %bitcast.3) | data formatting | bytes 2097152 | tf_op jit(solution)/shard_map/all_to_all | solution.py:65
  30.0 0.7 %convolution_convert_fusion = bf16[4,128,128]{2,1,0:T(8,128)(2,1)S(1)} fusion(f32[]{:T(128)S(6)} %convert_element_type.96, f32[512]{0:T(512)S(1)} %fusion.16, bf16[1,2,4,512,128]{4,3,2,1,0:T(8,128)(2,1)S(1)} %bitcast.58, bf16[128,4,128]{2,0,1:T(8,128)(2,1)S(1)} %copy.30), kind=kOutput, calls=%fused_computation.5 | convolution fusion | flops 136380416 | bytes 1312772 | tf_op jit(solution)/shard_map/hck,hkd->chd/dot_general | solution.py:28
  30.7 0.0 copy-start.3
  30.8 0.2 collective-permute-start.1
  31.0 0.7 %convolution_convert_fusion.1 = bf16[4,128,128]{2,1,0:T(8,128)(2,1)S(1)} fusion(f32[]{:T(128)S(6)} %convert_element_type.96, f32[512]{0:T(512)S(1)} %fusion.16, bf16[1,2,4,512,128]{4,3,2,1,0:T(8,128)(2,1)S(1)} %bitcast.59, bf16[128,4,128]{2,0,1:T(8,128)(2,1)S(1)} %copy.27), kind=kOutput, calls=%fused_computation.6 | convolution fusion | flops 136380416 | bytes 1312772 | tf_op jit(solution)/shard_map/hck,hkd->chd/dot_general | solution.py:28
  31.7 4.4 %collective-permute-done.1 = bf16[128,512]{0,1:T(8,128)(2,1)S(1)} collective-permute-done((bf16[128,512]{0,1:T(8,128)(2,1)S(1)}, bf16[128,512]{0,1:T(8,128)(2,1)S(1)}, u32[]{:S(2)}, u32[]{:S(2)}) %collective-permute-start.1) | collective-permute-done | bytes 131104 | tf_op jit(solution)/shard_map/ppermute | solution.py:87
  36.1 0.2 convert_reduce_fusion
  36.3 0.2 fusion.1
  36.4 0.0 collective-permute-done.2
  36.4 0.0 copy-done.3
  36.5 0.2 multiply_convert_fusion
  36.7 0.9 %copy.32 = bf16[1,128,1024]{2,1,0:T(8,128)(2,1)} copy(bf16[1,128,1024]{1,2,0:T(8,128)(2,1)S(1)} %multiply_convert_fusion) | data formatting | bytes 524288 | tf_op jit(solution)/shard_map/convert_element_type | solution.py:45
  (5 shorter events, 0.0 us)
Async XLA Ops:
  0.0 3.6 %copy-start = (bf16[4,64,2,1024]{3,2,1,0:T(2,128)(2,1)S(1)}, bf16[4,64,2,1024]{3,2,1,0:T(2,128)(2,1)}, u32[]{:S(2)}) copy-start(bf16[4,64,2,1024]{3,2,1,0:T(2,128)(2,1)} %param.7) | copy-start | bytes 3145732
  0.0 23.1 %collective-permute-start = (bf16[128,1024]{1,0:T(8,128)(2,1)}, bf16[128,1024]{1,0:T(8,128)(2,1)}, u32[]{:S(2)}, u32[]{:S(2)}) collective-permute-start(bf16[128,1024]{1,0:T(8,128)(2,1)} %bitcast.62), channel_id=1, source_target_pairs={{0,4},{4,0},{1,5},{5,1},{2,6},{6,2},{3,7},{7,3},{8,12},{12,8},{9,1... | collective-permute-start | bytes 786440 | tf_op jit(solution)/shard_map/ppermute | solution.py:82
  8.3 20.4 %all-to-all-start = ((bf16[8,2,4,64,128]{4,3,2,1,0:T(8,128)(2,1)}), bf16[8,2,4,64,128]{4,3,2,1,0:T(8,128)(2,1)}, u32[]{:S(2)}, u32[]{:S(2)}) async-start(bf16[8,2,4,64,128]{4,3,2,1,0:T(8,128)(2,1)} %bitcast.1), calls=%async_computation | async-start | bytes 2097152 | tf_op jit(solution)/shard_map/all_to_all | solution.py:65
  12.6 4.8 %copy-start.2 = (bf16[1,128,1024]{2,1,0:T(8,128)(2,1)S(1)}, bf16[1,128,1024]{2,1,0:T(8,128)(2,1)}, u32[]{:S(2)}) copy-start(bf16[1,128,1024]{2,1,0:T(8,128)(2,1)} %param.6) | copy-start | bytes 786436
  17.4 1.5 %copy-start.4 = (s32[4]{0:T(128)S(1)}, s32[4]{0:T(128)}, u32[]{:S(2)}) copy-start(s32[4]{0:T(128)} %param.11) | copy-start | bytes 52
  17.4 1.5 %copy-start.5 = (s32[4]{0:T(128)S(1)}, s32[4]{0:T(128)}, u32[]{:S(2)}) copy-start(s32[4]{0:T(128)} %param.10) | copy-start | bytes 52
  24.8 0.8 %copy-start.1 = (f32[2,128,512]{1,2,0:T(8,128)}, f32[2,128,512]{1,2,0:T(8,128)S(1)}, u32[]{:S(2)}) copy-start(f32[2,128,512]{1,2,0:T(8,128)S(1)} %convolution_bitcast_fusion) | copy-start | bytes 1572868
  26.7 9.7 %collective-permute-start.2 = (bf16[128,512]{0,1:T(8,128)(2,1)S(1)}, bf16[128,512]{0,1:T(8,128)(2,1)S(1)}, u32[]{:S(2)}, u32[]{:S(2)}) collective-permute-start(bf16[128,512]{0,1:T(8,128)(2,1)S(1)} %multiply_convert_fusion.1), channel_id=1, source_target_pairs={{0,4},{4,0},{1,5},{5,1},{2,6},{6,2},{3,7},{7,3},{8,12},{12,8},{9,1... | collective-permute-start | bytes 393224 | tf_op jit(solution)/shard_map/ppermute | solution.py:85
  30.7 5.7 %copy-start.3 = (f32[1024]{0:T(1024)S(1)}, f32[1024]{0:T(1024)}, u32[]{:S(2)}) copy-start(f32[1024]{0:T(1024)} %param.9) | copy-start | bytes 12292
  30.8 5.3 %collective-permute-start.1 = (bf16[128,512]{0,1:T(8,128)(2,1)S(1)}, bf16[128,512]{0,1:T(8,128)(2,1)S(1)}, u32[]{:S(2)}, u32[]{:S(2)}) collective-permute-start(bf16[128,512]{0,1:T(8,128)(2,1)S(1)} %bitcast.64), channel_id=1, source_target_pairs={{0,4},{4,0},{1,5},{5,1},{2,6},{6,2},{3,7},{7,3},{8,12},{12,8},{9,1... | collective-permute-start | bytes 393224 | tf_op jit(solution)/shard_map/ppermute | solution.py:87

commit v15 on v14

--- a/solution.py
+++ b/solution.py
@@ -80,11 +80,12 @@
     if n_blk == 2:
         swap = [(0, 1), (1, 0)]
         peer = lax.ppermute(mine, "blk", swap)
-        query_own, gate_own = project(mine)
         query_peer, gate_peer = project(peer)
         gate_back = lax.ppermute(gate_peer, "blk", swap)
         sent = attend(query_peer, keys, values, count).astype(jnp.bfloat16)
         back = lax.ppermute(sent, "blk", swap)
+        late, _ = lax.optimization_barrier((mine, sent))
+        query_own, gate_own = project(late)
         kept = attend(query_own, keys, values, count).astype(jnp.bfloat16)
         first = blk == 0
         attended = jnp.where(first, jnp.concatenate([kept, back], axis=1),

time: 38 us -> 43.4 us (1.14)
  waiting for transfers between devices: 4.4 us -> 16.8 us
  local copies, waits for them, and re-layouts: 13.7 us -> 6.38 us
  matrix products: 4.61 us -> 6.97 us
  other arithmetic: 4.65 us -> 2.85 us
    ppermute x1, waiting for transfers between devices: 0.01 us -> 16 us  [per_device(): peer = lax.ppermute(mine, 'blk', swap)]
    unnamed x13 -> x12, local copies, waits for them, and re-layouts: 5.58 us -> 0.52 us
    ppermute x1, waiting for transfers between devices: 4.39 us -> 0.79 us  [per_device(): back = lax.ppermute(sent, 'blk', swap)]
    convert_element_type x2, other arithmetic: 2.06 us -> 0.16 us  [project(): gate = jax.nn.silu(proj[1]).astype(jnp.bfloat16)]
    dot_general x2, matrix products: 3.16 us -> 4.85 us  [project(): jnp.einsum('cd,dkh->kch', feats, proj_weight, preferred_element_type=jnp....]
    ppermute x1, starting transfers between devices: 1.96 us -> 0.42 us  [per_device(): gate_back = lax.ppermute(gate_peer, 'blk', swap)]
    ppermute x1, starting transfers between devices: 0.21 us -> 1.67 us  [per_device(): back = lax.ppermute(sent, 'blk', swap)]
    all_to_all x1, local copies, waits for them, and re-layouts: 1.31 us -> 0.09 us  [per_device(): lax.all_to_all(ordered, ('blk', 'store'), split_axis=0, concat_axis=3, ti...]
  transfers between devices with their start and end apart: 4 -> 4, of which waited for: 1 -> 2; matrix products, arithmetic and copies ran while one was open for 56% -> 21% of each run, Pallas kernels for 0% -> 0%
where the time goes in v15:
time: 43.4 us; the launch traced here: 43.1 us
  waiting for transfers between devices  16.8 us (39%)
  starting transfers between devices  9.28 us (21%)
  matrix products  6.97 us (16%)
  local copies, waits for them, and re-layouts  6.38 us (15%)
  other arithmetic  2.85 us (7%)
  between operations  0.82 us (2%)
    ppermute x1, waiting for transfers between devices, per_device(): peer = lax.ppermute(mine, 'blk', swap)  16 us
    all_to_all x1, starting transfers between devices, per_device(): lax.all_to_all(ordered, ('blk', 'store'), split_axis=0, concat_axis=3, ti...  5.17 us
    dot_general x2, matrix products, project(): jnp.einsum('cd,dkh->kch', feats, proj_weight, preferred_element_type=jnp....  4.85 us
    gather x1, local copies, waits for them, and re-layouts, per_device(): kv_store.at[users].get(mode='promise_in_bounds', unique_indices=True)  2.65 us
    dot_general x2, matrix products, one_block(): jnp.einsum('hck,hkd->chd', weights, value_block, preferred_element_type=j...  2.13 us
    ppermute x1, starting transfers between devices, per_device(): peer = lax.ppermute(mine, 'blk', swap)  2.02 us
    reshape x2, local copies, waits for them, and re-layouts, per_device(): kv_store.at[users].get(mode='promise_in_bounds', unique_indices=True)  1.97 us
    ppermute x1, starting transfers between devices, per_device(): back = lax.ppermute(sent, 'blk', swap)  1.67 us
  transfers between devices with their start and end apart: 4, of which 2 were waited for; matrix products, arithmetic and copies ran while one was open for 21% of the time, Pallas kernels for 0%

profile of v15, /device:TPU:0, one launch (start us, length us, event | category | flops | bytes accessed | tf_op | source)
XLA Modules:
  0.0 43.1 jit_solution(415576265980105349)
XLA Ops:
  0.0 0.0 copy-start
  0.0 0.7 %compare_select_fusion = s32[4]{0:T(128)S(1)} fusion(s32[4]{0:T(128)} %param.10), kind=kLoop, calls=%fused_computation.41 | loop fusion | flops 12 | bytes 32 | tf_op jit(solution)/shard_map/select_n | solution.py:59
  0.8 0.5 %copy-done = bf16[4,64,2,1024]{3,2,1,0:T(2,128)(2,1)S(1)} copy-done((bf16[4,64,2,1024]{3,2,1,0:T(2,128)(2,1)S(1)}, bf16[4,64,2,1024]{3,2,1,0:T(2,128)(2,1)}, u32[]{:S(2)}) %copy-start) | copy-done | bytes 1048600
  1.2 2.7 %gather_fusion = bf16[4,64,2,1024]{3,2,1,0:T(2,128)(2,1)S(1)} fusion(bf16[4,64,2,1024]{3,2,1,0:T(2,128)(2,1)S(1)} %copy-done, s32[1024]{0:T(1024)S(1)} %pad_clamp_fusion), kind=kCustom, calls=%fused_computation | custom fusion | bytes 2097168 | tf_op jit(solution)/shard_map/gather | solution.py:59
  3.9 0.7 %reshape.223 = bf16[4,64,2,2,4,128]{5,4,3,2,1,0:T(4,128)(2,1)S(1)} reshape(bf16[4,64,2,1024]{3,2,1,0:T(2,128)(2,1)S(1)} %gather_fusion) | data formatting | bytes 2097152 | tf_op jit(solution)/shard_map/reshape | solution.py:59
  4.6 0.0 copy-start.4
  4.6 0.0 copy-start.2
  4.6 0.0 copy-start.3
  4.7 1.3 %copy.26 = bf16[4,64,2,2,4,128]{5,1,4,2,0,3:T(8,128)(2,1)} copy(bf16[4,64,2,2,4,128]{5,4,3,2,1,0:T(4,128)(2,1)S(1)} %reshape.223) | data formatting | bytes 2097152 | tf_op jit(solution)/shard_map/reshape | solution.py:59
  5.9 5.2 %all-to-all-start = ((bf16[8,2,4,64,128]{4,3,2,1,0:T(8,128)(2,1)}), bf16[8,2,4,64,128]{4,3,2,1,0:T(8,128)(2,1)S(1)}, u32[]{:S(2)}, u32[]{:S(2)}) async-start(bf16[8,2,4,64,128]{4,3,2,1,0:T(8,128)(2,1)} %bitcast.1), calls=%async_computation | async-start | bytes 2097152 | tf_op jit(solution)/shard_map/all_to_all | solution.py:65
  11.1 0.0 copy-done.4
  11.1 2.0 %collective-permute-start = (bf16[128,1024]{1,0:T(8,128)(2,1)S(1)}, bf16[128,1024]{1,0:T(8,128)(2,1)S(1)}, u32[]{:S(2)}, u32[]{:S(2)}) collective-permute-start(bf16[128,1024]{1,0:T(8,128)(2,1)S(1)} %bitcast.62), channel_id=1, source_target_pairs={{0,4},{4,0},{1,5},{5,1},{2,6},{6,2},{3,7},{7,3},{8,12},{12,8},{9,1... | collective-permute-start | bytes 786440 | tf_op jit(solution)/shard_map/ppermute | solution.py:82
  13.1 0.0 copy-done.2
  13.1 0.0 copy-done.3
  13.1 0.7 %select_reduce_fusion = s32[]{:T(128)} fusion(s32[4]{0:T(128)S(1)} %copy-done.2, s32[4]{0:T(128)S(1)} %copy-done.3, pred[4]{0:T(512)(128)(4,1)S(1)} %iota_compare_fusion.2), kind=kLoop, calls=%fused_computation.42 | loop fusion | flops 63 | bytes 40 | tf_op jit(solution)/shard_map/reduce_sum | solution.py:54
  14.5 0.7 %fusion.26 = f32[512]{0:T(512)S(1)} fusion(s32[]{:T(128)} %select_reduce_fusion), kind=kLoop, calls=%fused_computation.45 | loop fusion | flops 1024 | bytes 2052 | tf_op jit(solution)/shard_map/convert_element_type | solution.py:26
  15.1 16.0 %collective-permute-done = bf16[128,1024]{1,0:T(8,128)(2,1)S(1)} collective-permute-done((bf16[128,1024]{1,0:T(8,128)(2,1)S(1)}, bf16[128,1024]{1,0:T(8,128)(2,1)S(1)}, u32[]{:S(2)}, u32[]{:S(2)}) %collective-permute-start) | collective-permute-done | bytes 262176 | tf_op jit(solution)/shard_map/ppermute | solution.py:82
  31.2 2.3 %fusion.7 = f32[2,128,512]{1,2,0:T(8,128)S(1)} fusion(bf16[1024,2,512]{2,1,0:T(2,128)(2,1)} %param.8, bf16[128,1024]{1,0:T(8,128)(2,1)S(1)} %collective-permute-done), kind=kOutput, calls=%fused_computation.8 | convolution fusion | flops 268435456 | bytes 2883584 | tf_op jit(solution)/shard_map/cd,dkh->kch/dot_general | solution.py:75
  33.5 0.1 copy.29
  33.7 0.1 multiply_convert_fusion.1
  33.8 0.4 collective-permute-start.2
  34.2 0.0 all-to-all-done
  34.2 0.1 copy.27
  34.3 0.0 copy-start.5
  34.3 1.4 %convolution_convert_fusion.1 = bf16[4,128,128]{2,1,0:T(8,128)(2,1)} fusion(f32[]{:T(128)S(6)} %convert_element_type.96, f32[512]{0:T(512)S(1)} %fusion.26, bf16[1,2,4,512,128]{4,3,2,1,0:T(8,128)(2,1)S(1)} %bitcast.57, bf16[128,4,128]{2,0,1:T(8,128)(2,1)S(1)} %copy.29), kind=kOutput, calls=%fused_computation.10 | convolution fusion | flops 136380416 | bytes 1312772 | tf_op jit(solution)/shard_map/hck,hkd->chd/dot_general | solution.py:28
  35.7 1.7 %collective-permute-start.1 = (bf16[128,512]{0,1:T(8,128)(2,1)}, bf16[128,512]{0,1:T(8,128)(2,1)S(1)}, u32[]{:S(2)}, u32[]{:S(2)}) collective-permute-start(bf16[128,512]{0,1:T(8,128)(2,1)} %bitcast.13), channel_id=1, source_target_pairs={{0,4},{4,0},{1,5},{5,1},{2,6},{6,2},{3,7},{7,3},{8,12},{12,8},{9,1... | collective-permute-start | bytes 393224 | tf_op jit(solution)/shard_map/ppermute | solution.py:86
  37.4 0.0 copy-done.5
  37.4 2.5 %fusion.4 = f32[2,128,512]{1,2,0:T(8,128)S(1)} fusion(bf16[1024,2,512]{2,1,0:T(2,128)(2,1)} %param.8, bf16[128,1024]{1,0:T(8,128)(2,1)S(1)} %bitcast.63), kind=kOutput, calls=%fused_computation.7 | convolution fusion | flops 268435456 | bytes 2883584 | tf_op jit(solution)/shard_map/cd,dkh->kch/dot_general | solution.py:75
  39.9 0.1 copy.33
  40.0 0.0 copy-start.1
  40.0 0.7 %convolution_convert_fusion = bf16[4,128,128]{2,1,0:T(8,128)(2,1)S(1)} fusion(f32[]{:T(128)S(6)} %convert_element_type.96, f32[512]{0:T(512)S(1)} %fusion.26, bf16[1,2,4,512,128]{4,3,2,1,0:T(8,128)(2,1)S(1)} %bitcast.58, bf16[128,4,128]{2,0,1:T(8,128)(2,1)S(1)} %copy.33), kind=kOutput, calls=%fused_computation.9 | convolution fusion | flops 136380416 | bytes 1312772 | tf_op jit(solution)/shard_map/hck,hkd->chd/dot_general | solution.py:28
  40.8 0.1 multiply_convert_fusion.2
  40.9 0.8 %collective-permute-done.1 = bf16[128,512]{0,1:T(8,128)(2,1)S(1)} collective-permute-done((bf16[128,512]{0,1:T(8,128)(2,1)}, bf16[128,512]{0,1:T(8,128)(2,1)S(1)}, u32[]{:S(2)}, u32[]{:S(2)}) %collective-permute-start.1) | collective-permute-done | bytes 131104 | tf_op jit(solution)/shard_map/ppermute | solution.py:86
  41.7 0.2 convert_reduce_fusion
  41.8 0.2 fusion.11
  42.0 0.0 collective-permute-done.2
  42.0 0.0 copy-done.1
  42.0 0.2 multiply_convert_fusion
  42.3 0.9 %copy.35 = bf16[1,128,1024]{2,1,0:T(8,128)(2,1)} copy(bf16[1,128,1024]{1,2,0:T(8,128)(2,1)S(1)} %multiply_convert_fusion) | data formatting | bytes 524288 | tf_op jit(solution)/shard_map/convert_element_type | solution.py:45
  (6 shorter events, 0.1 us)
Async XLA Ops:
  0.0 1.2 %copy-start = (bf16[4,64,2,1024]{3,2,1,0:T(2,128)(2,1)S(1)}, bf16[4,64,2,1024]{3,2,1,0:T(2,128)(2,1)}, u32[]{:S(2)}) copy-start(bf16[4,64,2,1024]{3,2,1,0:T(2,128)(2,1)} %param.7) | copy-start | bytes 3145732
  4.6 6.5 %copy-start.4 = (bf16[1,128,1024]{2,1,0:T(8,128)(2,1)S(1)}, bf16[1,128,1024]{2,1,0:T(8,128)(2,1)}, u32[]{:S(2)}) copy-start(bf16[1,128,1024]{2,1,0:T(8,128)(2,1)} %param.6) | copy-start | bytes 786436
  4.6 8.5 %copy-start.2 = (s32[4]{0:T(128)S(1)}, s32[4]{0:T(128)}, u32[]{:S(2)}) copy-start(s32[4]{0:T(128)} %param.11) | copy-start | bytes 52
  4.6 8.5 %copy-start.3 = (s32[4]{0:T(128)S(1)}, s32[4]{0:T(128)}, u32[]{:S(2)}) copy-start(s32[4]{0:T(128)} %param.10) | copy-start | bytes 52
  5.9 28.3 %all-to-all-start = ((bf16[8,2,4,64,128]{4,3,2,1,0:T(8,128)(2,1)}), bf16[8,2,4,64,128]{4,3,2,1,0:T(8,128)(2,1)S(1)}, u32[]{:S(2)}, u32[]{:S(2)}) async-start(bf16[8,2,4,64,128]{4,3,2,1,0:T(8,128)(2,1)} %bitcast.1), calls=%async_computation | async-start | bytes 2097152 | tf_op jit(solution)/shard_map/all_to_all | solution.py:65
  11.1 20.1 %collective-permute-start = (bf16[128,1024]{1,0:T(8,128)(2,1)S(1)}, bf16[128,1024]{1,0:T(8,128)(2,1)S(1)}, u32[]{:S(2)}, u32[]{:S(2)}) collective-permute-start(bf16[128,1024]{1,0:T(8,128)(2,1)S(1)} %bitcast.62), channel_id=1, source_target_pairs={{0,4},{4,0},{1,5},{5,1},{2,6},{6,2},{3,7},{7,3},{8,12},{12,8},{9,1... | collective-permute-start | bytes 786440 | tf_op jit(solution)/shard_map/ppermute | solution.py:82
  33.8 8.3 %collective-permute-start.2 = (bf16[128,512]{0,1:T(8,128)(2,1)S(1)}, bf16[128,512]{0,1:T(8,128)(2,1)S(1)}, u32[]{:S(2)}, u32[]{:S(2)}) collective-permute-start(bf16[128,512]{0,1:T(8,128)(2,1)S(1)} %multiply_convert_fusion.1), channel_id=1, source_target_pairs={{0,4},{4,0},{1,5},{5,1},{2,6},{6,2},{3,7},{7,3},{8,12},{12,8},{9,1... | collective-permute-start | bytes 393224 | tf_op jit(solution)/shard_map/ppermute | solution.py:84
  34.3 3.1 %copy-start.5 = (bf16[1,128,1024]{2,1,0:T(8,128)(2,1)S(1)}, bf16[1,128,1024]{2,1,0:T(8,128)(2,1)}, u32[]{:S(2)}) copy-start(bf16[1,128,1024]{2,1,0:T(8,128)(2,1)} %param.6) | copy-start | bytes 786436
  35.7 6.0 %collective-permute-start.1 = (bf16[128,512]{0,1:T(8,128)(2,1)}, bf16[128,512]{0,1:T(8,128)(2,1)S(1)}, u32[]{:S(2)}, u32[]{:S(2)}) collective-permute-start(bf16[128,512]{0,1:T(8,128)(2,1)} %bitcast.13), channel_id=1, source_target_pairs={{0,4},{4,0},{1,5},{5,1},{2,6},{6,2},{3,7},{7,3},{8,12},{12,8},{9,1... | collective-permute-start | bytes 393224 | tf_op jit(solution)/shard_map/ppermute | solution.py:86
  40.0 2.0 %copy-start.1 = (f32[1024]{0:T(1024)S(1)}, f32[1024]{0:T(1024)}, u32[]{:S(2)}) copy-start(f32[1024]{0:T(1024)} %param.9) | copy-start | bytes 12292

commit v16 on v14

--- a/solution.py
+++ b/solution.py
@@ -2,6 +2,7 @@
 import jax.numpy as jnp
 from jax import lax
 from jax.sharding import PartitionSpec as P
+from jax.experimental.layout import Layout, with_layout_constraint
 
 D = 1024
 HEADS = 8
@@ -83,9 +84,13 @@
         query_own, gate_own = project(mine)
         query_peer, gate_peer = project(peer)
         gate_back = lax.ppermute(gate_peer, "blk", swap)
+        row_major = Layout(major_to_minor=(0, 1))
         sent = attend(query_peer, keys, values, count).astype(jnp.bfloat16)
+        sent = with_layout_constraint(sent, row_major)
         back = lax.ppermute(sent, "blk", swap)
+        query_own, gate_own, _ = lax.optimization_barrier((query_own, gate_own, sent))
         kept = attend(query_own, keys, values, count).astype(jnp.bfloat16)
+        kept = with_layout_constraint(kept, row_major)
         first = blk == 0
         attended = jnp.where(first, jnp.concatenate([kept, back], axis=1),
                              jnp.concatenate([back, kept], axis=1))

time: 38 us -> 37.8 us (level)
  local copies, waits for them, and re-layouts: 13.7 us -> 12.8 us
  other arithmetic: 4.65 us -> 5.31 us
    convert_element_type x1 -> x3, local copies, waits for them, and re-layouts: 0.85 us -> 0.15 us  [the longest x2 0.12 us: per_device(): kept = attend(query_own, keys, values, count).astype(jnp.bfloat16)]
    convert_element_type x1, other arithmetic: 0.22 us -> 0.87 us  [finish(): return (normed * gate.astype(jnp.float32)).astype(jnp.bfloat16)]
  transfers between devices with their start and end apart: 4 -> 4, of which waited for: 1 -> 1; matrix products, arithmetic and copies ran while one was open for 56% -> 57% of each run, Pallas kernels for 0% -> 0%
where the time goes in v16:
time: 37.8 us; the launch traced here: 37.3 us
  local copies, waits for them, and re-layouts  12.8 us (34%)
  starting transfers between devices  9.38 us (25%)
  other arithmetic  5.31 us (14%)
  matrix products  4.67 us (12%)
  waiting for transfers between devices  4.29 us (11%)
  between operations  0.85 us (2%)
    unnamed x13, local copies, waits for them, and re-layouts  5.58 us
    ppermute x1, waiting for transfers between devices, per_device(): back = lax.ppermute(sent, 'blk', swap)  4.29 us
    all_to_all x1, starting transfers between devices, per_device(): lax.all_to_all(ordered, ('blk', 'store'), split_axis=0, concat_axis=3, ti...  4.24 us
    dot_general x2, matrix products, project(): jnp.einsum('cd,dkh->kch', feats, proj_weight, preferred_element_type=jnp....  3.4 us
    ppermute x1, starting transfers between devices, per_device(): peer = lax.ppermute(mine, 'blk', swap)  2.97 us
    gather x1, local copies, waits for them, and re-layouts, per_device(): kv_store.at[users].get(mode='promise_in_bounds', unique_indices=True)  2.66 us
    convert_element_type x2, other arithmetic, project(): gate = jax.nn.silu(proj[1]).astype(jnp.bfloat16)  2.06 us
    reshape x2, local copies, waits for them, and re-layouts, per_device(): kv_store.at[users].get(mode='promise_in_bounds', unique_indices=True)  2.02 us
  transfers between devices with their start and end apart: 4, of which 1 were waited for; matrix products, arithmetic and copies ran while one was open for 57% of the time, Pallas kernels for 0%

profile of v16, /device:TPU:0, one launch (start us, length us, event | category | flops | bytes accessed | tf_op | source)
XLA Modules:
  0.0 37.3 jit_solution(15497531011760025280)
XLA Ops:
  0.0 0.0 copy-start
  0.0 3.0 %collective-permute-start = (bf16[128,1024]{1,0:T(8,128)(2,1)}, bf16[128,1024]{1,0:T(8,128)(2,1)}, u32[]{:S(2)}, u32[]{:S(2)}) collective-permute-start(bf16[128,1024]{1,0:T(8,128)(2,1)} %bitcast.66), channel_id=1, source_target_pairs={{0,4},{4,0},{1,5},{5,1},{2,6},{6,2},{3,7},{7,3},{8,12},{12,8},{9,1... | collective-permute-start | bytes 786440 | tf_op jit(solution)/shard_map/ppermute | solution.py:83
  3.0 0.7 %compare_select_fusion = s32[4]{0:T(128)S(1)} fusion(s32[4]{0:T(128)} %param.10), kind=kLoop, calls=%fused_computation.42 | loop fusion | flops 12 | bytes 32 | tf_op jit(solution)/shard_map/select_n | solution.py:60
  3.6 0.0 copy-done
  3.6 2.7 %gather_fusion = bf16[4,64,2,1024]{3,2,1,0:T(2,128)(2,1)S(1)} fusion(bf16[4,64,2,1024]{3,2,1,0:T(2,128)(2,1)S(1)} %copy-done, s32[1024]{0:T(1024)S(1)} %pad_clamp_fusion), kind=kCustom, calls=%fused_computation | custom fusion | bytes 2097168 | tf_op jit(solution)/shard_map/gather | solution.py:60
  6.3 0.7 %reshape.231 = bf16[4,64,2,2,4,128]{5,4,3,2,1,0:T(4,128)(2,1)S(1)} reshape(bf16[4,64,2,1024]{3,2,1,0:T(2,128)(2,1)S(1)} %gather_fusion) | data formatting | bytes 2097152 | tf_op jit(solution)/shard_map/reshape | solution.py:60
  7.0 1.3 %copy.26 = bf16[4,64,2,2,4,128]{5,1,4,2,0,3:T(8,128)(2,1)} copy(bf16[4,64,2,2,4,128]{5,4,3,2,1,0:T(4,128)(2,1)S(1)} %reshape.231) | data formatting | bytes 2097152 | tf_op jit(solution)/shard_map/reshape | solution.py:60
  8.3 4.2 %all-to-all-start = ((bf16[8,2,4,64,128]{4,3,2,1,0:T(8,128)(2,1)}), bf16[8,2,4,64,128]{4,3,2,1,0:T(8,128)(2,1)}, u32[]{:S(2)}, u32[]{:S(2)}) async-start(bf16[8,2,4,64,128]{4,3,2,1,0:T(8,128)(2,1)} %bitcast.1), calls=%async_computation | async-start | bytes 2097152 | tf_op jit(solution)/shard_map/all_to_all | solution.py:66
  12.6 0.0 copy-start.2
  12.6 4.8 %copy.28 = bf16[1024,2,512]{0,2,1:T(8,128)(2,1)S(1)} copy(bf16[1024,2,512]{2,1,0:T(2,128)(2,1)} %param.8) | data formatting | bytes 4194304 | tf_op args[2]
  17.4 0.0 copy-done.2
  17.4 0.0 copy-start.4
  17.4 0.0 copy-start.5
  17.4 1.6 %convolution_bitcast_fusion.1 = f32[2,128,512]{2,1,0:T(8,128)} fusion(bf16[1024,2,512]{0,2,1:T(8,128)(2,1)S(1)} %copy.28, bf16[1,128,1024]{2,1,0:T(8,128)(2,1)S(1)} %copy-done.2), kind=kOutput, calls=%fused_computation.4 | convolution fusion | flops 268435456 | bytes 2883584 | tf_op jit(solution)/shard_map/cd,dkh->kch/dot_general | solution.py:76
  19.0 0.0 copy-done.4
  19.0 0.0 copy-done.5
  19.0 0.7 %select_reduce_fusion = s32[]{:T(128)} fusion(s32[4]{0:T(128)S(1)} %copy-done.4, s32[4]{0:T(128)S(1)} %copy-done.5, pred[4]{0:T(512)(128)(4,1)S(1)} %iota_compare_fusion.2), kind=kLoop, calls=%fused_computation.43 | loop fusion | flops 63 | bytes 40 | tf_op jit(solution)/shard_map/reduce_sum | solution.py:55
  19.8 0.6 %fusion.17 = f32[512]{0:T(512)S(1)} fusion(s32[]{:T(128)} %select_reduce_fusion), kind=kLoop, calls=%fused_computation.46 | loop fusion | flops 1024 | bytes 2052 | tf_op jit(solution)/shard_map/convert_element_type | solution.py:27
  21.1 1.0 %slice.51 = bf16[1,128,512]{2,1,0:T(8,128)(2,1)S(1)} slice(f32[2,128,512]{2,1,0:T(8,128)} %convolution_bitcast_fusion.1), slice={[0:1], [0:128], [0:512]} | slice | bytes 262144 | tf_op jit(solution)/shard_map/slice | solution.py:77
  22.1 1.0 %multiply_convert_fusion.2 = bf16[128,512]{1,0:T(8,128)(2,1)S(1)} fusion(f32[2,128,512]{2,1,0:T(8,128)} %convolution_bitcast_fusion.1), kind=kLoop, calls=%fused_computation.35 | loop fusion | flops 327680 | bytes 393216 | tf_op jit(solution)/shard_map/convert_element_type | solution.py:78
  23.1 0.0 collective-permute-done
  23.1 1.8 %convolution_bitcast_fusion = f32[2,128,512]{2,1,0:T(8,128)S(1)} fusion(bf16[1024,2,512]{0,2,1:T(8,128)(2,1)S(1)} %copy.28, bf16[128,1024]{1,0:T(8,128)(2,1)} %collective-permute-done), kind=kOutput, calls=%fused_computation.3 | convolution fusion | flops 268435456 | bytes 2883584 | tf_op jit(solution)/shard_map/cd,dkh->kch/dot_general | solution.py:76
  24.9 0.0 copy-start.1
  24.9 0.8 %copy-done.1 = f32[2,128,512]{2,1,0:T(8,128)} copy-done((f32[2,128,512]{2,1,0:T(8,128)}, f32[2,128,512]{2,1,0:T(8,128)S(1)}, u32[]{:S(2)}) %copy-start.1) | copy-done | bytes 524312
  25.8 1.0 %multiply_convert_fusion.1 = bf16[128,512]{1,0:T(8,128)(2,1)S(1)} fusion(f32[2,128,512]{2,1,0:T(8,128)} %copy-done.1), kind=kLoop, calls=%fused_computation.34 | loop fusion | flops 327680 | bytes 393216 | tf_op jit(solution)/shard_map/convert_element_type | solution.py:78
  26.8 2.0 %collective-permute-start.2 = (bf16[128,512]{1,0:T(8,128)(2,1)S(1)}, bf16[128,512]{1,0:T(8,128)(2,1)S(1)}, u32[]{:S(2)}, u32[]{:S(2)}) collective-permute-start(bf16[128,512]{1,0:T(8,128)(2,1)S(1)} %multiply_convert_fusion.1), channel_id=1, source_target_pairs={{0,4},{4,0},{1,5},{5,1},{2,6},{6,2},{3,7},{7,3},{8,12},{12,8},{9,1... | collective-permute-start | bytes 393224 | tf_op jit(solution)/shard_map/ppermute | solution.py:86
  28.8 0.0 all-to-all-done
  28.8 1.3 %copy.27 = bf16[1,2,4,8,64,128]{5,4,3,2,1,0:T(8,128)(2,1)S(1)} copy(bf16[1,2,4,8,64,128]{5,4,2,1,3,0:T(8,128)(2,1)} %bitcast.3) | data formatting | bytes 2097152 | tf_op jit(solution)/shard_map/all_to_all | solution.py:66
  30.1 0.6 %fusion = bf16[4,16,8,128]{3,2,1,0:T(8,128)(2,1)S(1)} fusion(f32[]{:T(128)S(6)} %convert_element_type.88, f32[512]{0:T(512)S(1)} %fusion.17, bf16[1,2,4,512,128]{4,3,2,1,0:T(8,128)(2,1)S(1)} %bitcast.62, bf16[128,4,128]{2,1,0:T(4,128)(2,1)S(1)} %convert_element_type.86), kind=kOutput, calls=%fused_computation.7 | convolution fusion | flops 136380416 | bytes 1312772 | tf_op jit(solution)/shard_map/hck,hkd->chd/dot_general | solution.py:29
  30.8 0.2 collective-permute-start.1
  31.0 0.0 copy-start.3
  31.0 0.6 %convolution_convert_fusion = bf16[4,128,128]{1,2,0:T(8,128)(2,1)S(1)} fusion(bf16[4,128,128]{2,1,0:T(8,128)(2,1)S(1)} %bitcast.67, f32[]{:T(128)S(6)} %convert_element_type.88, f32[512]{0:T(512)S(1)} %fusion.17, bf16[1,2,4,512,128]{4,3,2,1,0:T(8,128)(2,1)S(1)} %bitcast.63), kind=kOutput, calls=%fused_computation.5 | convolution fusion | flops 136380416 | bytes 1312772 | tf_op jit(solution)/shard_map/hck,hkd->chd/dot_general | solution.py:29
  31.6 0.1 copy.35
  31.7 0.1 concatenate.52
  31.8 4.3 %collective-permute-done.1 = bf16[128,512]{1,0:T(8,128)(2,1)S(1)} collective-permute-done((bf16[128,512]{1,0:T(8,128)(2,1)S(1)}, bf16[128,512]{1,0:T(8,128)(2,1)S(1)}, u32[]{:S(2)}, u32[]{:S(2)}) %collective-permute-start.1) | collective-permute-done | bytes 131104 | tf_op jit(solution)/shard_map/ppermute | solution.py:90
  36.1 0.1 convert_reduce_fusion
  36.2 0.2 fusion.2
  36.5 0.0 collective-permute-done.2
  36.5 0.0 copy-done.3
  36.5 0.9 %multiply_convert_fusion = bf16[1,128,1024]{2,1,0:T(8,128)(2,1)} fusion(bf16[1,128,512]{2,1,0:T(8,128)(2,1)S(1)} %bitcast.61, bf16[1,128,512]{2,1,0:T(8,128)(2,1)S(1)} %concatenate.52, bf16[1,128,512]{2,1,0:T(8,128)(2,1)S(1)} %bitcast.69, bf16[1,128,512]{2,1,0:T(8,128)(2,1)S(1)} %bitcast.64, f32[1024]{0:T(1024)S(1)} %copy-done.3, f32[128]{0:T(128)S(1)} %add_rsqrt_fusion, ...), kind=kLoop, calls=%fused_computation.16 | loop fusion | flops 3276800 | bytes 791553 | tf_op jit(solution)/shard_map/convert_element_type | solution.py:46
  (10 shorter events, 0.2 us)
Async XLA Ops:
  0.0 3.6 %copy-start = (bf16[4,64,2,1024]{3,2,1,0:T(2,128)(2,1)S(1)}, bf16[4,64,2,1024]{3,2,1,0:T(2,128)(2,1)}, u32[]{:S(2)}) copy-start(bf16[4,64,2,1024]{3,2,1,0:T(2,128)(2,1)} %param.7) | copy-start | bytes 3145732
  0.0 23.1 %collective-permute-start = (bf16[128,1024]{1,0:T(8,128)(2,1)}, bf16[128,1024]{1,0:T(8,128)(2,1)}, u32[]{:S(2)}, u32[]{:S(2)}) collective-permute-start(bf16[128,1024]{1,0:T(8,128)(2,1)} %bitcast.66), channel_id=1, source_target_pairs={{0,4},{4,0},{1,5},{5,1},{2,6},{6,2},{3,7},{7,3},{8,12},{12,8},{9,1... | collective-permute-start | bytes 786440 | tf_op jit(solution)/shard_map/ppermute | solution.py:83
  8.3 20.4 %all-to-all-start = ((bf16[8,2,4,64,128]{4,3,2,1,0:T(8,128)(2,1)}), bf16[8,2,4,64,128]{4,3,2,1,0:T(8,128)(2,1)}, u32[]{:S(2)}, u32[]{:S(2)}) async-start(bf16[8,2,4,64,128]{4,3,2,1,0:T(8,128)(2,1)} %bitcast.1), calls=%async_computation | async-start | bytes 2097152 | tf_op jit(solution)/shard_map/all_to_all | solution.py:66
  12.6 4.8 %copy-start.2 = (bf16[1,128,1024]{2,1,0:T(8,128)(2,1)S(1)}, bf16[1,128,1024]{2,1,0:T(8,128)(2,1)}, u32[]{:S(2)}) copy-start(bf16[1,128,1024]{2,1,0:T(8,128)(2,1)} %param.6) | copy-start | bytes 786436
  17.4 1.6 %copy-start.4 = (s32[4]{0:T(128)S(1)}, s32[4]{0:T(128)}, u32[]{:S(2)}) copy-start(s32[4]{0:T(128)} %param.11) | copy-start | bytes 52
  17.4 1.6 %copy-start.5 = (s32[4]{0:T(128)S(1)}, s32[4]{0:T(128)}, u32[]{:S(2)}) copy-start(s32[4]{0:T(128)} %param.10) | copy-start | bytes 52
  24.9 0.8 %copy-start.1 = (f32[2,128,512]{2,1,0:T(8,128)}, f32[2,128,512]{2,1,0:T(8,128)S(1)}, u32[]{:S(2)}) copy-start(f32[2,128,512]{2,1,0:T(8,128)S(1)} %convolution_bitcast_fusion) | copy-start | bytes 1572868
  26.8 9.6 %collective-permute-start.2 = (bf16[128,512]{1,0:T(8,128)(2,1)S(1)}, bf16[128,512]{1,0:T(8,128)(2,1)S(1)}, u32[]{:S(2)}, u32[]{:S(2)}) collective-permute-start(bf16[128,512]{1,0:T(8,128)(2,1)S(1)} %multiply_convert_fusion.1), channel_id=1, source_target_pairs={{0,4},{4,0},{1,5},{5,1},{2,6},{6,2},{3,7},{7,3},{8,12},{12,8},{9,1... | collective-permute-start | bytes 393224 | tf_op jit(solution)/shard_map/ppermute | solution.py:86
  30.8 5.3 %collective-permute-start.1 = (bf16[128,512]{1,0:T(8,128)(2,1)S(1)}, bf16[128,512]{1,0:T(8,128)(2,1)S(1)}, u32[]{:S(2)}, u32[]{:S(2)}) collective-permute-start(bf16[128,512]{1,0:T(8,128)(2,1)S(1)} %bitcast.68), channel_id=1, source_target_pairs={{0,4},{4,0},{1,5},{5,1},{2,6},{6,2},{3,7},{7,3},{8,12},{12,8},{9,1... | collective-permute-start | bytes 393224 | tf_op jit(solution)/shard_map/ppermute | solution.py:90
  31.0 5.5 %copy-start.3 = (f32[1024]{0:T(1024)S(1)}, f32[1024]{0:T(1024)}, u32[]{:S(2)}) copy-start(f32[1024]{0:T(1024)} %param.9) | copy-start | bytes 12292

commit v17 on v14

--- a/solution.py
+++ b/solution.py
@@ -8,7 +8,7 @@
 HEAD_SIZE = D // HEADS
 
 
-def attend(qheads, keys, values, count):
+def attend(qheads, keys, values, positions, count):
     inverse = HEAD_SIZE ** (-0.5)
     local_heads, rows, _ = qheads.shape
     total = keys.shape[1]
@@ -23,7 +23,7 @@
             jnp.einsum("hcd,hkd->hck", qheads, key_block, preferred_element_type=jnp.float32)
             * inverse
         )
-        live = (start + jnp.arange(block) < count).astype(jnp.float32)
+        live = (lax.dynamic_slice_in_dim(positions, start, block) < count).astype(jnp.float32)
         weights = (jax.nn.silu(scores) * live[None, None, :] / scale_count).astype(jnp.bfloat16)
         part_sum = jnp.einsum(
             "hck,hkd->chd", weights, value_block, preferred_element_type=jnp.float32
@@ -59,14 +59,31 @@
     ordered = kv_store.at[users].get(mode="promise_in_bounds", unique_indices=True).reshape(
         n_users, n_pos, 2, n_blk, local_heads, HEAD_SIZE
     )
-    ordered = jnp.transpose(ordered, (3, 0, 2, 4, 1, 5)).reshape(
-        n_blk * n_users, 2, local_heads, n_pos, HEAD_SIZE
-    )
-    fetched = lax.all_to_all(
-        ordered, ("blk", "store"), split_axis=0, concat_axis=3, tiled=True
-    )
-    keys = fetched[0, 0]
-    values = fetched[0, 1]
+    group = n_blk * n_users
+    if group <= 8:
+        ordered = jnp.transpose(ordered, (0, 3, 2, 4, 1, 5)).reshape(
+            group, 2, local_heads, n_pos, HEAD_SIZE
+        )
+        me = slot * n_blk + blk
+        rotated = jnp.roll(ordered, -me, axis=0)
+        pieces = [rotated[0]]
+        for k in range(1, group):
+            shift = [(i, (i + k) % group) for i in range(group)]
+            pieces.append(lax.ppermute(rotated[k], ("store", "blk"), shift))
+        fetched = jnp.stack(pieces, axis=2).reshape(2, local_heads, group * n_pos, HEAD_SIZE)
+        sender = (me - jnp.arange(group, dtype=jnp.int32)) % group
+        source = (sender % n_blk) * n_users + sender // n_blk
+    else:
+        ordered = jnp.transpose(ordered, (3, 0, 2, 4, 1, 5)).reshape(
+            group, 2, local_heads, n_pos, HEAD_SIZE
+        )
+        fetched = lax.all_to_all(
+            ordered, ("blk", "store"), split_axis=0, concat_axis=3, tiled=True
+        )[0]
+        source = jnp.arange(group, dtype=jnp.int32)
+    positions = (source[:, None] * n_pos + jnp.arange(n_pos, dtype=jnp.int32)[None, :]).reshape(-1)
+    keys = fetched[0]
+    values = fetched[1]
 
     mine = cands[0]
     rows = mine.shape[0]
@@ -83,9 +100,9 @@
         query_own, gate_own = project(mine)
         query_peer, gate_peer = project(peer)
         gate_back = lax.ppermute(gate_peer, "blk", swap)
-        sent = attend(query_peer, keys, values, count).astype(jnp.bfloat16)
+        sent = attend(query_peer, keys, values, positions, count).astype(jnp.bfloat16)
         back = lax.ppermute(sent, "blk", swap)
-        kept = attend(query_own, keys, values, count).astype(jnp.bfloat16)
+        kept = attend(query_own, keys, values, positions, count).astype(jnp.bfloat16)
         first = blk == 0
         attended = jnp.where(first, jnp.concatenate([kept, back], axis=1),
                              jnp.concatenate([back, kept], axis=1))
@@ -95,7 +112,7 @@
 
     feats = lax.all_gather(mine, "blk", axis=0, tiled=True)
     query, gate = project(feats)
-    attended = attend(query, keys, values, count).astype(jnp.bfloat16)
+    attended = attend(query, keys, values, positions, count).astype(jnp.bfloat16)
     both = jnp.stack([attended, gate]).reshape(2, n_blk, rows, half)
     own = lax.all_to_all(both, "blk", split_axis=1, concat_axis=3, tiled=True)
     own = own.reshape(2, rows, n_blk * half)

time: 38 us -> 56.1 us (1.48)
  waiting for transfers between devices: 4.4 us -> 17.1 us
  local copies, waits for them, and re-layouts: 13.7 us -> 18.1 us
  matrix products: 4.61 us -> 6.27 us
  other arithmetic: 4.65 us -> 3.24 us
  starting transfers between devices: 9.38 us -> 10.1 us
    ppermute x0 -> x7, waiting for transfers between devices: none -> 13.2 us  [per_device(): pieces.append(lax.ppermute(rotated[k], ('store', 'blk'), shift))]
    ppermute x0 -> x7, starting transfers between devices: none -> 4.96 us  [per_device(): pieces.append(lax.ppermute(rotated[k], ('store', 'blk'), shift))]
    unnamed x13 -> x24, local copies, waits for them, and re-layouts: 5.58 us -> 10.3 us
    all_to_all x1 -> x0, starting transfers between devices: 4.24 us -> none  [per_device(): lax.all_to_all(ordered, ('blk', 'store'), split_axis=0, concat_axis=3, ti...]
    dot_general x2, matrix products: 1.45 us -> 3.91 us  [one_block(): jnp.einsum('hck,hkd->chd', weights, value_block, preferred_element_type=j...]
    convert_element_type x2, other arithmetic: 2.06 us -> 0.16 us  [project(): gate = jax.nn.silu(proj[1]).astype(jnp.bfloat16)]
    ppermute x1, waiting for transfers between devices: 4.39 us -> 2.79 us  [per_device(): back = lax.ppermute(sent, 'blk', swap)]
    all_to_all x1 -> x0, local copies, waits for them, and re-layouts: 1.31 us -> none  [per_device(): lax.all_to_all(ordered, ('blk', 'store'), split_axis=0, concat_axis=3, ti...]
  transfers between devices with their start and end apart: 4 -> 10, of which waited for: 1 -> 5; matrix products, arithmetic and copies ran while one was open for 56% -> 38% of each run, Pallas kernels for 0% -> 0%
where the time goes in v17:
time: 56.1 us; the launch traced here: 55.7 us
  local copies, waits for them, and re-layouts  18.1 us (32%)
  waiting for transfers between devices  17.1 us (30%)
  starting transfers between devices  10.1 us (18%)
  matrix products  6.27 us (11%)
  other arithmetic  3.24 us (6%)
  between operations  0.91 us (2%)
    ppermute x7, waiting for transfers between devices, per_device(): pieces.append(lax.ppermute(rotated[k], ('store', 'blk'), shift))  13.2 us
    unnamed x24, local copies, waits for them, and re-layouts  10.3 us
    ppermute x7, starting transfers between devices, per_device(): pieces.append(lax.ppermute(rotated[k], ('store', 'blk'), shift))  4.96 us
    dot_general x2, matrix products, one_block(): jnp.einsum('hck,hkd->chd', weights, value_block, preferred_element_type=j...  3.91 us
    ppermute x1, starting transfers between devices, per_device(): peer = lax.ppermute(mine, 'blk', swap)  2.97 us
    ppermute x1, waiting for transfers between devices, per_device(): back = lax.ppermute(sent, 'blk', swap)  2.79 us
    gather x1, local copies, waits for them, and re-layouts, per_device(): kv_store.at[users].get(mode='promise_in_bounds', unique_indices=True)  2.66 us
    dot_general x2, matrix products, project(): jnp.einsum('cd,dkh->kch', feats, proj_weight, preferred_element_type=jnp....  2.37 us
  transfers between devices with their start and end apart: 10, of which 5 were waited for; matrix products, arithmetic and copies ran while one was open for 38% of the time, Pallas kernels for 0%

profile of v17, /device:TPU:0, one launch (start us, length us, event | category | flops | bytes accessed | tf_op | source)
XLA Modules:
  0.0 55.7 jit_solution(1160047480993997505)
XLA Ops:
  0.0 0.0 copy-start
  0.0 3.0 %collective-permute-start.7 = (bf16[128,1024]{1,0:T(8,128)(2,1)}, bf16[128,1024]{1,0:T(8,128)(2,1)}, u32[]{:S(2)}, u32[]{:S(2)}) collective-permute-start(bf16[128,1024]{1,0:T(8,128)(2,1)} %bitcast.103), channel_id=1, source_target_pairs={{0,4},{4,0},{1,5},{5,1},{2,6},{6,2},{3,7},{7,3},{8,12},{12,8},{9,1... | collective-permute-start | bytes 786440 | tf_op jit(solution)/shard_map/ppermute | solution.py:99
  3.0 0.7 %compare_select_fusion = s32[4]{0:T(128)S(1)} fusion(s32[4]{0:T(128)} %param.10), kind=kLoop, calls=%fused_computation.56 | loop fusion | flops 12 | bytes 32 | tf_op jit(solution)/shard_map/select_n | solution.py:59
  3.6 0.0 copy-done
  3.6 2.7 %gather_fusion = bf16[4,64,2,1024]{3,2,1,0:T(2,128)(2,1)S(1)} fusion(bf16[4,64,2,1024]{3,2,1,0:T(2,128)(2,1)S(1)} %copy-done, s32[1024]{0:T(1024)S(1)} %pad_clamp_fusion), kind=kCustom, calls=%fused_computation | custom fusion | bytes 2097168 | tf_op jit(solution)/shard_map/gather | solution.py:59
  6.3 0.7 %reshape.287 = bf16[4,64,2,2,4,128]{5,4,3,2,1,0:T(4,128)(2,1)S(1)} reshape(bf16[4,64,2,1024]{3,2,1,0:T(2,128)(2,1)S(1)} %gather_fusion) | data formatting | bytes 2097152 | tf_op jit(solution)/shard_map/reshape | solution.py:59
  7.0 0.3 copy.36
  7.3 0.4 fusion
  7.7 0.0 copy-start.1
  7.7 1.0 %copy-done.1 = bf16[8,2,4,64,128]{4,3,2,1,0:T(8,128)(2,1)} copy-done((bf16[8,2,4,64,128]{4,3,2,1,0:T(8,128)(2,1)}, bf16[8,2,4,64,128]{4,3,2,1,0:T(8,128)(2,1)S(1)}, u32[]{:S(2)}) %copy-start.1) | copy-done | bytes 1048600
  8.7 0.9 %slice_bitcast_fusion.1 = (bf16[2,4,64,128]{3,2,1,0:T(8,128)(2,1)}, bf16[2,4,64,128]{3,2,1,0:T(8,128)(2,1)}, bf16[2,4,64,128]{3,2,1,0:T(8,128)(2,1)}, bf16[2,4,6...) fusion(bf16[8,2,4,64,128]{4,3,2,1,0:T(8,128)(2,1)S(1)} %fusion), kind=kLoop, calls=%fused_computation.35 | loop fusion | bytes 1835008 | tf_op jit(solution)/shard_map/squeeze | solution.py:72
  9.6 0.9 %collective-permute-start.6 = (bf16[2,4,64,128]{3,2,1,0:T(8,128)(2,1)}, bf16[2,4,64,128]{3,2,1,0:T(8,128)(2,1)}, u32[]{:S(2)}, u32[]{:S(2)}) collective-permute-start(bf16[2,4,64,128]{3,2,1,0:T(8,128)(2,1)} %get-tuple-element.7), channel_id=1, source_target_pairs={{0,28},{4,0},{8,4},{12,8},{16,12},{20,16},{24,20},{28,24},{1,29},{... | collective-permute-start | bytes 393224 | tf_op jit(solution)/shard_map/ppermute | solution.py:72
  10.5 0.8 %collective-permute-start.5 = (bf16[2,4,64,128]{3,2,1,0:T(8,128)(2,1)}, bf16[2,4,64,128]{3,2,1,0:T(8,128)(2,1)}, u32[]{:S(2)}, u32[]{:S(2)}) collective-permute-start(bf16[2,4,64,128]{3,2,1,0:T(8,128)(2,1)} %get-tuple-element.8), channel_id=1, source_target_pairs={{0,24},{4,28},{8,0},{12,4},{16,8},{20,12},{24,16},{28,20},{1,25},{... | collective-permute-start | bytes 393224 | tf_op jit(solution)/shard_map/ppermute | solution.py:72
  11.4 1.2 %collective-permute-start.4 = (bf16[2,4,64,128]{3,2,1,0:T(8,128)(2,1)}, bf16[2,4,64,128]{3,2,1,0:T(8,128)(2,1)}, u32[]{:S(2)}, u32[]{:S(2)}) collective-permute-start(bf16[2,4,64,128]{3,2,1,0:T(8,128)(2,1)} %get-tuple-element.9), channel_id=1, source_target_pairs={{0,20},{4,24},{8,28},{12,0},{16,4},{20,8},{24,12},{28,16},{1,21},{... | collective-permute-start | bytes 393224 | tf_op jit(solution)/shard_map/ppermute | solution.py:72
  12.6 0.3 collective-permute-start
  12.9 0.0 copy-start.4
  12.9 4.8 %copy.44 = bf16[1024,2,512]{0,2,1:T(8,128)(2,1)S(1)} copy(bf16[1024,2,512]{2,1,0:T(2,128)(2,1)} %param.8) | data formatting | bytes 4194304 | tf_op args[2]
  17.7 0.0 copy-done.4
  17.7 0.0 copy-start.6
  17.7 0.0 copy-start.7
  17.7 0.7 %convolution_bitcast_fusion.1 = f32[2,128,512]{1,2,0:T(8,128)S(1)} fusion(bf16[1024,2,512]{0,2,1:T(8,128)(2,1)S(1)} %copy.44, bf16[1,128,1024]{2,1,0:T(8,128)(2,1)S(1)} %copy-done.4), kind=kOutput, calls=%fused_computation.6 | convolution fusion | flops 268435456 | bytes 2883584 | tf_op jit(solution)/shard_map/cd,dkh->kch/dot_general | solution.py:92
  18.4 0.1 multiply_convert_fusion.2
  18.5 0.0 copy-done.6
  18.5 0.0 copy-done.7
  18.5 0.7 %select_reduce_fusion = s32[]{:T(128)} fusion(s32[4]{0:T(128)S(1)} %copy-done.7, s32[4]{0:T(128)S(1)} %copy-done.6, pred[4]{0:T(512)(128)(4,1)S(1)} %iota_compare_fusion.1), kind=kLoop, calls=%fused_computation.59 | loop fusion | flops 63 | bytes 40 | tf_op jit(solution)/shard_map/reduce_sum | solution.py:54
  19.9 0.7 %fusion.18 = f32[8,64]{1,0:T(8,128)S(1)} fusion(s32[]{:T(128)} %select_reduce_fusion, s32[8]{0:T(128)S(1)} %fusion.23), kind=kLoop, calls=%fused_computation.55 | loop fusion | flops 1536 | bytes 2084 | tf_op jit(solution)/shard_map/convert_element_type | solution.py:26
  20.6 0.1 reshape.289
  20.7 0.1 copy.45
  20.8 0.9 %fusion.13 = bf16[2,4,8,64,128]{4,3,2,1,0:T(8,128)(2,1)S(1)} fusion(bf16[8,2,4,64,128]{4,3,2,1,0:T(8,128)(2,1)} %copy-done.1), kind=kLoop, calls=%fused_computation.43 | loop fusion | bytes 262144
  21.8 0.0 collective-permute-done
  21.8 0.4 collective-permute-start.1
  22.2 0.9 %bitcast_dynamic-update-slice_fusion.5 = bf16[2,4,8,64,128]{4,3,2,1,0:T(8,128)(2,1)S(1)} fusion(bf16[2,4,8,64,128]{4,3,2,1,0:T(8,128)(2,1)S(1)} %fusion.13, bf16[2,4,64,128]{3,2,1,0:T(8,128)(2,1)} %collective-permute-done), kind=kLoop, calls=%fused_computation.49 | loop fusion | bytes 262144
  23.1 3.3 %collective-permute-done.1 = bf16[2,4,64,128]{3,2,1,0:T(8,128)(2,1)S(1)} collective-permute-done((bf16[2,4,64,128]{3,2,1,0:T(8,128)(2,1)}, bf16[2,4,64,128]{3,2,1,0:T(8,128)(2,1)S(1)}, u32[]{:S(2)}, u32[]{:S(2)}) %collective-permute-start.1) | collective-permute-done | bytes 131104 | tf_op jit(solution)/shard_map/ppermute | solution.py:72
  26.4 0.0 collective-permute-start.2
  26.4 6.1 %collective-permute-done.2 = bf16[2,4,64,128]{3,2,1,0:T(8,128)(2,1)S(1)} collective-permute-done((bf16[2,4,64,128]{3,2,1,0:T(8,128)(2,1)}, bf16[2,4,64,128]{3,2,1,0:T(8,128)(2,1)S(1)}, u32[]{:S(2)}, u32[]{:S(2)}) %collective-permute-start.2) | collective-permute-done | bytes 131104 | tf_op jit(solution)/shard_map/ppermute | solution.py:72
  32.5 1.3 %collective-permute-start.3 = (bf16[2,4,64,128]{3,2,1,0:T(8,128)(2,1)}, bf16[2,4,64,128]{3,2,1,0:T(8,128)(2,1)S(1)}, u32[]{:S(2)}, u32[]{:S(2)}) collective-permute-start(bf16[2,4,64,128]{3,2,1,0:T(8,128)(2,1)} %get-tuple-element.10), channel_id=1, source_target_pairs={{0,16},{4,20},{8,24},{12,28},{16,0},{20,4},{24,8},{28,12},{1,17},{... | collective-permute-start | bytes 393224 | tf_op jit(solution)/shard_map/ppermute | solution.py:72
  33.8 3.9 %collective-permute-done.3 = bf16[2,4,64,128]{3,2,1,0:T(8,128)(2,1)S(1)} collective-permute-done((bf16[2,4,64,128]{3,2,1,0:T(8,128)(2,1)}, bf16[2,4,64,128]{3,2,1,0:T(8,128)(2,1)S(1)}, u32[]{:S(2)}, u32[]{:S(2)}) %collective-permute-start.3) | collective-permute-done | bytes 131104 | tf_op jit(solution)/shard_map/ppermute | solution.py:72
  37.7 0.0 collective-permute-done.4
  37.7 0.9 %bitcast_dynamic-update-slice_fusion.1 = bf16[2,4,8,64,128]{4,3,2,1,0:T(8,128)(2,1)S(1)} fusion(bf16[2,4,8,64,128]{4,3,2,1,0:T(8,128)(2,1)S(1)} %bitcast_dynamic-update-slice_fusion.2, bf16[2,4,64,128]{3,2,1,0:T(8,128)(2,1)} %collective-permute-done.4), kind=kLoop, calls=%fused_computation.45 | loop fusion | bytes 262144
  38.6 0.0 collective-permute-done.5
  38.6 0.9 %bitcast_dynamic-update-slice_fusion = bf16[2,4,8,64,128]{4,3,2,1,0:T(8,128)(2,1)S(1)} fusion(bf16[2,4,8,64,128]{4,3,2,1,0:T(8,128)(2,1)S(1)} %bitcast_dynamic-update-slice_fusion.1, bf16[2,4,64,128]{3,2,1,0:T(8,128)(2,1)} %collective-permute-done.5), kind=kLoop, calls=%fused_computation.44 | loop fusion | bytes 262144
  39.6 0.0 collective-permute-done.6
  39.6 0.9 %bitcast_dynamic-update-slice_fusion.6 = bf16[2,4,8,64,128]{4,3,2,1,0:T(8,128)(2,1)S(1)} fusion(bf16[2,4,8,64,128]{4,3,2,1,0:T(8,128)(2,1)S(1)} %bitcast_dynamic-update-slice_fusion, bf16[2,4,64,128]{3,2,1,0:T(8,128)(2,1)} %collective-permute-done.6), kind=kLoop, calls=%fused_computation.52 | loop fusion | bytes 262144 | tf_op jit(solution)/shard_map/stack | solution.py:73
  40.5 1.1 %fusion.28 = (bf16[1,4,8,64,128]{4,3,2,1,0:T(8,128)(2,1)}, bf16[1,4,8,64,128]{4,3,2,1,0:T(8,128)(2,1)}) fusion(bf16[2,4,8,64,128]{4,3,2,1,0:T(8,128)(2,1)S(1)} %bitcast_dynamic-update-slice_fusion.6), kind=kLoop, calls=%fused_computation.79 | loop fusion | bytes 2097152 | tf_op jit(solution)/shard_map/slice | solution.py:85
  41.6 1.9 %convolution_convert_fusion.1 = bf16[4,128,128]{2,1,0:T(8,128)(2,1)S(1)} fusion(bf16[4,512,128]{2,1,0:T(8,128)(2,1)} %bitcast.101, bf16[4,512,128]{2,1,0:T(8,128)(2,1)} %bitcast.99, f32[]{:T(128)S(6)} %convert_element_type.100, f32[512]{0:T(512)S(1)} %reshape.289, bf16[128,4,128]{2,0,1:T(8,128)(2,1)S(1)} %copy.45), kind=kOutput, calls=%fused_computation.8 | convolution fusion | flops 136380416 | bytes 1312772 | tf_op jit(solution)/shard_map/hck,hkd->chd/dot_general | solution.py:28
  43.5 0.0 collective-permute-done.7
  43.5 1.7 %convolution_bitcast_fusion = f32[2,128,512]{1,2,0:T(8,128)S(1)} fusion(bf16[1024,2,512]{0,2,1:T(8,128)(2,1)S(1)} %copy.44, bf16[128,1024]{1,0:T(8,128)(2,1)} %collective-permute-done.7), kind=kOutput, calls=%fused_computation.5 | convolution fusion | flops 268435456 | bytes 2883584 | tf_op jit(solution)/shard_map/cd,dkh->kch/dot_general | solution.py:92
  45.2 0.0 copy-start.2
  45.2 0.8 %copy-done.2 = f32[2,128,512]{1,2,0:T(8,128)} copy-done((f32[2,128,512]{1,2,0:T(8,128)}, f32[2,128,512]{1,2,0:T(8,128)S(1)}, u32[]{:S(2)}) %copy-start.2) | copy-done | bytes 524312
  46.0 0.1 copy.48
  46.2 0.0 copy-start.3
  46.2 0.0 copy-start.5
  46.2 2.0 %convolution_convert_fusion = bf16[4,128,128]{2,1,0:T(8,128)(2,1)S(1)} fusion(bf16[4,512,128]{2,1,0:T(8,128)(2,1)} %bitcast.102, bf16[4,512,128]{2,1,0:T(8,128)(2,1)} %bitcast.100, f32[]{:T(128)S(6)} %convert_element_type.100, f32[512]{0:T(512)S(1)} %reshape.289, bf16[128,4,128]{2,0,1:T(8,128)(2,1)S(1)} %copy.48), kind=kOutput, calls=%fused_computation.7 | convolution fusion | flops 136380416 | bytes 1312772 | tf_op jit(solution)/shard_map/hck,hkd->chd/dot_general | solution.py:28
  48.2 1.1 %collective-permute-start.8 = (bf16[128,512]{0,1:T(8,128)(2,1)S(1)}, bf16[128,512]{0,1:T(8,128)(2,1)S(1)}, u32[]{:S(2)}, u32[]{:S(2)}) collective-permute-start(bf16[128,512]{0,1:T(8,128)(2,1)S(1)} %bitcast.105), channel_id=1, source_target_pairs={{0,4},{4,0},{1,5},{5,1},{2,6},{6,2},{3,7},{7,3},{8,12},{12,8},{9,1... | collective-permute-start | bytes 393224 | tf_op jit(solution)/shard_map/ppermute | solution.py:104
  49.3 0.0 copy-done.3
  49.3 0.1 multiply_convert_fusion.1
  49.4 1.1 %collective-permute-start.9 = (bf16[128,512]{0,1:T(8,128)(2,1)S(1)}, bf16[128,512]{0,1:T(8,128)(2,1)S(1)}, u32[]{:S(2)}, u32[]{:S(2)}) collective-permute-start(bf16[128,512]{0,1:T(8,128)(2,1)S(1)} %multiply_convert_fusion.1), channel_id=1, source_target_pairs={{0,4},{4,0},{1,5},{5,1},{2,6},{6,2},{3,7},{7,3},{8,12},{12,8},{9,1... | collective-permute-start | bytes 393224 | tf_op jit(solution)/shard_map/ppermute | solution.py:102
  50.4 2.8 %collective-permute-done.8 = bf16[128,512]{0,1:T(8,128)(2,1)S(1)} collective-permute-done((bf16[128,512]{0,1:T(8,128)(2,1)S(1)}, bf16[128,512]{0,1:T(8,128)(2,1)S(1)}, u32[]{:S(2)}, u32[]{:S(2)}) %collective-permute-start.8) | collective-permute-done | bytes 131104 | tf_op jit(solution)/shard_map/ppermute | solution.py:104
  53.2 0.2 convert_reduce_fusion
  53.4 0.2 fusion.2
  53.6 1.1 %collective-permute-done.9 = bf16[128,512]{0,1:T(8,128)(2,1)S(1)} collective-permute-done((bf16[128,512]{0,1:T(8,128)(2,1)S(1)}, bf16[128,512]{0,1:T(8,128)(2,1)S(1)}, u32[]{:S(2)}, u32[]{:S(2)}) %collective-permute-start.9) | collective-permute-done | bytes 131104 | tf_op jit(solution)/shard_map/ppermute | solution.py:102
  54.6 0.0 copy-done.5
  54.6 0.2 multiply_convert_fusion
  54.8 0.9 %copy.50 = bf16[1,128,1024]{2,1,0:T(8,128)(2,1)} copy(bf16[1,128,1024]{1,2,0:T(8,128)(2,1)S(1)} %multiply_convert_fusion) | data formatting | bytes 524288 | tf_op jit(solution)/shard_map/convert_element_type | solution.py:45
  (10 shorter events, 0.1 us)
Async XLA Ops:
  0.0 3.6 %copy-start = (bf16[4,64,2,1024]{3,2,1,0:T(2,128)(2,1)S(1)}, bf16[4,64,2,1024]{3,2,1,0:T(2,128)(2,1)}, u32[]{:S(2)}) copy-start(bf16[4,64,2,1024]{3,2,1,0:T(2,128)(2,1)} %param.7) | copy-start | bytes 3145732
  0.0 43.5 %collective-permute-start.7 = (bf16[128,1024]{1,0:T(8,128)(2,1)}, bf16[128,1024]{1,0:T(8,128)(2,1)}, u32[]{:S(2)}, u32[]{:S(2)}) collective-permute-start(bf16[128,1024]{1,0:T(8,128)(2,1)} %bitcast.103), channel_id=1, source_target_pairs={{0,4},{4,0},{1,5},{5,1},{2,6},{6,2},{3,7},{7,3},{8,12},{12,8},{9,1... | collective-permute-start | bytes 786440 | tf_op jit(solution)/shard_map/ppermute | solution.py:99
  7.7 1.0 %copy-start.1 = (bf16[8,2,4,64,128]{4,3,2,1,0:T(8,128)(2,1)}, bf16[8,2,4,64,128]{4,3,2,1,0:T(8,128)(2,1)S(1)}, u32[]{:S(2)}) copy-start(bf16[8,2,4,64,128]{4,3,2,1,0:T(8,128)(2,1)S(1)} %fusion) | copy-start | bytes 3145732
  9.6 30.0 %collective-permute-start.6 = (bf16[2,4,64,128]{3,2,1,0:T(8,128)(2,1)}, bf16[2,4,64,128]{3,2,1,0:T(8,128)(2,1)}, u32[]{:S(2)}, u32[]{:S(2)}) collective-permute-start(bf16[2,4,64,128]{3,2,1,0:T(8,128)(2,1)} %get-tuple-element.7), channel_id=1, source_target_pairs={{0,28},{4,0},{8,4},{12,8},{16,12},{20,16},{24,20},{28,24},{1,29},{... | collective-permute-start | bytes 393224 | tf_op jit(solution)/shard_map/ppermute | solution.py:72
  10.5 28.1 %collective-permute-start.5 = (bf16[2,4,64,128]{3,2,1,0:T(8,128)(2,1)}, bf16[2,4,64,128]{3,2,1,0:T(8,128)(2,1)}, u32[]{:S(2)}, u32[]{:S(2)}) collective-permute-start(bf16[2,4,64,128]{3,2,1,0:T(8,128)(2,1)} %get-tuple-element.8), channel_id=1, source_target_pairs={{0,24},{4,28},{8,0},{12,4},{16,8},{20,12},{24,16},{28,20},{1,25},{... | collective-permute-start | bytes 393224 | tf_op jit(solution)/shard_map/ppermute | solution.py:72
  11.4 26.3 %collective-permute-start.4 = (bf16[2,4,64,128]{3,2,1,0:T(8,128)(2,1)}, bf16[2,4,64,128]{3,2,1,0:T(8,128)(2,1)}, u32[]{:S(2)}, u32[]{:S(2)}) collective-permute-start(bf16[2,4,64,128]{3,2,1,0:T(8,128)(2,1)} %get-tuple-element.9), channel_id=1, source_target_pairs={{0,20},{4,24},{8,28},{12,0},{16,4},{20,8},{24,12},{28,16},{1,21},{... | collective-permute-start | bytes 393224 | tf_op jit(solution)/shard_map/ppermute | solution.py:72
  12.6 9.2 %collective-permute-start = (bf16[2,4,64,128]{3,2,1,0:T(8,128)(2,1)}, bf16[2,4,64,128]{3,2,1,0:T(8,128)(2,1)}, u32[]{:S(2)}, u32[]{:S(2)}) collective-permute-start(bf16[2,4,64,128]{3,2,1,0:T(8,128)(2,1)} %get-tuple-element.13), channel_id=1, source_target_pairs={{0,4},{4,8},{8,12},{12,16},{16,20},{20,24},{24,28},{28,0},{1,5},{5... | collective-permute-start | bytes 393224 | tf_op jit(solution)/shard_map/ppermute | solution.py:72
  12.9 4.8 %copy-start.4 = (bf16[1,128,1024]{2,1,0:T(8,128)(2,1)S(1)}, bf16[1,128,1024]{2,1,0:T(8,128)(2,1)}, u32[]{:S(2)}) copy-start(bf16[1,128,1024]{2,1,0:T(8,128)(2,1)} %param.6) | copy-start | bytes 786436
  17.7 0.9 %copy-start.6 = (s32[4]{0:T(128)S(1)}, s32[4]{0:T(128)}, u32[]{:S(2)}) copy-start(s32[4]{0:T(128)} %param.10) | copy-start | bytes 52
  17.7 0.9 %copy-start.7 = (s32[4]{0:T(128)S(1)}, s32[4]{0:T(128)}, u32[]{:S(2)}) copy-start(s32[4]{0:T(128)} %param.11) | copy-start | bytes 52
  21.8 4.7 %collective-permute-start.1 = (bf16[2,4,64,128]{3,2,1,0:T(8,128)(2,1)}, bf16[2,4,64,128]{3,2,1,0:T(8,128)(2,1)S(1)}, u32[]{:S(2)}, u32[]{:S(2)}) collective-permute-start(bf16[2,4,64,128]{3,2,1,0:T(8,128)(2,1)} %get-tuple-element.12), channel_id=1, source_target_pairs={{0,8},{4,12},{8,16},{12,20},{16,24},{20,28},{24,0},{28,4},{1,9},{5... | collective-permute-start | bytes 393224 | tf_op jit(solution)/shard_map/ppermute | solution.py:72
  26.4 6.1 %collective-permute-start.2 = (bf16[2,4,64,128]{3,2,1,0:T(8,128)(2,1)}, bf16[2,4,64,128]{3,2,1,0:T(8,128)(2,1)S(1)}, u32[]{:S(2)}, u32[]{:S(2)}) collective-permute-start(bf16[2,4,64,128]{3,2,1,0:T(8,128)(2,1)} %get-tuple-element.11), channel_id=1, source_target_pairs={{0,12},{4,16},{8,20},{12,24},{16,28},{20,0},{24,4},{28,8},{1,13},{... | collective-permute-start | bytes 393224 | tf_op jit(solution)/shard_map/ppermute | solution.py:72
  32.5 5.2 %collective-permute-start.3 = (bf16[2,4,64,128]{3,2,1,0:T(8,128)(2,1)}, bf16[2,4,64,128]{3,2,1,0:T(8,128)(2,1)S(1)}, u32[]{:S(2)}, u32[]{:S(2)}) collective-permute-start(bf16[2,4,64,128]{3,2,1,0:T(8,128)(2,1)} %get-tuple-element.10), channel_id=1, source_target_pairs={{0,16},{4,20},{8,24},{12,28},{16,0},{20,4},{24,8},{28,12},{1,17},{... | collective-permute-start | bytes 393224 | tf_op jit(solution)/shard_map/ppermute | solution.py:72
  45.2 0.8 %copy-start.2 = (f32[2,128,512]{1,2,0:T(8,128)}, f32[2,128,512]{1,2,0:T(8,128)S(1)}, u32[]{:S(2)}) copy-start(f32[2,128,512]{1,2,0:T(8,128)S(1)} %convolution_bitcast_fusion) | copy-start | bytes 1572868
  46.2 3.1 %copy-start.3 = (f32[2,128,512]{1,2,0:T(8,128)S(1)}, f32[2,128,512]{1,2,0:T(8,128)}, u32[]{:S(2)}) copy-start(f32[2,128,512]{1,2,0:T(8,128)} %copy-done.2) | copy-start | bytes 1572868
  46.2 8.4 %copy-start.5 = (f32[1024]{0:T(1024)S(1)}, f32[1024]{0:T(1024)}, u32[]{:S(2)}) copy-start(f32[1024]{0:T(1024)} %param.9) | copy-start | bytes 12292
  48.2 5.0 %collective-permute-start.8 = (bf16[128,512]{0,1:T(8,128)(2,1)S(1)}, bf16[128,512]{0,1:T(8,128)(2,1)S(1)}, u32[]{:S(2)}, u32[]{:S(2)}) collective-permute-start(bf16[128,512]{0,1:T(8,128)(2,1)S(1)} %bitcast.105), channel_id=1, source_target_pairs={{0,4},{4,0},{1,5},{5,1},{2,6},{6,2},{3,7},{7,3},{8,12},{12,8},{9,1... | collective-permute-start | bytes 393224 | tf_op jit(solution)/shard_map/ppermute | solution.py:104
  49.4 5.3 %collective-permute-start.9 = (bf16[128,512]{0,1:T(8,128)(2,1)S(1)}, bf16[128,512]{0,1:T(8,128)(2,1)S(1)}, u32[]{:S(2)}, u32[]{:S(2)}) collective-permute-start(bf16[128,512]{0,1:T(8,128)(2,1)S(1)} %multiply_convert_fusion.1), channel_id=1, source_target_pairs={{0,4},{4,0},{1,5},{5,1},{2,6},{6,2},{3,7},{7,3},{8,12},{12,8},{9,1... | collective-permute-start | bytes 393224 | tf_op jit(solution)/shard_map/ppermute | solution.py:102

commit v18 on v14

--- a/solution.py
+++ b/solution.py
@@ -56,7 +56,15 @@
     local_heads = half // HEAD_SIZE
 
     n_users, n_pos = kv_store.shape[0], kv_store.shape[1]
-    ordered = kv_store.at[users].get(mode="promise_in_bounds", unique_indices=True).reshape(
+    ordered = lax.gather(
+        kv_store, users[:, None],
+        lax.GatherDimensionNumbers(
+            offset_dims=(1, 2, 3), collapsed_slice_dims=(0,), start_index_map=(0,)
+        ),
+        (1,) + kv_store.shape[1:],
+        unique_indices=True,
+        mode=lax.GatherScatterMode.PROMISE_IN_BOUNDS,
+    ).reshape(
         n_users, n_pos, 2, n_blk, local_heads, HEAD_SIZE
     )
     ordered = jnp.transpose(ordered, (3, 0, 2, 4, 1, 5)).reshape(

time: 38 us -> 38 us (level)
    select_n x1 -> x0, other arithmetic: 0.66 us -> none  [per_device(): kv_store.at[users].get(mode='promise_in_bounds', unique_indices=True)]
    gather x1, other arithmetic: 0.01 us -> 0.66 us  [per_device(): lax.gather(kv_store, users[:, None], lax.GatherDimensionNumbers(offset_di...]
where the time goes in v18:
time: 38 us; the launch traced here: 37.5 us
  local copies, waits for them, and re-layouts  13.7 us (36%)
  starting transfers between devices  9.37 us (25%)
  other arithmetic  4.64 us (12%)
  matrix products  4.61 us (12%)
  waiting for transfers between devices  4.4 us (12%)
  between operations  0.84 us (2%)
    unnamed x13, local copies, waits for them, and re-layouts  5.58 us
    ppermute x1, waiting for transfers between devices, per_device(): back = lax.ppermute(sent, 'blk', swap)  4.4 us
    all_to_all x1, starting transfers between devices, per_device(): lax.all_to_all(ordered, ('blk', 'store'), split_axis=0, concat_axis=3, ti...  4.24 us
    dot_general x2, matrix products, project(): jnp.einsum('cd,dkh->kch', feats, proj_weight, preferred_element_type=jnp....  3.16 us
    ppermute x1, starting transfers between devices, per_device(): peer = lax.ppermute(mine, 'blk', swap)  2.97 us
    gather x1, local copies, waits for them, and re-layouts, per_device(): lax.gather(kv_store, users[:, None], lax.GatherDimensionNumbers(offset_di...  2.66 us
    convert_element_type x2, other arithmetic, project(): gate = jax.nn.silu(proj[1]).astype(jnp.bfloat16)  2.06 us
    reshape x2, local copies, waits for them, and re-layouts, per_device(): ordered = lax.gather(kv_store, users[:, None], lax.GatherDimensionNumbers...  2.02 us
  transfers between devices with their start and end apart: 4, of which 1 were waited for; matrix products, arithmetic and copies ran while one was open for 56% of the time, Pallas kernels for 0%

profile of v18, /device:TPU:0, one launch (start us, length us, event | category | flops | bytes accessed | tf_op | source)
XLA Modules:
  0.0 37.5 jit_solution(869489031116034007)
XLA Ops:
  0.0 0.0 copy-start
  0.0 3.0 %collective-permute-start = (bf16[128,1024]{1,0:T(8,128)(2,1)}, bf16[128,1024]{1,0:T(8,128)(2,1)}, u32[]{:S(2)}, u32[]{:S(2)}) collective-permute-start(bf16[128,1024]{1,0:T(8,128)(2,1)} %bitcast.62), channel_id=1, source_target_pairs={{0,4},{4,0},{1,5},{5,1},{2,6},{6,2},{3,7},{7,3},{8,12},{12,8},{9,1... | collective-permute-start | bytes 786440 | tf_op jit(solution)/shard_map/ppermute | solution.py:90
  3.0 0.7 %pad_clamp_fusion = s32[1024]{0:T(1024)S(1)} fusion(s32[4]{0:T(128)} %param.10), kind=kLoop, calls=%fused_computation.36 | loop fusion | flops 1024 | bytes 4112 | tf_op jit(solution)/shard_map/gather | solution.py:59
  3.6 0.0 copy-done
  3.6 2.7 %gather_fusion = bf16[4,64,2,1024]{3,2,1,0:T(2,128)(2,1)S(1)} fusion(bf16[4,64,2,1024]{3,2,1,0:T(2,128)(2,1)S(1)} %copy-done, s32[1024]{0:T(1024)S(1)} %pad_clamp_fusion), kind=kCustom, calls=%fused_computation | custom fusion | bytes 2097168 | tf_op jit(solution)/shard_map/gather | solution.py:59
  6.3 0.7 %reshape.223 = bf16[4,64,2,2,4,128]{5,4,3,2,1,0:T(4,128)(2,1)S(1)} reshape(bf16[4,64,2,1024]{3,2,1,0:T(2,128)(2,1)S(1)} %gather_fusion) | data formatting | bytes 2097152 | tf_op jit(solution)/shard_map/reshape | solution.py:67
  7.0 1.3 %copy.24 = bf16[4,64,2,2,4,128]{5,1,4,2,0,3:T(8,128)(2,1)} copy(bf16[4,64,2,2,4,128]{5,4,3,2,1,0:T(4,128)(2,1)S(1)} %reshape.223) | data formatting | bytes 2097152 | tf_op jit(solution)/shard_map/reshape | solution.py:67
  8.3 4.2 %all-to-all-start = ((bf16[8,2,4,64,128]{4,3,2,1,0:T(8,128)(2,1)}), bf16[8,2,4,64,128]{4,3,2,1,0:T(8,128)(2,1)}, u32[]{:S(2)}, u32[]{:S(2)}) async-start(bf16[8,2,4,64,128]{4,3,2,1,0:T(8,128)(2,1)} %bitcast.1), calls=%async_computation | async-start | bytes 2097152 | tf_op jit(solution)/shard_map/all_to_all | solution.py:73
  12.6 0.0 copy-start.2
  12.6 4.8 %copy.26 = bf16[1024,2,512]{0,2,1:T(8,128)(2,1)S(1)} copy(bf16[1024,2,512]{2,1,0:T(2,128)(2,1)} %param.8) | data formatting | bytes 4194304 | tf_op args[2]
  17.4 0.0 copy-done.2
  17.4 0.0 copy-start.4
  17.4 0.0 copy-start.5
  17.4 1.5 %convolution_bitcast_fusion.1 = f32[2,128,512]{1,2,0:T(8,128)} fusion(bf16[1024,2,512]{0,2,1:T(8,128)(2,1)S(1)} %copy.26, bf16[1,128,1024]{2,1,0:T(8,128)(2,1)S(1)} %copy-done.2), kind=kOutput, calls=%fused_computation.4 | convolution fusion | flops 268435456 | bytes 2883584 | tf_op jit(solution)/shard_map/cd,dkh->kch/dot_general | solution.py:83
  18.9 0.0 copy-done.4
  18.9 0.0 copy-done.5
  18.9 0.7 %select_reduce_fusion = s32[]{:T(128)} fusion(s32[4]{0:T(128)S(1)} %copy-done.5, s32[4]{0:T(128)S(1)} %copy-done.4, pred[4]{0:T(512)(128)(4,1)S(1)} %iota_compare_fusion.2), kind=kLoop, calls=%fused_computation.37 | loop fusion | flops 63 | bytes 40 | tf_op jit(solution)/shard_map/reduce_sum | solution.py:54
  19.6 0.6 %fusion.16 = f32[512]{0:T(512)S(1)} fusion(s32[]{:T(128)} %select_reduce_fusion), kind=kLoop, calls=%fused_computation.40 | loop fusion | flops 1024 | bytes 2052 | tf_op jit(solution)/shard_map/convert_element_type | solution.py:26
  20.9 1.0 %slice.49 = bf16[1,128,512]{1,2,0:T(8,128)(2,1)S(1)} slice(f32[2,128,512]{1,2,0:T(8,128)} %convolution_bitcast_fusion.1), slice={[0:1], [0:128], [0:512]} | slice | bytes 262144 | tf_op jit(solution)/shard_map/slice | solution.py:84
  21.9 0.1 copy.27
  22.0 1.0 %multiply_convert_fusion.2 = bf16[1,128,512]{1,2,0:T(8,128)(2,1)S(1)} fusion(f32[2,128,512]{1,2,0:T(8,128)} %convolution_bitcast_fusion.1), kind=kLoop, calls=%fused_computation.33 | loop fusion | flops 327680 | bytes 393216 | tf_op jit(solution)/shard_map/convert_element_type | solution.py:85
  23.1 0.0 collective-permute-done
  23.1 1.7 %convolution_bitcast_fusion = f32[2,128,512]{1,2,0:T(8,128)S(1)} fusion(bf16[1024,2,512]{0,2,1:T(8,128)(2,1)S(1)} %copy.26, bf16[128,1024]{1,0:T(8,128)(2,1)} %collective-permute-done), kind=kOutput, calls=%fused_computation.3 | convolution fusion | flops 268435456 | bytes 2883584 | tf_op jit(solution)/shard_map/cd,dkh->kch/dot_general | solution.py:83
  24.7 0.0 copy-start.1
  24.8 0.8 %copy-done.1 = f32[2,128,512]{1,2,0:T(8,128)} copy-done((f32[2,128,512]{1,2,0:T(8,128)}, f32[2,128,512]{1,2,0:T(8,128)S(1)}, u32[]{:S(2)}) %copy-start.1) | copy-done | bytes 524312
  25.6 0.1 copy.30
  25.7 1.0 %multiply_convert_fusion.1 = bf16[128,512]{0,1:T(8,128)(2,1)S(1)} fusion(f32[2,128,512]{1,2,0:T(8,128)} %copy-done.1), kind=kLoop, calls=%fused_computation.32 | loop fusion | flops 327680 | bytes 393216 | tf_op jit(solution)/shard_map/convert_element_type | solution.py:85
  26.7 2.0 %collective-permute-start.2 = (bf16[128,512]{0,1:T(8,128)(2,1)S(1)}, bf16[128,512]{0,1:T(8,128)(2,1)S(1)}, u32[]{:S(2)}, u32[]{:S(2)}) collective-permute-start(bf16[128,512]{0,1:T(8,128)(2,1)S(1)} %multiply_convert_fusion.1), channel_id=1, source_target_pairs={{0,4},{4,0},{1,5},{5,1},{2,6},{6,2},{3,7},{7,3},{8,12},{12,8},{9,1... | collective-permute-start | bytes 393224 | tf_op jit(solution)/shard_map/ppermute | solution.py:93
  28.7 0.0 all-to-all-done
  28.7 1.3 %copy.25 = bf16[1,2,4,8,64,128]{5,4,3,2,1,0:T(8,128)(2,1)S(1)} copy(bf16[1,2,4,8,64,128]{5,4,2,1,3,0:T(8,128)(2,1)} %bitcast.3) | data formatting | bytes 2097152 | tf_op jit(solution)/shard_map/all_to_all | solution.py:73
  30.0 0.7 %convolution_convert_fusion = bf16[4,128,128]{2,1,0:T(8,128)(2,1)S(1)} fusion(f32[]{:T(128)S(6)} %convert_element_type.96, f32[512]{0:T(512)S(1)} %fusion.16, bf16[1,2,4,512,128]{4,3,2,1,0:T(8,128)(2,1)S(1)} %bitcast.58, bf16[128,4,128]{2,0,1:T(8,128)(2,1)S(1)} %copy.30), kind=kOutput, calls=%fused_computation.5 | convolution fusion | flops 136380416 | bytes 1312772 | tf_op jit(solution)/shard_map/hck,hkd->chd/dot_general | solution.py:28
  30.7 0.0 copy-start.3
  30.8 0.2 collective-permute-start.1
  31.0 0.7 %convolution_convert_fusion.1 = bf16[4,128,128]{2,1,0:T(8,128)(2,1)S(1)} fusion(f32[]{:T(128)S(6)} %convert_element_type.96, f32[512]{0:T(512)S(1)} %fusion.16, bf16[1,2,4,512,128]{4,3,2,1,0:T(8,128)(2,1)S(1)} %bitcast.59, bf16[128,4,128]{2,0,1:T(8,128)(2,1)S(1)} %copy.27), kind=kOutput, calls=%fused_computation.6 | convolution fusion | flops 136380416 | bytes 1312772 | tf_op jit(solution)/shard_map/hck,hkd->chd/dot_general | solution.py:28
  31.7 4.4 %collective-permute-done.1 = bf16[128,512]{0,1:T(8,128)(2,1)S(1)} collective-permute-done((bf16[128,512]{0,1:T(8,128)(2,1)S(1)}, bf16[128,512]{0,1:T(8,128)(2,1)S(1)}, u32[]{:S(2)}, u32[]{:S(2)}) %collective-permute-start.1) | collective-permute-done | bytes 131104 | tf_op jit(solution)/shard_map/ppermute | solution.py:95
  36.1 0.2 convert_reduce_fusion
  36.3 0.2 fusion.1
  36.4 0.0 collective-permute-done.2
  36.4 0.0 copy-done.3
  36.4 0.2 multiply_convert_fusion
  36.7 0.9 %copy.32 = bf16[1,128,1024]{2,1,0:T(8,128)(2,1)} copy(bf16[1,128,1024]{1,2,0:T(8,128)(2,1)S(1)} %multiply_convert_fusion) | data formatting | bytes 524288 | tf_op jit(solution)/shard_map/convert_element_type | solution.py:45
  (4 shorter events, 0.0 us)
Async XLA Ops:
  0.0 3.6 %copy-start = (bf16[4,64,2,1024]{3,2,1,0:T(2,128)(2,1)S(1)}, bf16[4,64,2,1024]{3,2,1,0:T(2,128)(2,1)}, u32[]{:S(2)}) copy-start(bf16[4,64,2,1024]{3,2,1,0:T(2,128)(2,1)} %param.7) | copy-start | bytes 3145732
  0.0 23.1 %collective-permute-start = (bf16[128,1024]{1,0:T(8,128)(2,1)}, bf16[128,1024]{1,0:T(8,128)(2,1)}, u32[]{:S(2)}, u32[]{:S(2)}) collective-permute-start(bf16[128,1024]{1,0:T(8,128)(2,1)} %bitcast.62), channel_id=1, source_target_pairs={{0,4},{4,0},{1,5},{5,1},{2,6},{6,2},{3,7},{7,3},{8,12},{12,8},{9,1... | collective-permute-start | bytes 786440 | tf_op jit(solution)/shard_map/ppermute | solution.py:90
  8.3 20.4 %all-to-all-start = ((bf16[8,2,4,64,128]{4,3,2,1,0:T(8,128)(2,1)}), bf16[8,2,4,64,128]{4,3,2,1,0:T(8,128)(2,1)}, u32[]{:S(2)}, u32[]{:S(2)}) async-start(bf16[8,2,4,64,128]{4,3,2,1,0:T(8,128)(2,1)} %bitcast.1), calls=%async_computation | async-start | bytes 2097152 | tf_op jit(solution)/shard_map/all_to_all | solution.py:73
  12.6 4.8 %copy-start.2 = (bf16[1,128,1024]{2,1,0:T(8,128)(2,1)S(1)}, bf16[1,128,1024]{2,1,0:T(8,128)(2,1)}, u32[]{:S(2)}) copy-start(bf16[1,128,1024]{2,1,0:T(8,128)(2,1)} %param.6) | copy-start | bytes 786436
  17.4 1.5 %copy-start.4 = (s32[4]{0:T(128)S(1)}, s32[4]{0:T(128)}, u32[]{:S(2)}) copy-start(s32[4]{0:T(128)} %param.10) | copy-start | bytes 52
  17.4 1.5 %copy-start.5 = (s32[4]{0:T(128)S(1)}, s32[4]{0:T(128)}, u32[]{:S(2)}) copy-start(s32[4]{0:T(128)} %param.11) | copy-start | bytes 52
  24.7 0.8 %copy-start.1 = (f32[2,128,512]{1,2,0:T(8,128)}, f32[2,128,512]{1,2,0:T(8,128)S(1)}, u32[]{:S(2)}) copy-start(f32[2,128,512]{1,2,0:T(8,128)S(1)} %convolution_bitcast_fusion) | copy-start | bytes 1572868
  26.7 9.7 %collective-permute-start.2 = (bf16[128,512]{0,1:T(8,128)(2,1)S(1)}, bf16[128,512]{0,1:T(8,128)(2,1)S(1)}, u32[]{:S(2)}, u32[]{:S(2)}) collective-permute-start(bf16[128,512]{0,1:T(8,128)(2,1)S(1)} %multiply_convert_fusion.1), channel_id=1, source_target_pairs={{0,4},{4,0},{1,5},{5,1},{2,6},{6,2},{3,7},{7,3},{8,12},{12,8},{9,1... | collective-permute-start | bytes 393224 | tf_op jit(solution)/shard_map/ppermute | solution.py:93
  30.7 5.7 %copy-start.3 = (f32[1024]{0:T(1024)S(1)}, f32[1024]{0:T(1024)}, u32[]{:S(2)}) copy-start(f32[1024]{0:T(1024)} %param.9) | copy-start | bytes 12292
  30.8 5.3 %collective-permute-start.1 = (bf16[128,512]{0,1:T(8,128)(2,1)S(1)}, bf16[128,512]{0,1:T(8,128)(2,1)S(1)}, u32[]{:S(2)}, u32[]{:S(2)}) collective-permute-start(bf16[128,512]{0,1:T(8,128)(2,1)S(1)} %bitcast.64), channel_id=1, source_target_pairs={{0,4},{4,0},{1,5},{5,1},{2,6},{6,2},{3,7},{7,3},{8,12},{12,8},{9,1... | collective-permute-start | bytes 393224 | tf_op jit(solution)/shard_map/ppermute | solution.py:95
